TPU v7x, 128 devices: a whole 4x4x4 slice. The times are simulated.
128 devices in a mesh: row: 8 (over z_hi, x), lmk: 8 (over z_lo, y), bw: 2 (over core).
Axes of the slice: x: 4, y: 4, z: 4 (z_hi: 2, z_lo: 2; z = z_hi * 2 + z_lo), core: 2. Of those that a mesh axis runs over, the one named last changes fastest.
Arguments:
- embeddings: bfloat16 [24576, 1024], P(('row', 'lmk')), may hold values from -6 to 6
- candidates: bfloat16 [131072, 1024], P(('row', 'lmk')), may hold values from -6 to 6
- block_owner: int32 [2], replicated, may hold values from 0 to 63, as said below
- landmark_picks: int32 [2, 2048], replicated, may hold values from 0 to 2047, each once within a row
- inverse_width: float32 [8], P('bw'), may hold values from 2 to 16
- mixture: float32 [8], P('bw'), may hold values from 0.05 to 0.25
- whitening: bfloat16 [4096, 4096], P(None, 'bw'), may hold values from -0.09375 to 0.09375
Outputs:
- features: bfloat16 [24576, 4096], P(('row', 'lmk'), 'bw')
Inputs may be any that keep to these rules, and one draw needn't show every extreme that they name: `block_owner`: the 2 owners are different, and 63 is one of them. `landmark_picks`: each row is an ordering of 0 to 2047.
All inputs are finite; a program needn't handle non-finite values.
Results may differ from a plain program's by a relative error of at most 0.0055.
Values may be sent and summed in bfloat16 or wider, within the bound.
No kernel may reach another device: no remote copies, remote signals or barrier semaphores. Data moves between devices by JAX's collectives and lax.ppermute only.
A program may use at most 128 MiB of HBM per device.

v0:
```python
import jax
import jax.numpy as jnp
from jax import lax
from jax.sharding import PartitionSpec as P


def spread(block, axis, source):
    block = jnp.where(lax.axis_index(axis) == source, block, jnp.zeros_like(block))
    return lax.psum(block, axis)


def normalize(matrix_rows):
    widened = matrix_rows.astype(jnp.float32)
    scale = lax.rsqrt(jnp.sum(widened * widened, axis=-1, keepdims=True) + 1e-06)
    return (widened * scale).astype(jnp.bfloat16)


def kernel_of(cosine, widths, weights):
    running = jnp.zeros(cosine.shape, jnp.float32)
    for which in range(widths.shape[0]):
        running = running + weights[which] * jnp.exp(2.0 * widths[which] * cosine)
    return running


def inner_products(unit_rows, landmark):
    return jnp.einsum("rd,md->rm", unit_rows, landmark, preferred_element_type=jnp.float32)


def per_device(
    embeddings, candidates, block_owner, landmark_picks, inverse_width, mixture, whitening
):
    unit_rows = normalize(embeddings)
    block_count = block_owner.shape[0]
    landmark_blocks = []
    for number in range(block_count):
        owner = block_owner[number]
        chosen = jnp.take(candidates, landmark_picks[number], axis=0)
        arrived = spread(chosen, ("row", "lmk"), owner)
        landmark_blocks.append(normalize(arrived))
    partial_value = jnp.concatenate(
        [
            kernel_of(inner_products(unit_rows, landmark), inverse_width, mixture)
            for landmark in landmark_blocks
        ],
        axis=1,
    )
    kernel = lax.psum(partial_value, "bw").astype(jnp.bfloat16)
    features = jnp.dot(kernel, whitening, preferred_element_type=jnp.float32)
    return features.astype(jnp.bfloat16)


def solution(mesh):
    in_specs = (
        P(("row", "lmk"), None),
        P(("row", "lmk"), None),
        P(),
        P(),
        P("bw"),
        P("bw"),
        P(None, "bw"),
    )
    out_specs = P(("row", "lmk"), "bw")
    return jax.shard_map(
        per_device, mesh=mesh, in_specs=in_specs, out_specs=out_specs, check_vma=False
    )
```

profile of v0, /device:TPU:1, one launch (start us, length us, event | category | flops | bytes accessed | tf_op | source)
XLA Modules:
  0.0 278.1 jit_solution(18227267106462145578)
XLA Ops:
  6.5 0.0 all-reduce.4.cloned.1.call-start
  6.5 0.8 fusion.25
  7.4 1.3 fusion.28
  10.0 13.7 %gather_fusion = bf16[2048,1024]{1,0:T(8,128)(2,1)} fusion(bf16[2048,1024]{1,0:T(8,128)(2,1)} %param.10, s32[2048]{0:T(1024)S(1)} %fusion.23), kind=kCustom, calls=%fused_computation.clone | custom fusion | bytes 8396800 | tf_op jit(solution)/shard_map/jit(_take)/gather | solution.py:37
  23.8 13.7 %gather_fusion.1 = bf16[2048,1024]{1,0:T(8,128)(2,1)} fusion(bf16[2048,1024]{1,0:T(8,128)(2,1)} %param.10, s32[2048]{0:T(1024)S(1)} %fusion.24), kind=kCustom, calls=%fused_computation.1.clone | custom fusion | bytes 8396800 | tf_op jit(solution)/shard_map/jit(_take)/gather | solution.py:37
  37.5 0.0 copy-start
  37.5 4.0 %select_select_fusion.1 = bf16[2048,1024]{1,0:T(8,128)(2,1)} fusion(bf16[2048,1024]{1,0:T(8,128)(2,1)} %gather_fusion, pred[2048]{0:T(1024)(128)(4,1)S(1)} %compare_and_fusion.1, pred[]{:T(512)S(6)} %eq.6), kind=kLoop, calls=%fused_computation.14 | loop fusion | flops 4194304 | bytes 8390657 | tf_op jit(solution)/shard_map/jit(_where)/select_n | solution.py:8
  41.5 0.5 copy-done
  42.0 2.3 select_select_fusion
  44.3 0.0 copy-start.4
  44.3 0.0 copy-start.5
  44.3 0.0 copy-start.3
  44.3 0.0 all-reduce.4.cloned.1.call-update
  44.3 0.6 copy-done.4
  45.0 0.7 fusion.27
  48.2 0.0 copy-done.5
  48.2 0.7 fusion.26
  48.9 0.0 copy-done.3
  48.9 0.2 fusion.19
  49.1 166.0 %all-reduce.4.cloned.1.call-done = (bf16[2048,1024]{1,0:T(8,128)(2,1)}, bf16[2048,1024]{1,0:T(8,128)(2,1)}) async-done(((bf16[2048,1024]{1,0:T(8,128)(2,1)}, bf16[2048,1024]{1,0:T(8,128)(2,1)}), (bf16[2048,1024]{1,0:T(8,128)(2,1)}, bf16[2048,1024]{1,0:T(8,128)(2,1)})) %all-reduce.4.cloned.1.call-update) | async-done | bytes 8388624 | tf_op jit(solution)/shard_map/psum | solution.py:9
  215.1 0.0 copy-start.2
  215.1 5.3 %fusion = (f32[2048]{0:T(1024)S(1)}, f32[2048]{0:T(1024)S(1)}) fusion(bf16[2048,1024]{1,0:T(8,128)(2,1)} %get-tuple-element.7, bf16[2048,1024]{1,0:T(8,128)(2,1)} %get-tuple-element.6), kind=kLoop, calls=%fused_computation.6 | loop fusion | flops 12578816 | bytes 8404992 | tf_op jit(solution)/shard_map/reduce_sum | solution.py:14
  220.4 0.0 copy-done.2
  220.4 0.0 copy-start.1
  220.4 6.5 %multiply_add_fusion.1 = f32[384,2048]{1,0:T(8,128)S(1)} fusion(bf16[2048,1024]{1,0:T(8,128)(2,1)S(1)} %copy-done.2, f32[2048]{0:T(1024)S(1)} %add_rsqrt_fusion.1, f32[]{:T(128)} %bitcast.9, f32[]{:T(128)} %bitcast.8, f32[]{:T(128)} %bitcast.7, f32[]{:T(128)} %bitcast.6, f32[]{:T(128)} %bitcast.5, f32[]{:T(128)} %bitcast.4, f32[]{:T(128)} %bitcast.1, ...), kind=kOutput, calls=%fused_computation.20 | convolution fusion | flops 1626734592 | bytes 8136224 | tf_op jit(solution)/shard_map/rd,md->rm/dot_general | solution.py:26
  226.9 0.0 copy-done.1
  226.9 6.1 %multiply_add_fusion = f32[384,2048]{1,0:T(8,128)S(1)} fusion(bf16[2048,1024]{1,0:T(8,128)(2,1)S(1)} %copy-done.1, f32[2048]{0:T(1024)S(1)} %add_rsqrt_fusion, f32[]{:T(128)} %bitcast.9, f32[]{:T(128)} %bitcast.8, f32[]{:T(128)} %bitcast.7, f32[]{:T(128)} %bitcast.6, f32[]{:T(128)} %bitcast.5, f32[]{:T(128)} %bitcast.4, f32[]{:T(128)} %bitcast.1, ...), kind=kOutput, calls=%fused_computation.19 | convolution fusion | flops 1626734592 | bytes 8136224 | tf_op jit(solution)/shard_map/rd,md->rm/dot_general | solution.py:26
  233.0 3.1 %pad_maximum_fusion = f32[384,4096]{1,0:T(8,128)} fusion(f32[384,2048]{1,0:T(8,128)S(1)} %multiply_add_fusion, f32[384,2048]{1,0:T(8,128)S(1)} %multiply_add_fusion.1), kind=kLoop, calls=%fused_computation.10 | loop fusion | flops 1572864 | bytes 12582912 | tf_op jit(solution)/shard_map/concatenate | solution.py:40
  236.1 23.5 %all-reduce.5 = bf16[384,4096]{1,0:T(8,128)(2,1)S(1)} all-reduce(f32[384,4096]{1,0:T(8,128)} %pad_maximum_fusion), channel_id=1, replica_groups=mesh['row'=8,'lmk'=8,'bw'=2] {'bw'}, use_global_device_ids=true, to_apply=%region_5.7 | all-reduce | flops 1572864 | bytes 9437184 | tf_op jit(solution)/shard_map/psum | solution.py:47
  259.6 11.6 %fusion.12 = bf16[384,2048]{1,0:T(8,128)(2,1)} fusion(bf16[4096,2048]{1,0:T(8,128)(2,1)} %param.15, bf16[384,4096]{1,0:T(8,128)(2,1)S(1)} %all-reduce.5), kind=kOutput, calls=%fused_computation.21 | convolution fusion | flops 6443237376 | bytes 21495808 | tf_op jit(solution)/shard_map/dot_general | solution.py:48
  (7 shorter events, 0.0 us)
Async XLA Ops:
  6.5 208.5 %all-reduce.4.cloned.1.call-start = ((), (), s32[]{:S(2)}) async-start(), calls=%async_computation | async-start | bytes 16777216 | tf_op jit(solution)/shard_map/psum | solution.py:9
  37.5 4.6 %copy-start = (bf16[2048,1024]{1,0:T(8,128)(2,1)S(1)}, bf16[2048,1024]{1,0:T(8,128)(2,1)}, u32[]{:S(2)}) copy-start(bf16[2048,1024]{1,0:T(8,128)(2,1)} %gather_fusion.1) | copy-start | bytes 12582916
  44.3 0.7 copy-start.4
  44.3 3.9 %copy-start.5 = (f32[4]{0:T(128)S(1)}, f32[4]{0:T(128)}, u32[]{:S(2)}) copy-start(f32[4]{0:T(128)} %param.14) | copy-start | bytes 52
  44.3 4.6 %copy-start.3 = (bf16[384,1024]{1,0:T(8,128)(2,1)S(1)}, bf16[384,1024]{1,0:T(8,128)(2,1)}, u32[]{:S(2)}) copy-start(bf16[384,1024]{1,0:T(8,128)(2,1)} %param.9) | copy-start | bytes 2359300
  215.1 5.3 %copy-start.2 = (bf16[2048,1024]{1,0:T(8,128)(2,1)S(1)}, bf16[2048,1024]{1,0:T(8,128)(2,1)}, u32[]{:S(2)}) copy-start(bf16[2048,1024]{1,0:T(8,128)(2,1)} %get-tuple-element.7) | copy-start | bytes 12582916
  220.4 6.5 %copy-start.1 = (bf16[2048,1024]{1,0:T(8,128)(2,1)S(1)}, bf16[2048,1024]{1,0:T(8,128)(2,1)}, u32[]{:S(2)}) copy-start(bf16[2048,1024]{1,0:T(8,128)(2,1)} %get-tuple-element.6) | copy-start | bytes 12582916
Sparse Core Ops, SparseCore 0:
  44.5 170.5 all-reduce.3
where the time goes:
time: 278 us
  waiting for transfers between devices  166 us (60%)
  local copies, waits for them, and re-layouts  32.1 us (12%)
  matrix products  24.2 us (9%)
  blocking collectives  23.5 us (8%)
  between operations  17.4 us (6%)
  other arithmetic  14.9 us (5%)
    psum x1, waiting for transfers between devices, spread(): return lax.psum(block, axis)  166 us
    gather x2, local copies, waits for them, and re-layouts, per_device(): chosen = jnp.take(candidates, landmark_picks[number], axis=0)  27.4 us
    psum x1, blocking collectives, per_device(): kernel = lax.psum(partial_value, 'bw').astype(jnp.bfloat16)  23.5 us
    dot_general x2, matrix products, inner_products(): jnp.einsum('rd,md->rm', unit_rows, landmark, preferred_element_type=jnp.f...  12.6 us
    dot_general x1, matrix products, per_device(): features = jnp.dot(kernel, whitening, preferred_element_type=jnp.float32)  11.6 us
    select_n x2, other arithmetic, spread(): jnp.where(lax.axis_index(axis) == source, block, jnp.zeros_like(block))  6.28 us
  transfers between devices with their start and end apart: 1, of which 1 were waited for; matrix products, arithmetic and copies ran while one was open for 1% of the time, Pallas kernels for 0%

commit v1 on v0

--- a/solution.py
+++ b/solution.py
@@ -2,11 +2,6 @@
 import jax.numpy as jnp
 from jax import lax
 from jax.sharding import PartitionSpec as P
-
-
-def spread(block, axis, source):
-    block = jnp.where(lax.axis_index(axis) == source, block, jnp.zeros_like(block))
-    return lax.psum(block, axis)
 
 
 def normalize(matrix_rows):
@@ -30,21 +25,28 @@
     embeddings, candidates, block_owner, landmark_picks, inverse_width, mixture, whitening
 ):
     unit_rows = normalize(embeddings)
-    block_count = block_owner.shape[0]
-    landmark_blocks = []
+    block_count, block_rows = landmark_picks.shape
+    cores = lax.axis_size("bw")
+    half = block_rows // cores
+    core = lax.axis_index("bw")
+    here = lax.axis_index(("row", "lmk"))
+    widths = lax.all_gather(inverse_width, "bw", tiled=True)
+    weights = lax.all_gather(mixture, "bw", tiled=True)
+    pieces = []
     for number in range(block_count):
-        owner = block_owner[number]
-        chosen = jnp.take(candidates, landmark_picks[number], axis=0)
-        arrived = spread(chosen, ("row", "lmk"), owner)
-        landmark_blocks.append(normalize(arrived))
-    partial_value = jnp.concatenate(
+        picks = lax.dynamic_slice_in_dim(landmark_picks[number], core * half, half)
+        chosen = normalize(jnp.take(candidates, picks, axis=0))
+        chosen = jnp.where(here == block_owner[number], chosen, jnp.zeros_like(chosen))
+        pieces.append(chosen)
+    arrived = lax.psum(pieces, ("row", "lmk"))
+    blocks = [lax.all_gather(piece, "bw", tiled=True) for piece in arrived]
+    kernel = jnp.concatenate(
         [
-            kernel_of(inner_products(unit_rows, landmark), inverse_width, mixture)
-            for landmark in landmark_blocks
+            kernel_of(inner_products(unit_rows, landmark), widths, weights).astype(jnp.bfloat16)
+            for landmark in blocks
         ],
         axis=1,
     )
-    kernel = lax.psum(partial_value, "bw").astype(jnp.bfloat16)
     features = jnp.dot(kernel, whitening, preferred_element_type=jnp.float32)
     return features.astype(jnp.bfloat16)
 

time: 278 us -> 243 us (0.87)
  blocking collectives: 23.5 us -> 4.51 us
  matrix products: 24.2 us -> 37.2 us
  waiting for transfers between devices: 166 us -> 153 us
  local copies, waits for them, and re-layouts: 32.1 us -> 19.6 us
  other arithmetic: 14.9 us -> 7.36 us
  between operations: 17.4 us -> 20.3 us
    psum x1, waiting for transfers between devices: 166 us -> 141 us  [per_device(): arrived = lax.psum(pieces, ('row', 'lmk'))]
    psum x1 -> x0, blocking collectives: 23.5 us -> none  [per_device(): kernel = lax.psum(partial_value, 'bw').astype(jnp.bfloat16)]
    dot_general x2, matrix products: 12.6 us -> 25.2 us  [inner_products(): jnp.einsum('rd,md->rm', unit_rows, landmark, preferred_element_type=jnp.f...]
    all_gather x0 -> x2, waiting for transfers between devices: none -> 11.3 us  [per_device(): blocks = [lax.all_gather(piece, 'bw', tiled=True) for piece in arrived]]
    gather x2, local copies, waits for them, and re-layouts: 27.4 us -> 16.4 us  [per_device(): chosen = normalize(jnp.take(candidates, picks, axis=0))]
    unnamed x0 -> x1, blocking collectives: none -> 4.51 us
    concatenate x1 -> x0, other arithmetic: 3.06 us -> none  [per_device(): jnp.concatenate([kernel_of(inner_products(unit_rows, landmark), inverse_w...]
  transfers between devices with their start and end apart: 1 -> 3, of which waited for: 1 -> 3; matrix products, arithmetic and copies ran while one was open for 1% -> 6% of each run, Pallas kernels for 0% -> 0%
where the time goes in v1:
time: 243 us; the launch traced here: 242 us
  waiting for transfers between devices  153 us (63%)
  matrix products  37.2 us (15%)
  between operations  20.3 us (8%)
  local copies, waits for them, and re-layouts  19.6 us (8%)
  other arithmetic  7.36 us (3%)
  blocking collectives  4.51 us (2%)
    psum x1, waiting for transfers between devices, per_device(): arrived = lax.psum(pieces, ('row', 'lmk'))  141 us
    dot_general x2, matrix products, inner_products(): jnp.einsum('rd,md->rm', unit_rows, landmark, preferred_element_type=jnp.f...  25.2 us
    gather x2, local copies, waits for them, and re-layouts, per_device(): chosen = normalize(jnp.take(candidates, picks, axis=0))  16.4 us
    dot_general x1, matrix products, per_device(): features = jnp.dot(kernel, whitening, preferred_element_type=jnp.float32)  12 us
    all_gather x2, waiting for transfers between devices, per_device(): blocks = [lax.all_gather(piece, 'bw', tiled=True) for piece in arrived]  11.3 us
  transfers between devices with their start and end apart: 3, of which 3 were waited for; matrix products, arithmetic and copies ran while one was open for 6% of the time, Pallas kernels for 0%

profile of v1, /device:TPU:1, one launch (start us, length us, event | category | flops | bytes accessed | tf_op | source)
XLA Modules:
  0.0 241.9 jit_solution(16817355328936555351)
XLA Ops:
  6.5 0.8 fusion.26
  7.4 0.0 copy-start.2
  7.4 7.7 %gather_fusion = bf16[1024,1024]{1,0:T(8,128)(2,1)S(1)} fusion(bf16[2048,1024]{1,0:T(8,128)(2,1)} %param.10, s32[1024]{0:T(1024)S(1)} %fusion.23), kind=kCustom, calls=%fused_computation.clone | custom fusion | bytes 4198400 | tf_op jit(solution)/shard_map/jit(_take)/gather | solution.py:38
  15.2 0.7 fusion
  15.9 0.6 fusion.27
  16.5 8.7 %gather_fusion.1 = bf16[1024,1024]{1,0:T(8,128)(2,1)} fusion(bf16[2048,1024]{1,0:T(8,128)(2,1)} %param.10, s32[1024]{0:T(1024)S(1)} %fusion.24), kind=kCustom, calls=%fused_computation.1.clone | custom fusion | bytes 4198400 | tf_op jit(solution)/shard_map/jit(_take)/gather | solution.py:38
  25.2 2.3 fusion.2
  28.8 2.0 fusion.12
  30.8 2.0 fusion.11
  32.8 0.0 all-reduce.6.cloned.1.call-update
  32.8 0.0 copy-start.5
  32.8 0.0 copy-start.3
  32.9 0.0 copy-start.4
  32.9 0.0 copy-start.1
  32.9 0.0 all-gather.3.cloned.1.call-start
  32.9 140.9 %all-reduce.6.cloned.1.call-done = (bf16[1024,1024]{1,0:T(8,128)(2,1)}, bf16[1024,1024]{1,0:T(8,128)(2,1)}) async-done(((bf16[1024,1024]{1,0:T(8,128)(2,1)}, bf16[1024,1024]{1,0:T(8,128)(2,1)}), (bf16[1024,1024]{1,0:T(8,128)(2,1)}, bf16[1024,1024]{1,0:T(8,128)(2,1)})) %all-reduce.6.cloned.1.call-update) | async-done | bytes 4194320 | tf_op jit(solution)/shard_map/psum | solution.py:41
  173.8 0.0 all-gather.3.cloned.1.call-update
  173.8 0.0 all-gather.5.cloned.1.call-start
  173.9 0.7 all-gather.5.cloned.1.call-update
  174.6 0.6 dynamic-slice.2
  175.8 0.0 copy-done.3
  175.8 0.2 dynamic-update-slice
  176.1 0.0 copy-done.4
  176.1 0.2 dynamic-update-slice.1
  176.3 4.5 %all-reduce.2 = (f32[8]{0:T(128)S(1)}, f32[8]{0:T(128)S(1)}) all-reduce(f32[8]{0:T(128)S(1)} %dynamic-update-slice.1, f32[8]{0:T(128)S(1)} %dynamic-update-slice), channel_id=1, replica_groups=mesh['row'=8,'lmk'=8,'bw'=2] {'bw'}, use_global_device_ids=true, to_apply=%add.1 | all-reduce | flops 16 | bytes 128
  180.8 0.7 fusion.28
  186.7 0.2 fusion.13
  186.9 4.5 %all-gather.3.cloned.1.call-done = bf16[2048,1024]{1,0:T(8,128)(2,1)} async-done(((bf16[1024,1024]{1,0:T(8,128)(2,1)}), bf16[2048,1024]{1,0:T(8,128)(2,1)}) %all-gather.3.cloned.1.call-update) | async-done | bytes 4194320 | tf_op jit(solution)/shard_map/all_gather | solution.py:42
  191.4 12.6 %add_convert_fusion.1 = bf16[384,2048]{1,0:T(8,128)(2,1)S(1)} fusion(f32[]{:T(128)} %bitcast.18, f32[]{:T(128)} %bitcast.17, f32[]{:T(128)} %bitcast.16, f32[]{:T(128)} %bitcast.15, f32[]{:T(128)} %bitcast.14, f32[]{:T(128)} %bitcast.13, f32[]{:T(128)} %bitcast.12, f32[]{:T(128)} %bitcast.11, f32[]{:T(128)} %bitcast.10, f32[]{:T(128)} %bitcast.9, ...), kind=kOutput, calls=%fused_computation.15 | convolution fusion | flops 1630666752 | bytes 6555200 | tf_op jit(solution)/shard_map/rd,md->rm/dot_general | solution.py:21
  204.0 6.8 %all-gather.5.cloned.1.call-done = bf16[2048,1024]{1,0:T(8,128)(2,1)} async-done(((bf16[1024,1024]{1,0:T(8,128)(2,1)}), bf16[2048,1024]{1,0:T(8,128)(2,1)}) %all-gather.5.cloned.1.call-update) | async-done | bytes 4194320 | tf_op jit(solution)/shard_map/all_gather | solution.py:42
  210.8 12.6 %add_convert_fusion = bf16[384,2048]{1,0:T(8,128)(2,1)S(1)} fusion(f32[]{:T(128)} %bitcast.18, f32[]{:T(128)} %bitcast.17, f32[]{:T(128)} %bitcast.16, f32[]{:T(128)} %bitcast.15, f32[]{:T(128)} %bitcast.14, f32[]{:T(128)} %bitcast.13, f32[]{:T(128)} %bitcast.12, f32[]{:T(128)} %bitcast.11, f32[]{:T(128)} %bitcast.10, f32[]{:T(128)} %bitcast.9, ...), kind=kOutput, calls=%fused_computation.14 | convolution fusion | flops 1630666752 | bytes 6555200 | tf_op jit(solution)/shard_map/rd,md->rm/dot_general | solution.py:21
  223.4 12.0 %fusion.8 = bf16[384,2048]{1,0:T(8,128)(2,1)} fusion(bf16[4096,2048]{1,0:T(8,128)(2,1)} %param.15, bf16[384,2048]{1,0:T(8,128)(2,1)S(1)} %add_convert_fusion, bf16[384,2048]{1,0:T(8,128)(2,1)S(1)} %add_convert_fusion.1), kind=kOutput, calls=%fused_computation.16 | convolution fusion | flops 6449528832 | bytes 21495808 | tf_op jit(solution)/shard_map/dot_general | solution.py:50
  (16 shorter events, 0.1 us)
Async XLA Ops:
  6.5 167.3 %all-reduce.6.cloned.1.call-start = ((), (), s32[]{:S(2)}) async-start(), calls=%async_computation.2 | async-start | bytes 8388608 | tf_op jit(solution)/shard_map/psum | solution.py:41
  7.4 8.5 %copy-start.2 = (s32[2]{0:T(128)S(1)}, s32[2]{0:T(128)}, u32[]{:S(2)}) copy-start(s32[2]{0:T(128)} %param.11) | copy-start | bytes 28
  28.8 2.1 copy-start
  32.8 141.8 %copy-start.5 = (u32[128]{0:T(128)S(1)}, u32[128]{0:T(128)}, u32[]{:S(2)}) copy-start(u32[128]{0:T(128)} %constant.51) | copy-start | bytes 1540
  32.8 143.0 %copy-start.3 = (f32[4]{0:T(128)S(1)}, f32[4]{0:T(128)}, u32[]{:S(2)}) copy-start(f32[4]{0:T(128)} %param.14) | copy-start | bytes 52
  32.9 143.2 %copy-start.4 = (f32[4]{0:T(128)S(1)}, f32[4]{0:T(128)}, u32[]{:S(2)}) copy-start(f32[4]{0:T(128)} %param.13) | copy-start | bytes 52
  32.9 153.8 %copy-start.1 = (bf16[384,1024]{1,0:T(8,128)(2,1)S(1)}, bf16[384,1024]{1,0:T(8,128)(2,1)}, u32[]{:S(2)}) copy-start(bf16[384,1024]{1,0:T(8,128)(2,1)} %param.9) | copy-start | bytes 2359300
  32.9 158.5 %all-gather.3.cloned.1.call-start = ((), (), s32[]{:S(2)}) async-start(), calls=%async_computation | async-start | bytes 6291456 | tf_op jit(solution)/shard_map/all_gather | solution.py:42
  173.8 37.0 %all-gather.5.cloned.1.call-start = ((), (), s32[]{:S(2)}) async-start(), calls=%async_computation.1 | async-start | bytes 6291456 | tf_op jit(solution)/shard_map/all_gather | solution.py:42
Sparse Core Ops, SparseCore 0:
  32.9 140.8 all-reduce.5
  175.5 15.8 all-gather.2
  193.1 17.6 all-gather.4

commit v2 on v1

v2 whole, which is shorter than its diff:
```python
import jax
import jax.numpy as jnp
from jax import lax
from jax.sharding import PartitionSpec as P

SPREAD = ("row", "lmk")


def normalize(matrix_rows):
    widened = matrix_rows.astype(jnp.float32)
    scale = lax.rsqrt(jnp.sum(widened * widened, axis=-1, keepdims=True) + 1e-06)
    return (widened * scale).astype(jnp.bfloat16)


def kernel_of(cosine, widths, weights):
    running = jnp.zeros(cosine.shape, jnp.float32)
    for which in range(widths.shape[0]):
        running = running + weights[which] * jnp.exp(2.0 * widths[which] * cosine)
    return running


def inner_products(unit_rows, landmark):
    return jnp.einsum("rd,md->rm", unit_rows, landmark, preferred_element_type=jnp.float32)


def shifted(value, shift, count):
    return lax.ppermute(value, SPREAD, [(i, (i + shift) % count) for i in range(count)])


def broadcast(rows, owner, count):
    here = lax.axis_index(SPREAD)
    pieces = rows.reshape(count, rows.shape[0] // count, rows.shape[1])
    got = [pieces[0] * 0 + lax.dynamic_index_in_dim(pieces, here, 0, keepdims=False)]
    for shift in range(1, count):
        piece = lax.dynamic_index_in_dim(pieces, (here + shift) % count, 0, keepdims=False)
        got.append(shifted(piece, shift, count))
    mine = lax.dynamic_index_in_dim(jnp.stack(got), (here - owner) % count, 0, keepdims=False)
    held = [mine] + [shifted(mine, shift, count) for shift in range(1, count)]
    reordered = jnp.stack([held[0]] + held[:0:-1])
    doubled = jnp.concatenate([reordered, reordered], axis=0)
    whole = lax.dynamic_slice_in_dim(doubled, (count - here) % (2 * count), count, axis=0)
    return whole.reshape(rows.shape)


def per_device(
    embeddings, candidates, block_owner, landmark_picks, inverse_width, mixture, whitening
):
    unit_rows = normalize(embeddings)
    block_count, block_rows = landmark_picks.shape
    cores = lax.axis_size("bw")
    count = lax.axis_size(SPREAD)
    half = block_rows // cores
    core = lax.axis_index("bw")
    widths = lax.all_gather(inverse_width, "bw", tiled=True)
    weights = lax.all_gather(mixture, "bw", tiled=True)
    kernels = []
    for number in range(block_count):
        picks = lax.dynamic_slice_in_dim(landmark_picks[number], core * half, half)
        chosen = normalize(jnp.take(candidates, picks, axis=0))
        mine = broadcast(chosen, block_owner[number], count)
        other = lax.ppermute(mine, "bw", [(0, 1), (1, 0)])
        landmark = jnp.where(
            core == 0,
            jnp.concatenate([mine, other], axis=0),
            jnp.concatenate([other, mine], axis=0),
        )
        kernels.append(
            kernel_of(inner_products(unit_rows, landmark), widths, weights).astype(jnp.bfloat16)
        )
    kernel = jnp.concatenate(kernels, axis=1)
    features = jnp.dot(kernel, whitening, preferred_element_type=jnp.float32)
    return features.astype(jnp.bfloat16)


def solution(mesh):
    in_specs = (
        P(SPREAD, None),
        P(SPREAD, None),
        P(),
        P(),
        P("bw"),
        P("bw"),
        P(None, "bw"),
    )
    out_specs = P(SPREAD, "bw")
    return jax.shard_map(
        per_device, mesh=mesh, in_specs=in_specs, out_specs=out_specs, check_vma=False
    )
```

time: 243 us -> 1500 us (6.17)
  starting transfers between devices: 0.08 us -> 1340 us
  waiting for transfers between devices: 153 us -> 7.41 us
  local copies, waits for them, and re-layouts: 19.6 us -> 73.9 us
    ppermute x0 -> x254, starting transfers between devices: none -> 1340 us  [the longest x252 1310 us: shifted(): lax.ppermute(value, SPREAD, [(i, (i + shift) % count) for i in range(coun...]
    psum x1 -> x0, waiting for transfers between devices: 141 us -> none  [per_device(): arrived = lax.psum(pieces, ('row', 'lmk'))]
    unnamed x17 -> x411, local copies, waits for them, and re-layouts: 1.09 us -> 46.3 us
  transfers between devices with their start and end apart: 3 -> 254, of which waited for: 3 -> 4; matrix products, arithmetic and copies ran while one was open for 6% -> 6% of each run, Pallas kernels for 0% -> 0%
where the time goes in v2:
time: 1500 us; the launch traced here: 1490 us
  starting transfers between devices  1340 us (89%)
  local copies, waits for them, and re-layouts  73.9 us (5%)
  matrix products  41.3 us (3%)
    ppermute x252, starting transfers between devices, shifted(): lax.ppermute(value, SPREAD, [(i, (i + shift) % count) for i in range(coun...  1310 us
    unnamed x411, local copies, waits for them, and re-layouts  46.3 us
    dot_general x2, matrix products, inner_products(): jnp.einsum('rd,md->rm', unit_rows, landmark, preferred_element_type=jnp.f...  33.6 us
  transfers between devices with their start and end apart: 254, of which 4 were waited for; matrix products, arithmetic and copies ran while one was open for 6% of the time, Pallas kernels for 0%

profile of v2, /device:TPU:1, one launch (start us, length us, event | category | flops | bytes accessed | tf_op | source)
XLA Modules:
  0.0 1488.3 jit_solution(12562269316461936065)
XLA Ops:
  141.4 15.3 %collective-permute-start.36 = (bf16[16,1024]{1,0:T(8,128)(2,1)S(1)}, bf16[16,1024]{1,0:T(8,128)(2,1)S(1)}, u32[]{:S(2)}, u32[]{:S(2)}) collective-permute-start(bf16[16,1024]{1,0:T(8,128)(2,1)S(1)} %get-tuple-element.36), channel_id=1, source_target_pairs={{0,74},{2,76},{4,78},{6,80},{8,82},{10,84},{12,86},{14,88},{16,90}... | collective-permute-start | bytes 98312 | tf_op jit(solution)/shard_map/ppermute | solution.py:27
  166.9 8.9 collective-permute-start.38
  195.5 8.9 collective-permute-start.41
  243.0 9.4 collective-permute-start.46
  272.0 8.9 collective-permute-start.49
  291.0 8.9 collective-permute-start.51
  329.1 8.9 collective-permute-start.55
  357.7 8.9 collective-permute-start.58
  395.7 8.9 collective-permute-start.62
  492.3 15.2 %collective-permute-start.163 = (bf16[16,1024]{1,0:T(8,128)(2,1)S(1)}, bf16[16,1024]{1,0:T(8,128)(2,1)S(1)}, u32[]{:S(2)}, u32[]{:S(2)}) collective-permute-start(bf16[16,1024]{1,0:T(8,128)(2,1)S(1)} %get-tuple-element.102), channel_id=1, source_target_pairs={{0,74},{2,76},{4,78},{6,80},{8,82},{10,84},{12,86},{14,88},{16,90}... | collective-permute-start | bytes 98312 | tf_op jit(solution)/shard_map/ppermute | solution.py:27
  507.6 8.9 collective-permute-start.164
  516.5 8.9 collective-permute-start.165
  525.4 8.9 collective-permute-start.166
  534.3 8.9 collective-permute-start.167
  543.2 8.9 collective-permute-start.168
  596.6 8.9 collective-permute-start.174
  605.5 8.9 collective-permute-start.175
  614.4 8.9 collective-permute-start.176
  623.3 8.9 collective-permute-start.177
  658.9 9.4 collective-permute-start.181
  668.3 8.9 collective-permute-start.182
  677.2 8.9 collective-permute-start.183
  686.1 8.9 collective-permute-start.184
  695.0 8.9 collective-permute-start.185
  784.8 9.0 collective-permute-start.68
  1064.4 17.2 %collective-permute-start.190 = (bf16[16,1024]{1,0:T(8,128)(2,1)S(1)}, bf16[16,1024]{1,0:T(8,128)(2,1)S(1)}, u32[]{:S(2)}, u32[]{:S(2)}) collective-permute-start(bf16[16,1024]{1,0:T(8,128)(2,1)S(1)} %get-tuple-element.74), channel_id=1, source_target_pairs={{0,126},{2,0},{4,2},{6,4},{8,6},{10,8},{12,10},{14,12},{16,14},{18... | collective-permute-start | bytes 98312 | tf_op jit(solution)/shard_map/ppermute | solution.py:27
  1118.8 9.0 collective-permute-start.195
  1398.7 17.2 %collective-permute-start.126 = (bf16[1024,1024]{1,0:T(8,128)(2,1)S(1)}, bf16[1024,1024]{1,0:T(8,128)(2,1)}, u32[]{:S(2)}, u32[]{:S(2)}) collective-permute-start(bf16[1024,1024]{1,0:T(8,128)(2,1)S(1)} %bitcast.928), channel_id=1, source_target_pairs={{0,1},{1,0},{2,3},{3,2},{4,5},{5,4},{6,7},{7,6},{8,9},{9,8},{10,11... | collective-permute-start | bytes 6291464 | tf_op jit(solution)/shard_map/ppermute | solution.py:61
  1418.3 9.0 collective-permute-start.253
  1429.1 11.8 all-reduce.2
  1446.7 17.4 %add_convert_fusion.1 = bf16[384,2048]{1,0:T(8,128)(2,1)S(1)} fusion(f32[]{:T(128)} %bitcast.211, f32[]{:T(128)} %bitcast.210, f32[]{:T(128)} %bitcast.209, f32[]{:T(128)} %bitcast.208, f32[]{:T(128)} %bitcast.207, f32[]{:T(128)} %bitcast.206, f32[]{:T(128)} %bitcast.205, f32[]{:T(128)} %bitcast.204, f32[]{:T(128)} %bitcast.203, f32[]{:T(128)} %bitcast.202, ...), kind=kOutput, calls=%fused_computation.31 | convolution fusion | flops 1649541120 | bytes 6555201 | tf_op jit(solution)/shard_map/rd,md->rm/dot_general | solution.py:23
  1464.2 16.2 %add_convert_fusion = bf16[384,2048]{1,0:T(8,128)(2,1)S(1)} fusion(f32[]{:T(128)} %bitcast.211, f32[]{:T(128)} %bitcast.210, f32[]{:T(128)} %bitcast.209, f32[]{:T(128)} %bitcast.208, f32[]{:T(128)} %bitcast.207, f32[]{:T(128)} %bitcast.206, f32[]{:T(128)} %bitcast.205, f32[]{:T(128)} %bitcast.204, f32[]{:T(128)} %bitcast.203, f32[]{:T(128)} %bitcast.202, ...), kind=kOutput, calls=%fused_computation.30 | convolution fusion | flops 1649541120 | bytes 6555201 | tf_op jit(solution)/shard_map/rd,md->rm/dot_general | solution.py:23
  (926 shorter events, 1145.1 us)
Async XLA Ops:
  141.4 54.0 %collective-permute-start.36 = (bf16[16,1024]{1,0:T(8,128)(2,1)S(1)}, bf16[16,1024]{1,0:T(8,128)(2,1)S(1)}, u32[]{:S(2)}, u32[]{:S(2)}) collective-permute-start(bf16[16,1024]{1,0:T(8,128)(2,1)S(1)} %get-tuple-element.36), channel_id=1, source_target_pairs={{0,74},{2,76},{4,78},{6,80},{8,82},{10,84},{12,86},{14,88},{16,90}... | collective-permute-start | bytes 98312 | tf_op jit(solution)/shard_map/ppermute | solution.py:27
  157.4 47.6 %collective-permute-start.37 = (bf16[16,1024]{1,0:T(8,128)(2,1)S(1)}, bf16[16,1024]{1,0:T(8,128)(2,1)S(1)}, u32[]{:S(2)}, u32[]{:S(2)}) collective-permute-start(bf16[16,1024]{1,0:T(8,128)(2,1)S(1)} %get-tuple-element.35), channel_id=1, source_target_pairs={{0,76},{2,78},{4,80},{6,82},{8,84},{10,86},{12,88},{14,90},{16,92}... | collective-permute-start | bytes 98312 | tf_op jit(solution)/shard_map/ppermute | solution.py:27
  166.9 47.6 %collective-permute-start.38 = (bf16[16,1024]{1,0:T(8,128)(2,1)S(1)}, bf16[16,1024]{1,0:T(8,128)(2,1)S(1)}, u32[]{:S(2)}, u32[]{:S(2)}) collective-permute-start(bf16[16,1024]{1,0:T(8,128)(2,1)S(1)} %get-tuple-element.34), channel_id=1, source_target_pairs={{0,78},{2,80},{4,82},{6,84},{8,86},{10,88},{12,90},{14,92},{16,94}... | collective-permute-start | bytes 98312 | tf_op jit(solution)/shard_map/ppermute | solution.py:27
  176.4 47.6 %collective-permute-start.39 = (bf16[16,1024]{1,0:T(8,128)(2,1)S(1)}, bf16[16,1024]{1,0:T(8,128)(2,1)S(1)}, u32[]{:S(2)}, u32[]{:S(2)}) collective-permute-start(bf16[16,1024]{1,0:T(8,128)(2,1)S(1)} %get-tuple-element.33), channel_id=1, source_target_pairs={{0,80},{2,82},{4,84},{6,86},{8,88},{10,90},{12,92},{14,94},{16,96}... | collective-permute-start | bytes 98312 | tf_op jit(solution)/shard_map/ppermute | solution.py:27
  185.9 47.6 %collective-permute-start.40 = (bf16[16,1024]{1,0:T(8,128)(2,1)S(1)}, bf16[16,1024]{1,0:T(8,128)(2,1)S(1)}, u32[]{:S(2)}, u32[]{:S(2)}) collective-permute-start(bf16[16,1024]{1,0:T(8,128)(2,1)S(1)} %get-tuple-element.32), channel_id=1, source_target_pairs={{0,82},{2,84},{4,86},{6,88},{8,90},{10,92},{12,94},{14,96},{16,98}... | collective-permute-start | bytes 98312 | tf_op jit(solution)/shard_map/ppermute | solution.py:27
  195.5 47.6 %collective-permute-start.41 = (bf16[16,1024]{1,0:T(8,128)(2,1)S(1)}, bf16[16,1024]{1,0:T(8,128)(2,1)S(1)}, u32[]{:S(2)}, u32[]{:S(2)}) collective-permute-start(bf16[16,1024]{1,0:T(8,128)(2,1)S(1)} %get-tuple-element.31), channel_id=1, source_target_pairs={{0,84},{2,86},{4,88},{6,90},{8,92},{10,94},{12,96},{14,98},{16,100... | collective-permute-start | bytes 98312 | tf_op jit(solution)/shard_map/ppermute | solution.py:27
  205.0 48.0 %collective-permute-start.42 = (bf16[16,1024]{1,0:T(8,128)(2,1)S(1)}, bf16[16,1024]{1,0:T(8,128)(2,1)S(1)}, u32[]{:S(2)}, u32[]{:S(2)}) collective-permute-start(bf16[16,1024]{1,0:T(8,128)(2,1)S(1)} %get-tuple-element.30), channel_id=1, source_target_pairs={{0,86},{2,88},{4,90},{6,92},{8,94},{10,96},{12,98},{14,100},{16,10... | collective-permute-start | bytes 98312 | tf_op jit(solution)/shard_map/ppermute | solution.py:27
  214.5 48.0 %collective-permute-start.43 = (bf16[16,1024]{1,0:T(8,128)(2,1)S(1)}, bf16[16,1024]{1,0:T(8,128)(2,1)S(1)}, u32[]{:S(2)}, u32[]{:S(2)}) collective-permute-start(bf16[16,1024]{1,0:T(8,128)(2,1)S(1)} %get-tuple-element.29), channel_id=1, source_target_pairs={{0,88},{2,90},{4,92},{6,94},{8,96},{10,98},{12,100},{14,102},{16,1... | collective-permute-start | bytes 98312 | tf_op jit(solution)/shard_map/ppermute | solution.py:27
  224.0 48.0 %collective-permute-start.44 = (bf16[16,1024]{1,0:T(8,128)(2,1)S(1)}, bf16[16,1024]{1,0:T(8,128)(2,1)S(1)}, u32[]{:S(2)}, u32[]{:S(2)}) collective-permute-start(bf16[16,1024]{1,0:T(8,128)(2,1)S(1)} %get-tuple-element.28), channel_id=1, source_target_pairs={{0,90},{2,92},{4,94},{6,96},{8,98},{10,100},{12,102},{14,104},{16,... | collective-permute-start | bytes 98312 | tf_op jit(solution)/shard_map/ppermute | solution.py:27
  233.5 48.0 %collective-permute-start.45 = (bf16[16,1024]{1,0:T(8,128)(2,1)S(1)}, bf16[16,1024]{1,0:T(8,128)(2,1)S(1)}, u32[]{:S(2)}, u32[]{:S(2)}) collective-permute-start(bf16[16,1024]{1,0:T(8,128)(2,1)S(1)} %get-tuple-element.27), channel_id=1, source_target_pairs={{0,92},{2,94},{4,96},{6,98},{8,100},{10,102},{12,104},{14,106},{16... | collective-permute-start | bytes 98312 | tf_op jit(solution)/shard_map/ppermute | solution.py:27
  243.0 48.0 %collective-permute-start.46 = (bf16[16,1024]{1,0:T(8,128)(2,1)S(1)}, bf16[16,1024]{1,0:T(8,128)(2,1)S(1)}, u32[]{:S(2)}, u32[]{:S(2)}) collective-permute-start(bf16[16,1024]{1,0:T(8,128)(2,1)S(1)} %get-tuple-element.26), channel_id=1, source_target_pairs={{0,94},{2,96},{4,98},{6,100},{8,102},{10,104},{12,106},{14,108},{1... | collective-permute-start | bytes 98312 | tf_op jit(solution)/shard_map/ppermute | solution.py:27
  253.0 47.6 %collective-permute-start.47 = (bf16[16,1024]{1,0:T(8,128)(2,1)S(1)}, bf16[16,1024]{1,0:T(8,128)(2,1)S(1)}, u32[]{:S(2)}, u32[]{:S(2)}) collective-permute-start(bf16[16,1024]{1,0:T(8,128)(2,1)S(1)} %get-tuple-element.25), channel_id=1, source_target_pairs={{0,96},{2,98},{4,100},{6,102},{8,104},{10,106},{12,108},{14,110},{... | collective-permute-start | bytes 98312 | tf_op jit(solution)/shard_map/ppermute | solution.py:27
  262.5 47.6 %collective-permute-start.48 = (bf16[16,1024]{1,0:T(8,128)(2,1)S(1)}, bf16[16,1024]{1,0:T(8,128)(2,1)S(1)}, u32[]{:S(2)}, u32[]{:S(2)}) collective-permute-start(bf16[16,1024]{1,0:T(8,128)(2,1)S(1)} %get-tuple-element.24), channel_id=1, source_target_pairs={{0,98},{2,100},{4,102},{6,104},{8,106},{10,108},{12,110},{14,112},... | collective-permute-start | bytes 98312 | tf_op jit(solution)/shard_map/ppermute | solution.py:27
  272.0 47.6 %collective-permute-start.49 = (bf16[16,1024]{1,0:T(8,128)(2,1)S(1)}, bf16[16,1024]{1,0:T(8,128)(2,1)S(1)}, u32[]{:S(2)}, u32[]{:S(2)}) collective-permute-start(bf16[16,1024]{1,0:T(8,128)(2,1)S(1)} %get-tuple-element.23), channel_id=1, source_target_pairs={{0,100},{2,102},{4,104},{6,106},{8,108},{10,110},{12,112},{14,114}... | collective-permute-start | bytes 98312 | tf_op jit(solution)/shard_map/ppermute | solution.py:27
  281.5 47.6 %collective-permute-start.50 = (bf16[16,1024]{1,0:T(8,128)(2,1)S(1)}, bf16[16,1024]{1,0:T(8,128)(2,1)S(1)}, u32[]{:S(2)}, u32[]{:S(2)}) collective-permute-start(bf16[16,1024]{1,0:T(8,128)(2,1)S(1)} %get-tuple-element.22), channel_id=1, source_target_pairs={{0,102},{2,104},{4,106},{6,108},{8,110},{10,112},{12,114},{14,116}... | collective-permute-start | bytes 98312 | tf_op jit(solution)/shard_map/ppermute | solution.py:27
  291.0 47.6 %collective-permute-start.51 = (bf16[16,1024]{1,0:T(8,128)(2,1)S(1)}, bf16[16,1024]{1,0:T(8,128)(2,1)S(1)}, u32[]{:S(2)}, u32[]{:S(2)}) collective-permute-start(bf16[16,1024]{1,0:T(8,128)(2,1)S(1)} %get-tuple-element.21), channel_id=1, source_target_pairs={{0,104},{2,106},{4,108},{6,110},{8,112},{10,114},{12,116},{14,118}... | collective-permute-start | bytes 98312 | tf_op jit(solution)/shard_map/ppermute | solution.py:27
  300.5 47.6 %collective-permute-start.52 = (bf16[16,1024]{1,0:T(8,128)(2,1)S(1)}, bf16[16,1024]{1,0:T(8,128)(2,1)S(1)}, u32[]{:S(2)}, u32[]{:S(2)}) collective-permute-start(bf16[16,1024]{1,0:T(8,128)(2,1)S(1)} %get-tuple-element.20), channel_id=1, source_target_pairs={{0,106},{2,108},{4,110},{6,112},{8,114},{10,116},{12,118},{14,120}... | collective-permute-start | bytes 98312 | tf_op jit(solution)/shard_map/ppermute | solution.py:27
  310.1 47.6 %collective-permute-start.53 = (bf16[16,1024]{1,0:T(8,128)(2,1)S(1)}, bf16[16,1024]{1,0:T(8,128)(2,1)S(1)}, u32[]{:S(2)}, u32[]{:S(2)}) collective-permute-start(bf16[16,1024]{1,0:T(8,128)(2,1)S(1)} %get-tuple-element.19), channel_id=1, source_target_pairs={{0,108},{2,110},{4,112},{6,114},{8,116},{10,118},{12,120},{14,122}... | collective-permute-start | bytes 98312 | tf_op jit(solution)/shard_map/ppermute | solution.py:27
  319.6 47.6 %collective-permute-start.54 = (bf16[16,1024]{1,0:T(8,128)(2,1)S(1)}, bf16[16,1024]{1,0:T(8,128)(2,1)S(1)}, u32[]{:S(2)}, u32[]{:S(2)}) collective-permute-start(bf16[16,1024]{1,0:T(8,128)(2,1)S(1)} %get-tuple-element.18), channel_id=1, source_target_pairs={{0,110},{2,112},{4,114},{6,116},{8,118},{10,120},{12,122},{14,124}... | collective-permute-start | bytes 98312 | tf_op jit(solution)/shard_map/ppermute | solution.py:27
  329.1 47.6 %collective-permute-start.55 = (bf16[16,1024]{1,0:T(8,128)(2,1)S(1)}, bf16[16,1024]{1,0:T(8,128)(2,1)S(1)}, u32[]{:S(2)}, u32[]{:S(2)}) collective-permute-start(bf16[16,1024]{1,0:T(8,128)(2,1)S(1)} %get-tuple-element.17), channel_id=1, source_target_pairs={{0,112},{2,114},{4,116},{6,118},{8,120},{10,122},{12,124},{14,126}... | collective-permute-start | bytes 98312 | tf_op jit(solution)/shard_map/ppermute | solution.py:27
  338.6 47.6 %collective-permute-start.56 = (bf16[16,1024]{1,0:T(8,128)(2,1)S(1)}, bf16[16,1024]{1,0:T(8,128)(2,1)S(1)}, u32[]{:S(2)}, u32[]{:S(2)}) collective-permute-start(bf16[16,1024]{1,0:T(8,128)(2,1)S(1)} %get-tuple-element.16), channel_id=1, source_target_pairs={{0,114},{2,116},{4,118},{6,120},{8,122},{10,124},{12,126},{14,0},{... | collective-permute-start | bytes 98312 | tf_op jit(solution)/shard_map/ppermute | solution.py:27
  348.1 47.6 %collective-permute-start.57 = (bf16[16,1024]{1,0:T(8,128)(2,1)S(1)}, bf16[16,1024]{1,0:T(8,128)(2,1)S(1)}, u32[]{:S(2)}, u32[]{:S(2)}) collective-permute-start(bf16[16,1024]{1,0:T(8,128)(2,1)S(1)} %get-tuple-element.15), channel_id=1, source_target_pairs={{0,116},{2,118},{4,120},{6,122},{8,124},{10,126},{12,0},{14,2},{16... | collective-permute-start | bytes 98312 | tf_op jit(solution)/shard_map/ppermute | solution.py:27
  357.7 47.6 %collective-permute-start.58 = (bf16[16,1024]{1,0:T(8,128)(2,1)S(1)}, bf16[16,1024]{1,0:T(8,128)(2,1)S(1)}, u32[]{:S(2)}, u32[]{:S(2)}) collective-permute-start(bf16[16,1024]{1,0:T(8,128)(2,1)S(1)} %get-tuple-element.14), channel_id=1, source_target_pairs={{0,118},{2,120},{4,122},{6,124},{8,126},{10,0},{12,2},{14,4},{16,6... | collective-permute-start | bytes 98312 | tf_op jit(solution)/shard_map/ppermute | solution.py:27
  492.3 50.8 %collective-permute-start.163 = (bf16[16,1024]{1,0:T(8,128)(2,1)S(1)}, bf16[16,1024]{1,0:T(8,128)(2,1)S(1)}, u32[]{:S(2)}, u32[]{:S(2)}) collective-permute-start(bf16[16,1024]{1,0:T(8,128)(2,1)S(1)} %get-tuple-element.102), channel_id=1, source_target_pairs={{0,74},{2,76},{4,78},{6,80},{8,82},{10,84},{12,86},{14,88},{16,90}... | collective-permute-start | bytes 98312 | tf_op jit(solution)/shard_map/ppermute | solution.py:27
  695.0 45.3 %collective-permute-start.185 = (bf16[16,1024]{1,0:T(8,128)(2,1)S(1)}, bf16[16,1024]{1,0:T(8,128)(2,1)S(1)}, u32[]{:S(2)}, u32[]{:S(2)}) collective-permute-start(bf16[16,1024]{1,0:T(8,128)(2,1)S(1)} %get-tuple-element.80), channel_id=1, source_target_pairs={{0,118},{2,120},{4,122},{6,124},{8,126},{10,0},{12,2},{14,4},{16,6... | collective-permute-start | bytes 98312 | tf_op jit(solution)/shard_map/ppermute | solution.py:27
  1064.4 54.4 %collective-permute-start.190 = (bf16[16,1024]{1,0:T(8,128)(2,1)S(1)}, bf16[16,1024]{1,0:T(8,128)(2,1)S(1)}, u32[]{:S(2)}, u32[]{:S(2)}) collective-permute-start(bf16[16,1024]{1,0:T(8,128)(2,1)S(1)} %get-tuple-element.74), channel_id=1, source_target_pairs={{0,126},{2,0},{4,2},{6,4},{8,6},{10,8},{12,10},{14,12},{16,14},{18... | collective-permute-start | bytes 98312 | tf_op jit(solution)/shard_map/ppermute | solution.py:27
  1081.6 46.1 %collective-permute-start.191 = (bf16[16,1024]{1,0:T(8,128)(2,1)S(1)}, bf16[16,1024]{1,0:T(8,128)(2,1)S(1)}, u32[]{:S(2)}, u32[]{:S(2)}) collective-permute-start(bf16[16,1024]{1,0:T(8,128)(2,1)S(1)} %get-tuple-element.74), channel_id=1, source_target_pairs={{0,124},{2,126},{4,0},{6,2},{8,4},{10,6},{12,8},{14,10},{16,12},{1... | collective-permute-start | bytes 98312 | tf_op jit(solution)/shard_map/ppermute | solution.py:27
  1090.5 46.1 %collective-permute-start.192 = (bf16[16,1024]{1,0:T(8,128)(2,1)S(1)}, bf16[16,1024]{1,0:T(8,128)(2,1)S(1)}, u32[]{:S(2)}, u32[]{:S(2)}) collective-permute-start(bf16[16,1024]{1,0:T(8,128)(2,1)S(1)} %get-tuple-element.74), channel_id=1, source_target_pairs={{0,122},{2,124},{4,126},{6,0},{8,2},{10,4},{12,6},{14,8},{16,10},{... | collective-permute-start | bytes 98312 | tf_op jit(solution)/shard_map/ppermute | solution.py:27
  1099.4 46.1 %collective-permute-start.193 = (bf16[16,1024]{1,0:T(8,128)(2,1)S(1)}, bf16[16,1024]{1,0:T(8,128)(2,1)S(1)}, u32[]{:S(2)}, u32[]{:S(2)}) collective-permute-start(bf16[16,1024]{1,0:T(8,128)(2,1)S(1)} %get-tuple-element.74), channel_id=1, source_target_pairs={{0,120},{2,122},{4,124},{6,126},{8,0},{10,2},{12,4},{14,6},{16,8},... | collective-permute-start | bytes 98312 | tf_op jit(solution)/shard_map/ppermute | solution.py:27
  1108.3 46.1 %collective-permute-start.194 = (bf16[16,1024]{1,0:T(8,128)(2,1)S(1)}, bf16[16,1024]{1,0:T(8,128)(2,1)S(1)}, u32[]{:S(2)}, u32[]{:S(2)}) collective-permute-start(bf16[16,1024]{1,0:T(8,128)(2,1)S(1)} %get-tuple-element.74), channel_id=1, source_target_pairs={{0,118},{2,120},{4,122},{6,124},{8,126},{10,0},{12,2},{14,4},{16,6... | collective-permute-start | bytes 98312 | tf_op jit(solution)/shard_map/ppermute | solution.py:27
  1398.7 48.0 %collective-permute-start.126 = (bf16[1024,1024]{1,0:T(8,128)(2,1)S(1)}, bf16[1024,1024]{1,0:T(8,128)(2,1)}, u32[]{:S(2)}, u32[]{:S(2)}) collective-permute-start(bf16[1024,1024]{1,0:T(8,128)(2,1)S(1)} %bitcast.928), channel_id=1, source_target_pairs={{0,1},{1,0},{2,3},{3,2},{4,5},{5,4},{6,7},{7,6},{8,9},{9,8},{10,11... | collective-permute-start | bytes 6291464 | tf_op jit(solution)/shard_map/ppermute | solution.py:61
  1418.3 45.8 %collective-permute-start.253 = (bf16[1024,1024]{1,0:T(8,128)(2,1)}, bf16[1024,1024]{1,0:T(8,128)(2,1)}, u32[]{:S(2)}, u32[]{:S(2)}) collective-permute-start(bf16[1024,1024]{1,0:T(8,128)(2,1)} %bitcast.406), channel_id=1, source_target_pairs={{0,1},{1,0},{2,3},{3,2},{4,5},{5,4},{6,7},{7,6},{8,9},{9,8},{10,11... | collective-permute-start | bytes 6291464 | tf_op jit(solution)/shard_map/ppermute | solution.py:61
  (237 other events, 7616.4 us)

commit v3 on v1

v3 whole, which is shorter than its diff:
```python
import jax
import jax.numpy as jnp
from jax import lax
from jax.sharding import PartitionSpec as P

SPREAD = ("row", "lmk")


def normalize(matrix_rows):
    widened = matrix_rows.astype(jnp.float32)
    scale = lax.rsqrt(jnp.sum(widened * widened, axis=-1, keepdims=True) + 1e-06)
    return (widened * scale).astype(jnp.bfloat16)


def kernel_of(cosine, widths, weights):
    running = jnp.zeros(cosine.shape, jnp.float32)
    for which in range(widths.shape[0]):
        running = running + weights[which] * jnp.exp(2.0 * widths[which] * cosine)
    return running


def inner_products(unit_rows, landmark):
    return jnp.einsum("rd,md->rm", unit_rows, landmark, preferred_element_type=jnp.float32)


def select_rows(rows, picks):
    onehot = (picks[:, None] == lax.broadcasted_iota(jnp.int32, (picks.shape[0], rows.shape[0]), 1))
    chosen = jnp.dot(onehot.astype(rows.dtype), rows, preferred_element_type=jnp.float32)
    return chosen.astype(rows.dtype)


def swap_cores(value):
    return lax.ppermute(value, "bw", [(0, 1), (1, 0)])


def per_device(
    embeddings, candidates, block_owner, landmark_picks, inverse_width, mixture, whitening
):
    unit_rows = normalize(embeddings)
    block_count, block_rows = landmark_picks.shape
    cores = lax.axis_size("bw")
    half = block_rows // cores
    core = lax.axis_index("bw")
    here = lax.axis_index(SPREAD)
    widths = jnp.concatenate([inverse_width, swap_cores(inverse_width)])
    weights = jnp.concatenate([mixture, swap_cores(mixture)])
    pieces = []
    for number in range(block_count):
        picks = lax.dynamic_slice_in_dim(landmark_picks[number], core * half, half)
        chosen = normalize(select_rows(candidates, picks))
        chosen = jnp.where(here == block_owner[number], chosen, jnp.zeros_like(chosen))
        pieces.append(chosen)
    arrived = lax.psum(pieces, SPREAD)
    features = jnp.zeros((unit_rows.shape[0], whitening.shape[1]), jnp.float32)
    quarters = []
    for number, mine in enumerate(arrived):
        quarters.append((number, core, mine))
    for number, mine in enumerate(arrived):
        quarters.append((number, 1 - core, swap_cores(mine)))
    for number, which, landmark in quarters:
        kernel = kernel_of(inner_products(unit_rows, landmark), widths, weights).astype(jnp.bfloat16)
        start = number * block_rows + which * half
        rows = lax.dynamic_slice_in_dim(whitening, start, half, axis=0)
        features = features + jnp.dot(kernel, rows, preferred_element_type=jnp.float32)
    return features.astype(jnp.bfloat16)


def solution(mesh):
    in_specs = (
        P(SPREAD, None),
        P(SPREAD, None),
        P(),
        P(),
        P("bw"),
        P("bw"),
        P(None, "bw"),
    )
    out_specs = P(SPREAD, "bw")
    return jax.shard_map(
        per_device, mesh=mesh, in_specs=in_specs, out_specs=out_specs, check_vma=False
    )
```

time: 243 us -> 242 us (level)
  matrix products: 37.2 us -> 68.5 us
  local copies, waits for them, and re-layouts: 19.6 us -> 4.87 us
  waiting for transfers between devices: 153 us -> 141 us
  blocking collectives: 4.51 us -> 0 us
  other arithmetic: 7.36 us -> 4.11 us
  starting transfers between devices: 0.08 us -> 3.07 us
    dot_general x3 -> x6, matrix products: 37.2 us -> 68.5 us  [the longest x4 55.5 us: per_device(): jnp.dot(kernel, rows, preferred_element_type=jnp.float32)]
    gather x2 -> x0, local copies, waits for them, and re-layouts: 16.4 us -> none  [per_device(): chosen = normalize(jnp.take(candidates, picks, axis=0))]
    all_gather x2 -> x0, waiting for transfers between devices: 11.3 us -> none  [per_device(): blocks = [lax.all_gather(piece, 'bw', tiled=True) for piece in arrived]]
    unnamed x1 -> x0, blocking collectives: 4.51 us -> none
    ppermute x0 -> x4, starting transfers between devices: none -> 3.07 us  [swap_cores(): return lax.ppermute(value, 'bw', [(0, 1), (1, 0)])]
    reduce_sum x3 -> x1, other arithmetic: 3.3 us -> 0.23 us  [normalize(): jnp.sum(widened * widened, axis=-1, keepdims=True) + 1e-06]
  transfers between devices with their start and end apart: 3 -> 5, of which waited for: 3 -> 1; matrix products, arithmetic and copies ran while one was open for 6% -> 12% of each run, Pallas kernels for 0% -> 0%
where the time goes in v3:
time: 242 us; the launch traced here: 241 us
  waiting for transfers between devices  141 us (58%)
  matrix products  68.5 us (28%)
  between operations  19.8 us (8%)
  local copies, waits for them, and re-layouts  4.87 us (2%)
  other arithmetic  4.11 us (2%)
  starting transfers between devices  3.07 us (1%)
    psum x1, waiting for transfers between devices, per_device(): arrived = lax.psum(pieces, SPREAD)  141 us
    dot_general x4, matrix products, per_device(): jnp.dot(kernel, rows, preferred_element_type=jnp.float32)  55.5 us
    dot_general x2, matrix products, select_rows(): jnp.dot(onehot.astype(rows.dtype), rows, preferred_element_type=jnp.float32)  13 us
  transfers between devices with their start and end apart: 5, of which 1 were waited for; matrix products, arithmetic and copies ran while one was open for 12% of the time, Pallas kernels for 0%

profile of v3, /device:TPU:1, one launch (start us, length us, event | category | flops | bytes accessed | tf_op | source)
XLA Modules:
  0.0 241.4 jit_solution(4417277707269343504)
XLA Ops:
  6.5 0.0 all-reduce.3.cloned.1.call-start
  6.5 1.4 fusion.117
  9.2 0.8 fusion.116
  10.0 0.0 copy-start.3
  10.0 7.6 %fusion.2 = (f32[1024]{0:T(1024)S(1)}, bf16[1024,1024]{0,1:T(8,128)(2,1)S(1)}) fusion(bf16[2048,1024]{1,0:T(8,128)(2,1)} %param.8, s32[1024]{0:T(1024)S(1)} %bitcast.27), kind=kOutput, calls=%fused_computation.8 | convolution fusion | flops 4301257728 | bytes 6299648 | tf_op jit(solution)/shard_map/dot_general | solution.py:28
  17.7 0.0 copy-done.3
  17.7 5.4 %fusion.4 = (f32[1024]{0:T(1024)S(1)}, bf16[1024,1024]{0,1:T(8,128)(2,1)S(1)}) fusion(bf16[2048,1024]{1,0:T(8,128)(2,1)S(1)} %copy-done.3, s32[1024]{0:T(1024)S(1)} %bitcast.26), kind=kOutput, calls=%fused_computation.10 | convolution fusion | flops 4301257728 | bytes 6299648 | tf_op jit(solution)/shard_map/dot_general | solution.py:28
  23.1 1.9 fusion.19
  25.0 1.9 fusion.18
  26.9 0.0 all-reduce.3.cloned.1.call-update
  27.0 141.0 %all-reduce.3.cloned.1.call-done = (bf16[1024,1024]{0,1:T(8,128)(2,1)}, bf16[1024,1024]{0,1:T(8,128)(2,1)}) async-done(((bf16[1024,1024]{0,1:T(8,128)(2,1)}, bf16[1024,1024]{0,1:T(8,128)(2,1)}), (bf16[1024,1024]{0,1:T(8,128)(2,1)}, bf16[1024,1024]{0,1:T(8,128)(2,1)})) %all-reduce.3.cloned.1.call-update) | async-done | bytes 4194320 | tf_op jit(solution)/shard_map/psum | solution.py:53
  167.9 2.2 collective-permute-start.3
  170.2 0.0 copy-done.1
  170.2 0.0 collective-permute-start.1
  170.2 0.0 copy-done.2
  170.2 0.5 collective-permute-start
  170.7 0.7 fusion.119
  173.9 0.0 copy-done
  173.9 0.2 fusion.22
  174.2 0.3 collective-permute-start.2
  174.5 0.7 fusion.118
  175.2 0.0 collective-permute-done.1
  175.2 0.7 fusion.121
  178.3 0.0 collective-permute-done
  178.3 0.7 fusion.120
  179.0 13.6 %fusion.10 = f32[384,2048]{1,0:T(8,128)} fusion(bf16[4096,2048]{1,0:T(8,128)(2,1)} %param.13, s32[]{:T(128)S(6)} %select_n.36, f32[]{:T(128)} %bitcast.17, f32[]{:T(128)} %bitcast.16, f32[]{:T(128)} %bitcast.15, f32[]{:T(128)} %bitcast.14, f32[]{:T(128)} %bitcast.13, f32[]{:T(128)} %bitcast.12, f32[]{:T(128)} %bitcast.11, f32[]{:T(128)} %bitcast.10, ...), kind=kOutput, calls=%fused_computation.16 | convolution fusion | flops 2426535936 | bytes 10233348 | tf_op jit(solution)/shard_map/dot_general | solution.py:64
  192.6 0.0 collective-permute-done.3
  192.6 13.0 %fusion.6 = f32[384,2048]{1,0:T(8,128)} fusion(bf16[4096,2048]{1,0:T(8,128)(2,1)} %param.13, s32[]{:T(128)S(6)} %select_n.38, f32[]{:T(128)} %bitcast.17, f32[]{:T(128)} %bitcast.16, f32[]{:T(128)} %bitcast.15, f32[]{:T(128)} %bitcast.14, f32[]{:T(128)} %bitcast.13, f32[]{:T(128)} %bitcast.12, f32[]{:T(128)} %bitcast.11, f32[]{:T(128)} %bitcast.10, ...), kind=kOutput, calls=%fused_computation.12 | convolution fusion | flops 2426535936 | bytes 10233348 | tf_op jit(solution)/shard_map/dot_general | solution.py:64
  205.6 0.0 collective-permute-done.2
  205.6 13.9 %fusion.8 = f32[384,2048]{1,0:T(8,128)} fusion(bf16[4096,2048]{1,0:T(8,128)(2,1)} %param.13, s32[]{:T(128)S(6)} %select_n.37, f32[]{:T(128)} %bitcast.17, f32[]{:T(128)} %bitcast.16, f32[]{:T(128)} %bitcast.15, f32[]{:T(128)} %bitcast.14, f32[]{:T(128)} %bitcast.13, f32[]{:T(128)} %bitcast.12, f32[]{:T(128)} %bitcast.11, f32[]{:T(128)} %bitcast.10, ...), kind=kOutput, calls=%fused_computation.14 | convolution fusion | flops 2426535936 | bytes 10233348 | tf_op jit(solution)/shard_map/dot_general | solution.py:64
  219.5 0.0 copy-done.4
  219.5 15.0 %add_convert_fusion = bf16[384,2048]{1,0:T(8,128)(2,1)} fusion(f32[384,2048]{1,0:T(8,128)} %fusion.6, f32[384,2048]{1,0:T(8,128)} %fusion.8, f32[384,2048]{1,0:T(8,128)} %fusion.10, bf16[4096,2048]{1,0:T(8,128)(2,1)} %param.13, s32[]{:T(128)S(6)} %select_n.33, f32[]{:T(128)} %bitcast.17, f32[]{:T(128)} %bitcast.16, f32[]{:T(128)} %bitcast.15, f32[]{:T(128)} %bitcast.14, ...), kind=kOutput, calls=%fused_computation.22 | convolution fusion | flops 2429681664 | bytes 18097668 | tf_op jit(solution)/shard_map/dot_general | solution.py:64
  (8 shorter events, 0.0 us)
Async XLA Ops:
  6.5 161.4 %all-reduce.3.cloned.1.call-start = ((), (), s32[]{:S(2)}) async-start(), calls=%async_computation | async-start | bytes 8388608 | tf_op jit(solution)/shard_map/psum | solution.py:53
  10.0 7.7 %copy-start.3 = (bf16[2048,1024]{1,0:T(8,128)(2,1)S(1)}, bf16[2048,1024]{1,0:T(8,128)(2,1)}, u32[]{:S(2)}) copy-start(bf16[2048,1024]{1,0:T(8,128)(2,1)} %param.8) | copy-start | bytes 12582916
  26.9 143.2 %copy-start.1 = (f32[4]{0:T(128)S(1)}, f32[4]{0:T(128)}, u32[]{:S(2)}) copy-start(f32[4]{0:T(128)} %param.11) | copy-start | bytes 52
  26.9 143.2 %copy-start.2 = (f32[4]{0:T(128)S(1)}, f32[4]{0:T(128)}, u32[]{:S(2)}) copy-start(f32[4]{0:T(128)} %param.12) | copy-start | bytes 52
  26.9 147.0 %copy-start = (bf16[384,1024]{1,0:T(8,128)(2,1)S(1)}, bf16[384,1024]{1,0:T(8,128)(2,1)}, u32[]{:S(2)}) copy-start(bf16[384,1024]{1,0:T(8,128)(2,1)} %param.7) | copy-start | bytes 2359300
  167.9 24.7 %collective-permute-start.3 = (bf16[1024,1024]{0,1:T(8,128)(2,1)}, bf16[1024,1024]{0,1:T(8,128)(2,1)S(1)}, u32[]{:S(2)}, u32[]{:S(2)}) collective-permute-start(bf16[1024,1024]{0,1:T(8,128)(2,1)} %get-tuple-element.5), channel_id=1, source_target_pairs={{0,1},{1,0},{2,3},{3,2},{4,5},{5,4},{6,7},{7,6},{8,9},{9,8},{10,11... | collective-permute-start | bytes 6291464 | tf_op jit(solution)/shard_map/ppermute | solution.py:33
  170.2 5.0 %collective-permute-start.1 = (f32[4]{0:T(128)S(1)}, f32[4]{0:T(128)S(1)}, u32[]{:S(2)}, u32[]{:S(2)}) collective-permute-start(f32[4]{0:T(128)S(1)} %copy-done.1), channel_id=1, source_target_pairs={{0,1},{1,0},{2,3},{3,2},{4,5},{5,4},{6,7},{7,6},{8,9},{9,8},{10,11... | collective-permute-start | bytes 56 | tf_op jit(solution)/shard_map/ppermute | solution.py:33
  170.2 8.1 %collective-permute-start = (f32[4]{0:T(128)S(1)}, f32[4]{0:T(128)S(1)}, u32[]{:S(2)}, u32[]{:S(2)}) collective-permute-start(f32[4]{0:T(128)S(1)} %copy-done.2), channel_id=1, source_target_pairs={{0,1},{1,0},{2,3},{3,2},{4,5},{5,4},{6,7},{7,6},{8,9},{9,8},{10,11... | collective-permute-start | bytes 56 | tf_op jit(solution)/shard_map/ppermute | solution.py:33
  174.2 31.5 %collective-permute-start.2 = (bf16[1024,1024]{0,1:T(8,128)(2,1)}, bf16[1024,1024]{0,1:T(8,128)(2,1)}, u32[]{:S(2)}, u32[]{:S(2)}) collective-permute-start(bf16[1024,1024]{0,1:T(8,128)(2,1)} %get-tuple-element.6), channel_id=1, source_target_pairs={{0,1},{1,0},{2,3},{3,2},{4,5},{5,4},{6,7},{7,6},{8,9},{9,8},{10,11... | collective-permute-start | bytes 6291464 | tf_op jit(solution)/shard_map/ppermute | solution.py:33
  205.6 13.9 %copy-start.4 = (bf16[1024,1024]{0,1:T(8,128)(2,1)S(1)}, bf16[1024,1024]{0,1:T(8,128)(2,1)}, u32[]{:S(2)}) copy-start(bf16[1024,1024]{0,1:T(8,128)(2,1)} %get-tuple-element.6) | copy-start | bytes 6291460
Sparse Core Ops, SparseCore 0:
  27.1 140.7 all-reduce.2

commit v4 on v3

v4 whole, which is shorter than its diff:
```python
import jax
import jax.numpy as jnp
from jax import lax
from jax.sharding import PartitionSpec as P

SPREAD = ("row", "lmk")


def normalize(matrix_rows):
    widened = matrix_rows.astype(jnp.float32)
    scale = lax.rsqrt(jnp.sum(widened * widened, axis=-1, keepdims=True) + 1e-06)
    return (widened * scale).astype(jnp.bfloat16)


def kernel_of(cosine, widths, weights):
    scales = 2.0 * widths
    offsets = jnp.log(weights)
    running = jnp.zeros(cosine.shape, jnp.float32)
    for which in range(widths.shape[0]):
        running = running + jnp.exp(scales[which] * cosine + offsets[which])
    return running


def inner_products(unit_rows, landmark):
    return jnp.einsum("rd,md->rm", unit_rows, landmark, preferred_element_type=jnp.float32)


def reorder_columns(kernel, picks, first):
    natural = first + lax.broadcasted_iota(jnp.int32, (kernel.shape[1], picks.shape[0]), 0)
    onehot = (picks[None, :] == natural).astype(kernel.dtype)
    return jnp.dot(kernel, onehot, preferred_element_type=jnp.float32)


def swap_cores(value):
    return lax.ppermute(value, "bw", [(0, 1), (1, 0)])


def per_device(
    embeddings, candidates, block_owner, landmark_picks, inverse_width, mixture, whitening
):
    unit_rows = normalize(embeddings)
    block_count, block_rows = landmark_picks.shape
    cores = lax.axis_size("bw")
    half = block_rows // cores
    core = lax.axis_index("bw")
    here = lax.axis_index(SPREAD)
    widths = jnp.concatenate([inverse_width, swap_cores(inverse_width)])
    weights = jnp.concatenate([mixture, swap_cores(mixture)])
    pieces = []
    for number in range(block_count):
        rows = lax.dynamic_slice_in_dim(candidates, core * half, half, axis=0)
        chosen = normalize(rows)
        chosen = jnp.where(here == block_owner[number], chosen, jnp.zeros_like(chosen))
        pieces.append(chosen)
    arrived = lax.psum(pieces, SPREAD)
    features = jnp.zeros((unit_rows.shape[0], whitening.shape[1]), jnp.float32)
    for number, mine in enumerate(arrived):
        ordered = jnp.zeros((unit_rows.shape[0], block_rows), jnp.float32)
        for which, landmark in ((core, mine), (1 - core, swap_cores(mine))):
            kernel = kernel_of(inner_products(unit_rows, landmark), widths, weights)
            ordered = ordered + reorder_columns(
                kernel.astype(jnp.bfloat16), landmark_picks[number], which * half
            )
        rows = lax.dynamic_slice_in_dim(whitening, number * block_rows, block_rows, axis=0)
        features = features + jnp.dot(
            ordered.astype(jnp.bfloat16), rows, preferred_element_type=jnp.float32
        )
    return features.astype(jnp.bfloat16)


def solution(mesh):
    in_specs = (
        P(SPREAD, None),
        P(SPREAD, None),
        P(),
        P(),
        P("bw"),
        P("bw"),
        P(None, "bw"),
    )
    out_specs = P(SPREAD, "bw")
    return jax.shard_map(
        per_device, mesh=mesh, in_specs=in_specs, out_specs=out_specs, check_vma=False
    )
```

time: 242 us -> 253 us (1.045)
  matrix products: 68.5 us -> 85.4 us
  between operations: 19.8 us -> 14.8 us
  other arithmetic: 4.11 us -> 6.85 us
    dot_general x6, matrix products: 68.5 us -> 85.4 us  [the longest x2 46.3 us: per_device(): jnp.dot(ordered.astype(jnp.bfloat16), rows, preferred_element_type=jnp.fl...]
  transfers between devices with their start and end apart: 5 -> 5, of which waited for: 1 -> 1; matrix products, arithmetic and copies ran while one was open for 12% -> 19% of each run, Pallas kernels for 0% -> 0%
where the time goes in v4:
time: 253 us; the launch traced here: 252 us
  waiting for transfers between devices  139 us (55%)
  matrix products  85.4 us (34%)
  between operations  14.8 us (6%)
  other arithmetic  6.85 us (3%)
  starting transfers between devices  3.85 us (2%)
  local copies, waits for them, and re-layouts  2.55 us (1%)
    psum x1, waiting for transfers between devices, per_device(): arrived = lax.psum(pieces, SPREAD)  139 us
    dot_general x2, matrix products, per_device(): jnp.dot(ordered.astype(jnp.bfloat16), rows, preferred_element_type=jnp.fl...  46.3 us
    dot_general x2, matrix products, reorder_columns(): return jnp.dot(kernel, onehot, preferred_element_type=jnp.float32)  33 us
    dot_general x2, matrix products, inner_products(): jnp.einsum('rd,md->rm', unit_rows, landmark, preferred_element_type=jnp.f...  6.08 us
  transfers between devices with their start and end apart: 5, of which 1 were waited for; matrix products, arithmetic and copies ran while one was open for 19% of the time, Pallas kernels for 0%

profile of v4, /device:TPU:1, one launch (start us, length us, event | category | flops | bytes accessed | tf_op | source)
XLA Modules:
  0.0 252.4 jit_solution(14116394206828144302)
XLA Ops:
  6.5 0.0 all-reduce.3.cloned.1.call-start
  6.5 2.1 fusion.12
  8.6 0.0 copy-done.2
  8.6 0.6 fusion.147
  10.5 4.4 %broadcast_select_fusion.1 = (bf16[1024,1024]{1,0:T(8,128)(2,1)}, bf16[1024,1024]{1,0:T(8,128)(2,1)}) fusion(pred[]{:T(512)S(6)} %eq.38, f32[1024]{0:T(1024)S(1)} %add_rsqrt_fusion, bf16[2048,1024]{1,0:T(8,128)(2,1)} %param.8, s32[]{:T(128)S(6)} %select_n.19, pred[]{:T(512)S(6)} %eq.43), kind=kLoop, calls=%fused_computation.28 | loop fusion | flops 5242880 | bytes 6295558 | tf_op jit(solution)/shard_map/jit(_where)/select_n | solution.py:53
  14.9 0.0 all-reduce.3.cloned.1.call-update
  14.9 0.6 copy-done.4
  15.6 1.4 collective-permute-start
  16.9 0.0 copy-done.5
  17.0 0.0 collective-permute-start.1
  17.0 139.0 %all-reduce.3.cloned.1.call-done = (bf16[1024,1024]{1,0:T(8,128)(2,1)}, bf16[1024,1024]{1,0:T(8,128)(2,1)}) async-done(((bf16[1024,1024]{1,0:T(8,128)(2,1)}, bf16[1024,1024]{1,0:T(8,128)(2,1)}), (bf16[1024,1024]{1,0:T(8,128)(2,1)}, bf16[1024,1024]{1,0:T(8,128)(2,1)})) %all-reduce.3.cloned.1.call-update) | async-done | bytes 4194320 | tf_op jit(solution)/shard_map/psum | solution.py:55
  155.9 2.2 collective-permute-start.3
  158.2 0.0 copy-done
  158.2 0.2 fusion.28
  158.4 0.0 copy-done.1
  158.4 0.0 collective-permute-done
  158.5 0.1 maximum_multiply_fusion
  158.5 0.0 collective-permute-done.1
  158.5 0.1 maximum_log_fusion
  158.6 0.6 fusion.148
  159.2 0.7 fusion.149
  159.9 0.2 collective-permute-start.2
  160.1 3.9 %fusion.132 = f32[384,1024]{1,0:T(8,128)} fusion(bf16[1024,1024]{1,0:T(8,128)(2,1)} %get-tuple-element.5, bf16[384,1024]{1,0:T(8,128)(2,1)S(1)} %copy-done, f32[384]{0:T(512)S(1)} %add_rsqrt_fusion.1), kind=kOutput, calls=%fused_computation.108 | convolution fusion | flops 806486016 | bytes 4457984 | tf_op jit(solution)/shard_map/rd,md->rm/dot_general | solution.py:25
  164.0 0.0 copy-done.3
  164.0 2.2 fusion.136
  166.2 0.0 collective-permute-done.3
  166.2 15.7 %fusion.4 = f32[384,2048]{1,0:T(8,128)} fusion(s32[2048]{0:T(1024)S(1)} %bitcast.26, s32[1024]{0:T(1024)S(1)} %iota_add_fusion, f32[]{:T(128)} %bitcast.16, f32[]{:T(128)} %bitcast.15, f32[]{:T(128)} %bitcast.14, f32[]{:T(128)} %bitcast.13, f32[]{:T(128)} %bitcast.12, f32[]{:T(128)} %bitcast.11, f32[]{:T(128)} %bitcast.10, f32[]{:T(128)} %bitcast.9, ...), kind=kOutput, calls=%fused_computation.4 | convolution fusion | flops 2428633088 | bytes 6043200 | tf_op jit(solution)/shard_map/dot_general | solution.py:31
  181.9 23.3 %fusion = f32[384,2048]{1,0:T(8,128)} fusion(bf16[4096,2048]{1,0:T(8,128)(2,1)} %param.13, f32[384,2048]{1,0:T(8,128)} %fusion.4, s32[2048]{0:T(1024)S(1)} %bitcast.27, s32[1024]{0:T(1024)S(1)} %iota_add_fusion.1, f32[384,1024]{1,0:T(8,128)} %fusion.132, f32[]{:T(128)} %bitcast.16, f32[]{:T(128)} %bitcast.15, f32[]{:T(128)} %bitcast.14, f32[]{:T(128)} %bitcast.13, ...), kind=kOutput, calls=%fused_computation | convolution fusion | flops 4844945408 | bytes 16273408 | tf_op jit(solution)/shard_map/dot_general | solution.py:65
  205.2 0.0 collective-permute-done.2
  205.2 17.4 %fusion.8 = f32[384,2048]{1,0:T(8,128)} fusion(s32[2048]{0:T(1024)S(1)} %bitcast.24, s32[1024]{0:T(1024)S(1)} %iota_add_fusion, f32[]{:T(128)} %bitcast.16, f32[]{:T(128)} %bitcast.15, f32[]{:T(128)} %bitcast.14, f32[]{:T(128)} %bitcast.13, f32[]{:T(128)} %bitcast.12, f32[]{:T(128)} %bitcast.11, f32[]{:T(128)} %bitcast.10, f32[]{:T(128)} %bitcast.9, ...), kind=kOutput, calls=%fused_computation.8 | convolution fusion | flops 2428633088 | bytes 6043200 | tf_op jit(solution)/shard_map/dot_general | solution.py:31
  222.6 0.0 copy-done.6
  222.6 23.0 %add_convert_fusion = bf16[384,2048]{1,0:T(8,128)(2,1)} fusion(f32[384,2048]{1,0:T(8,128)} %fusion, bf16[4096,2048]{1,0:T(8,128)(2,1)} %param.13, f32[384,2048]{1,0:T(8,128)} %fusion.8, s32[2048]{0:T(1024)S(1)} %bitcast.25, s32[1024]{0:T(1024)S(1)} %iota_add_fusion.1, f32[384,1024]{1,0:T(8,128)S(1)} %copy-done.6, f32[]{:T(128)} %bitcast.16, f32[]{:T(128)} %bitcast.15, ...), kind=kOutput, calls=%fused_computation.24 | convolution fusion | flops 4846518272 | bytes 17846272 | tf_op jit(solution)/shard_map/dot_general | solution.py:65
  (12 shorter events, 0.0 us)
Async XLA Ops:
  6.5 2.1 copy-start.2
  6.5 149.4 %all-reduce.3.cloned.1.call-start = ((), (), s32[]{:S(2)}) async-start(), calls=%async_computation | async-start | bytes 8388608 | tf_op jit(solution)/shard_map/psum | solution.py:55
  14.9 0.7 copy-start.4
  14.9 2.0 copy-start.5
  14.9 143.3 %copy-start = (bf16[384,1024]{1,0:T(8,128)(2,1)S(1)}, bf16[384,1024]{1,0:T(8,128)(2,1)}, u32[]{:S(2)}) copy-start(bf16[384,1024]{1,0:T(8,128)(2,1)} %param.7) | copy-start | bytes 2359300
  14.9 143.5 %copy-start.1 = (s32[2,2048]{1,0:T(2,128)S(1)}, s32[2,2048]{1,0:T(2,128)}, u32[]{:S(2)}) copy-start(s32[2,2048]{1,0:T(2,128)} %param.10) | copy-start | bytes 49156
  15.6 142.9 %collective-permute-start = (f32[4]{0:T(128)S(1)}, f32[4]{0:T(128)S(1)}, u32[]{:S(2)}, u32[]{:S(2)}) collective-permute-start(f32[4]{0:T(128)S(1)} %copy-done.4), channel_id=1, source_target_pairs={{0,1},{1,0},{2,3},{3,2},{4,5},{5,4},{6,7},{7,6},{8,9},{9,8},{10,11... | collective-permute-start | bytes 56 | tf_op jit(solution)/shard_map/ppermute | solution.py:35
  17.0 141.6 %collective-permute-start.1 = (f32[4]{0:T(128)S(1)}, f32[4]{0:T(128)S(1)}, u32[]{:S(2)}, u32[]{:S(2)}) collective-permute-start(f32[4]{0:T(128)S(1)} %copy-done.5), channel_id=1, source_target_pairs={{0,1},{1,0},{2,3},{3,2},{4,5},{5,4},{6,7},{7,6},{8,9},{9,8},{10,11... | collective-permute-start | bytes 56 | tf_op jit(solution)/shard_map/ppermute | solution.py:35
  155.9 10.3 %collective-permute-start.3 = (bf16[1024,1024]{1,0:T(8,128)(2,1)}, bf16[1024,1024]{1,0:T(8,128)(2,1)S(1)}, u32[]{:S(2)}, u32[]{:S(2)}) collective-permute-start(bf16[1024,1024]{1,0:T(8,128)(2,1)} %get-tuple-element.5), channel_id=1, source_target_pairs={{0,1},{1,0},{2,3},{3,2},{4,5},{5,4},{6,7},{7,6},{8,9},{9,8},{10,11... | collective-permute-start | bytes 6291464 | tf_op jit(solution)/shard_map/ppermute | solution.py:35
  159.9 4.1 %copy-start.3 = (bf16[1024,1024]{1,0:T(8,128)(2,1)S(1)}, bf16[1024,1024]{1,0:T(8,128)(2,1)}, u32[]{:S(2)}) copy-start(bf16[1024,1024]{1,0:T(8,128)(2,1)} %get-tuple-element.6) | copy-start | bytes 6291460
  159.9 45.3 %collective-permute-start.2 = (bf16[1024,1024]{1,0:T(8,128)(2,1)}, bf16[1024,1024]{1,0:T(8,128)(2,1)}, u32[]{:S(2)}, u32[]{:S(2)}) collective-permute-start(bf16[1024,1024]{1,0:T(8,128)(2,1)} %get-tuple-element.6), channel_id=1, source_target_pairs={{0,1},{1,0},{2,3},{3,2},{4,5},{5,4},{6,7},{7,6},{8,9},{9,8},{10,11... | collective-permute-start | bytes 6291464 | tf_op jit(solution)/shard_map/ppermute | solution.py:35
  205.2 17.4 %copy-start.6 = (f32[384,1024]{1,0:T(8,128)S(1)}, f32[384,1024]{1,0:T(8,128)}, u32[]{:S(2)}) copy-start(f32[384,1024]{1,0:T(8,128)} %fusion.136) | copy-start | bytes 4718596
Sparse Core Ops, SparseCore 0:
  15.1 140.8 all-reduce.2

commit v5 on v4

--- a/solution.py
+++ b/solution.py
@@ -58,9 +58,8 @@
         ordered = jnp.zeros((unit_rows.shape[0], block_rows), jnp.float32)
         for which, landmark in ((core, mine), (1 - core, swap_cores(mine))):
             kernel = kernel_of(inner_products(unit_rows, landmark), widths, weights)
-            ordered = ordered + reorder_columns(
-                kernel.astype(jnp.bfloat16), landmark_picks[number], which * half
-            )
+            kernel = lax.optimization_barrier(kernel.astype(jnp.bfloat16))
+            ordered = ordered + reorder_columns(kernel, landmark_picks[number], which * half)
         rows = lax.dynamic_slice_in_dim(whitening, number * block_rows, block_rows, axis=0)
         features = features + jnp.dot(
             ordered.astype(jnp.bfloat16), rows, preferred_element_type=jnp.float32

time: 253 us -> 254 us (level)
    dot_general x2 -> x4, matrix products: 6.08 us -> 56.1 us  [inner_products(): jnp.einsum('rd,md->rm', unit_rows, landmark, preferred_element_type=jnp.f...]
    dot_general x2, matrix products: 33 us -> 7.23 us  [reorder_columns(): return jnp.dot(kernel, onehot, preferred_element_type=jnp.float32)]
    dot_general x2, matrix products: 46.3 us -> 22.7 us  [per_device(): jnp.dot(ordered.astype(jnp.bfloat16), rows, preferred_element_type=jnp.fl...]
  transfers between devices with their start and end apart: 5 -> 5, of which waited for: 1 -> 1; matrix products, arithmetic and copies ran while one was open for 19% -> 17% of each run, Pallas kernels for 0% -> 0%
where the time goes in v5:
time: 254 us; the launch traced here: 253 us
  waiting for transfers between devices  139 us (55%)
  matrix products  86.1 us (34%)
  between operations  14.8 us (6%)
  other arithmetic  6.79 us (3%)
  starting transfers between devices  3.65 us (1%)
  local copies, waits for them, and re-layouts  2.67 us (1%)
    psum x1, waiting for transfers between devices, per_device(): arrived = lax.psum(pieces, SPREAD)  139 us
    dot_general x4, matrix products, inner_products(): jnp.einsum('rd,md->rm', unit_rows, landmark, preferred_element_type=jnp.f...  56.1 us
    dot_general x2, matrix products, per_device(): jnp.dot(ordered.astype(jnp.bfloat16), rows, preferred_element_type=jnp.fl...  22.7 us
    dot_general x2, matrix products, reorder_columns(): return jnp.dot(kernel, onehot, preferred_element_type=jnp.float32)  7.23 us
  transfers between devices with their start and end apart: 5, of which 1 were waited for; matrix products, arithmetic and copies ran while one was open for 17% of the time, Pallas kernels for 0%

profile of v5, /device:TPU:1, one launch (start us, length us, event | category | flops | bytes accessed | tf_op | source)
XLA Modules:
  0.0 252.7 jit_solution(856047712066727170)
XLA Ops:
  6.5 0.0 all-reduce.3.cloned.1.call-start
  6.5 2.1 fusion.12
  8.6 0.0 copy-done.2
  8.6 0.6 fusion.51
  10.6 4.3 %broadcast_select_fusion.1 = (bf16[1024,1024]{1,0:T(8,128)(2,1)}, bf16[1024,1024]{1,0:T(8,128)(2,1)}) fusion(pred[]{:T(512)S(6)} %eq.38, f32[1024]{0:T(1024)S(1)} %add_rsqrt_fusion, bf16[2048,1024]{1,0:T(8,128)(2,1)} %param.8, s32[]{:T(128)S(6)} %select_n.19, pred[]{:T(512)S(6)} %eq.43), kind=kLoop, calls=%fused_computation.28 | loop fusion | flops 5242880 | bytes 6295558 | tf_op jit(solution)/shard_map/jit(_where)/select_n | solution.py:53
  14.9 0.0 all-reduce.3.cloned.1.call-update
  14.9 0.6 copy-done.4
  15.5 1.4 collective-permute-start
  16.9 0.0 copy-done.5
  16.9 0.0 collective-permute-start.1
  16.9 0.0 copy-done
  17.0 0.2 fusion.28
  17.2 138.7 %all-reduce.3.cloned.1.call-done = (bf16[1024,1024]{1,0:T(8,128)(2,1)}, bf16[1024,1024]{1,0:T(8,128)(2,1)}) async-done(((bf16[1024,1024]{1,0:T(8,128)(2,1)}, bf16[1024,1024]{1,0:T(8,128)(2,1)}), (bf16[1024,1024]{1,0:T(8,128)(2,1)}, bf16[1024,1024]{1,0:T(8,128)(2,1)})) %all-reduce.3.cloned.1.call-update) | async-done | bytes 4194320 | tf_op jit(solution)/shard_map/psum | solution.py:55
  155.9 2.2 collective-permute-start.3
  158.1 0.0 copy-done.1
  158.2 0.0 collective-permute-done
  158.2 0.1 maximum_multiply_fusion
  158.2 0.0 collective-permute-start.2
  158.3 0.0 collective-permute-done.1
  158.3 0.1 maximum_log_fusion
  158.4 0.7 fusion.52
  159.1 0.7 fusion.53
  159.7 14.7 %add_convert_fusion.4 = bf16[384,1024]{1,0:T(8,128)(2,1)S(1)} fusion(f32[]{:T(128)} %bitcast.16, f32[]{:T(128)} %bitcast.15, f32[]{:T(128)} %bitcast.14, f32[]{:T(128)} %bitcast.13, f32[]{:T(128)} %bitcast.12, f32[]{:T(128)} %bitcast.11, f32[]{:T(128)} %bitcast.10, f32[]{:T(128)} %bitcast.9, f32[]{:T(128)} %bitcast.8, f32[]{:T(128)} %bitcast.7, ...), kind=kOutput, calls=%fused_computation.34 | convolution fusion | flops 815923200 | bytes 3671616 | tf_op jit(solution)/shard_map/rd,md->rm/dot_general | solution.py:25
  174.5 13.7 %add_convert_fusion.6 = bf16[384,1024]{1,0:T(8,128)(2,1)S(1)} fusion(f32[]{:T(128)} %bitcast.16, f32[]{:T(128)} %bitcast.15, f32[]{:T(128)} %bitcast.14, f32[]{:T(128)} %bitcast.13, f32[]{:T(128)} %bitcast.12, f32[]{:T(128)} %bitcast.11, f32[]{:T(128)} %bitcast.10, f32[]{:T(128)} %bitcast.9, f32[]{:T(128)} %bitcast.8, f32[]{:T(128)} %bitcast.7, ...), kind=kOutput, calls=%fused_computation.36 | convolution fusion | flops 815923200 | bytes 3671616 | tf_op jit(solution)/shard_map/rd,md->rm/dot_general | solution.py:25
  188.2 0.0 collective-permute-done.3
  188.3 13.7 %add_convert_fusion.3 = bf16[384,1024]{1,0:T(8,128)(2,1)S(1)} fusion(f32[]{:T(128)} %bitcast.16, f32[]{:T(128)} %bitcast.15, f32[]{:T(128)} %bitcast.14, f32[]{:T(128)} %bitcast.13, f32[]{:T(128)} %bitcast.12, f32[]{:T(128)} %bitcast.11, f32[]{:T(128)} %bitcast.10, f32[]{:T(128)} %bitcast.9, f32[]{:T(128)} %bitcast.8, f32[]{:T(128)} %bitcast.7, ...), kind=kOutput, calls=%fused_computation.33 | convolution fusion | flops 815923200 | bytes 3671616 | tf_op jit(solution)/shard_map/rd,md->rm/dot_general | solution.py:25
  202.0 0.0 collective-permute-done.2
  202.0 13.9 %add_convert_fusion.5 = bf16[384,1024]{1,0:T(8,128)(2,1)S(1)} fusion(f32[]{:T(128)} %bitcast.16, f32[]{:T(128)} %bitcast.15, f32[]{:T(128)} %bitcast.14, f32[]{:T(128)} %bitcast.13, f32[]{:T(128)} %bitcast.12, f32[]{:T(128)} %bitcast.11, f32[]{:T(128)} %bitcast.10, f32[]{:T(128)} %bitcast.9, f32[]{:T(128)} %bitcast.8, f32[]{:T(128)} %bitcast.7, ...), kind=kOutput, calls=%fused_computation.35 | convolution fusion | flops 815923200 | bytes 3671616 | tf_op jit(solution)/shard_map/rd,md->rm/dot_general | solution.py:25
  215.9 3.6 %fusion.4 = f32[384,2048]{1,0:T(8,128)} fusion(bf16[384,1024]{1,0:T(8,128)(2,1)S(1)} %add_convert_fusion.3, s32[2048]{0:T(1024)S(1)} %bitcast.30, s32[1024]{0:T(1024)S(1)} %iota_add_fusion), kind=kOutput, calls=%fused_computation.4 | convolution fusion | flops 1612709888 | bytes 3944448 | tf_op jit(solution)/shard_map/dot_general | solution.py:31
  219.5 3.7 %fusion.8 = f32[384,2048]{1,0:T(8,128)} fusion(bf16[384,1024]{1,0:T(8,128)(2,1)S(1)} %add_convert_fusion.5, s32[2048]{0:T(1024)S(1)} %bitcast.28, s32[1024]{0:T(1024)S(1)} %iota_add_fusion), kind=kOutput, calls=%fused_computation.8 | convolution fusion | flops 1612709888 | bytes 3944448 | tf_op jit(solution)/shard_map/dot_general | solution.py:31
  223.2 11.2 %fusion = f32[384,2048]{1,0:T(8,128)} fusion(bf16[4096,2048]{1,0:T(8,128)(2,1)} %param.13, f32[384,2048]{1,0:T(8,128)} %fusion.4, bf16[384,1024]{1,0:T(8,128)(2,1)S(1)} %add_convert_fusion.4, s32[2048]{0:T(1024)S(1)} %bitcast.31, s32[1024]{0:T(1024)S(1)} %iota_add_fusion.1), kind=kOutput, calls=%fused_computation | convolution fusion | flops 4835508224 | bytes 15478784 | tf_op jit(solution)/shard_map/dot_general | solution.py:64
  234.4 11.5 %add_convert_fusion = bf16[384,2048]{1,0:T(8,128)(2,1)} fusion(f32[384,2048]{1,0:T(8,128)} %fusion, bf16[4096,2048]{1,0:T(8,128)(2,1)} %param.13, f32[384,2048]{1,0:T(8,128)} %fusion.8, bf16[384,1024]{1,0:T(8,128)(2,1)S(1)} %add_convert_fusion.6, s32[2048]{0:T(1024)S(1)} %bitcast.29, s32[1024]{0:T(1024)S(1)} %iota_add_fusion.1), kind=kOutput, calls=%fused_computation.24 | convolution fusion | flops 4837081088 | bytes 17051648 | tf_op jit(solution)/shard_map/dot_general | solution.py:64
  (12 shorter events, 0.0 us)
Async XLA Ops:
  6.5 2.1 copy-start.2
  6.5 149.4 %all-reduce.3.cloned.1.call-start = ((), (), s32[]{:S(2)}) async-start(), calls=%async_computation | async-start | bytes 8388608 | tf_op jit(solution)/shard_map/psum | solution.py:55
  14.9 0.7 copy-start.4
  14.9 2.0 copy-start.5
  14.9 2.1 copy-start
  14.9 143.2 %copy-start.1 = (s32[2,2048]{1,0:T(2,128)S(1)}, s32[2,2048]{1,0:T(2,128)}, u32[]{:S(2)}) copy-start(s32[2,2048]{1,0:T(2,128)} %param.10) | copy-start | bytes 49156
  15.5 142.6 %collective-permute-start = (f32[4]{0:T(128)S(1)}, f32[4]{0:T(128)S(1)}, u32[]{:S(2)}, u32[]{:S(2)}) collective-permute-start(f32[4]{0:T(128)S(1)} %copy-done.4), channel_id=1, source_target_pairs={{0,1},{1,0},{2,3},{3,2},{4,5},{5,4},{6,7},{7,6},{8,9},{9,8},{10,11... | collective-permute-start | bytes 56 | tf_op jit(solution)/shard_map/ppermute | solution.py:35
  16.9 141.4 %collective-permute-start.1 = (f32[4]{0:T(128)S(1)}, f32[4]{0:T(128)S(1)}, u32[]{:S(2)}, u32[]{:S(2)}) collective-permute-start(f32[4]{0:T(128)S(1)} %copy-done.5), channel_id=1, source_target_pairs={{0,1},{1,0},{2,3},{3,2},{4,5},{5,4},{6,7},{7,6},{8,9},{9,8},{10,11... | collective-permute-start | bytes 56 | tf_op jit(solution)/shard_map/ppermute | solution.py:35
  155.9 32.3 %collective-permute-start.3 = (bf16[1024,1024]{1,0:T(8,128)(2,1)}, bf16[1024,1024]{1,0:T(8,128)(2,1)S(1)}, u32[]{:S(2)}, u32[]{:S(2)}) collective-permute-start(bf16[1024,1024]{1,0:T(8,128)(2,1)} %get-tuple-element.5), channel_id=1, source_target_pairs={{0,1},{1,0},{2,3},{3,2},{4,5},{5,4},{6,7},{7,6},{8,9},{9,8},{10,11... | collective-permute-start | bytes 6291464 | tf_op jit(solution)/shard_map/ppermute | solution.py:35
  158.2 43.8 %collective-permute-start.2 = (bf16[1024,1024]{1,0:T(8,128)(2,1)}, bf16[1024,1024]{1,0:T(8,128)(2,1)S(1)}, u32[]{:S(2)}, u32[]{:S(2)}) collective-permute-start(bf16[1024,1024]{1,0:T(8,128)(2,1)} %get-tuple-element.6), channel_id=1, source_target_pairs={{0,1},{1,0},{2,3},{3,2},{4,5},{5,4},{6,7},{7,6},{8,9},{9,8},{10,11... | collective-permute-start | bytes 6291464 | tf_op jit(solution)/shard_map/ppermute | solution.py:35
  159.7 14.7 %copy-start.3 = (bf16[1024,1024]{1,0:T(8,128)(2,1)S(1)}, bf16[1024,1024]{1,0:T(8,128)(2,1)}, u32[]{:S(2)}) copy-start(bf16[1024,1024]{1,0:T(8,128)(2,1)} %get-tuple-element.6) | copy-start | bytes 6291460
Sparse Core Ops, SparseCore 0:
  15.0 140.8 all-reduce.2

commit v6 on v3

--- a/solution.py
+++ b/solution.py
@@ -51,16 +51,27 @@
         chosen = jnp.where(here == block_owner[number], chosen, jnp.zeros_like(chosen))
         pieces.append(chosen)
     arrived = lax.psum(pieces, SPREAD)
+    share = unit_rows.shape[0] // cores
+    own_rows = lax.dynamic_slice_in_dim(unit_rows, core * share, share, axis=0)
     features = jnp.zeros((unit_rows.shape[0], whitening.shape[1]), jnp.float32)
-    quarters = []
     for number, mine in enumerate(arrived):
-        quarters.append((number, core, mine))
-    for number, mine in enumerate(arrived):
-        quarters.append((number, 1 - core, swap_cores(mine)))
-    for number, which, landmark in quarters:
-        kernel = kernel_of(inner_products(unit_rows, landmark), widths, weights).astype(jnp.bfloat16)
-        start = number * block_rows + which * half
-        rows = lax.dynamic_slice_in_dim(whitening, start, half, axis=0)
+        other = swap_cores(mine)
+        parts = [
+            kernel_of(inner_products(own_rows, landmark), widths, weights).astype(jnp.bfloat16)
+            for landmark in (mine, other)
+        ]
+        own_kernel = jnp.where(
+            core == 0,
+            jnp.concatenate(parts, axis=1),
+            jnp.concatenate(parts[::-1], axis=1),
+        )
+        other_kernel = swap_cores(own_kernel)
+        kernel = jnp.where(
+            core == 0,
+            jnp.concatenate([own_kernel, other_kernel], axis=0),
+            jnp.concatenate([other_kernel, own_kernel], axis=0),
+        )
+        rows = lax.dynamic_slice_in_dim(whitening, number * block_rows, block_rows, axis=0)
         features = features + jnp.dot(kernel, rows, preferred_element_type=jnp.float32)
     return features.astype(jnp.bfloat16)
 

time: 242 us -> 229 us (0.946)
  matrix products: 68.5 us -> 54.6 us
    dot_general x4 -> x2, matrix products: 55.5 us -> 8.01 us  [per_device(): jnp.dot(kernel, rows, preferred_element_type=jnp.float32)]
    dot_general x0 -> x4, matrix products: none -> 30.6 us  [inner_products(): jnp.einsum('rd,md->rm', unit_rows, landmark, preferred_element_type=jnp.f...]
    dot_general x2, matrix products: 13 us -> 16 us  [select_rows(): jnp.dot(onehot.astype(rows.dtype), rows, preferred_element_type=jnp.float32)]
  transfers between devices with their start and end apart: 5 -> 7, of which waited for: 1 -> 1; matrix products, arithmetic and copies ran while one was open for 12% -> 17% of each run, Pallas kernels for 0% -> 0%
where the time goes in v6:
time: 229 us; the launch traced here: 228 us
  waiting for transfers between devices  141 us (62%)
  matrix products  54.6 us (24%)
  between operations  20 us (9%)
  other arithmetic  4.94 us (2%)
  local copies, waits for them, and re-layouts  4.12 us (2%)
  starting transfers between devices  3.68 us (2%)
    psum x1, waiting for transfers between devices, per_device(): arrived = lax.psum(pieces, SPREAD)  141 us
    dot_general x4, matrix products, inner_products(): jnp.einsum('rd,md->rm', unit_rows, landmark, preferred_element_type=jnp.f...  30.6 us
    dot_general x2, matrix products, select_rows(): jnp.dot(onehot.astype(rows.dtype), rows, preferred_element_type=jnp.float32)  16 us
    dot_general x2, matrix products, per_device(): jnp.dot(kernel, rows, preferred_element_type=jnp.float32)  8.01 us
  transfers between devices with their start and end apart: 7, of which 1 were waited for; matrix products, arithmetic and copies ran while one was open for 17% of the time, Pallas kernels for 0%

profile of v6, /device:TPU:1, one launch (start us, length us, event | category | flops | bytes accessed | tf_op | source)
XLA Modules:
  0.0 228.3 jit_solution(12239653883930893705)
XLA Ops:
  6.5 0.8 fusion.33
  7.4 7.5 %fusion.6 = (f32[1024]{0:T(1024)S(1)}, bf16[1024,1024]{0,1:T(8,128)(2,1)S(1)}) fusion(bf16[2048,1024]{1,0:T(8,128)(2,1)} %param.8, s32[1024]{0:T(1024)S(1)} %bitcast.31), kind=kOutput, calls=%fused_computation.12 | convolution fusion | flops 4301257728 | bytes 6299648 | tf_op jit(solution)/shard_map/dot_general | solution.py:28
  14.9 0.6 fusion.38
  15.5 8.5 %fusion.8 = (f32[1024]{0:T(1024)S(1)}, bf16[1024,1024]{0,1:T(8,128)(2,1)}) fusion(bf16[2048,1024]{1,0:T(8,128)(2,1)} %param.8, s32[1024]{0:T(1024)S(1)} %bitcast.30), kind=kOutput, calls=%fused_computation.14 | convolution fusion | flops 4301257728 | bytes 6299648 | tf_op jit(solution)/shard_map/dot_general | solution.py:28
  25.3 1.9 fusion.15
  27.2 2.0 fusion.14
  29.2 0.0 all-reduce.3.cloned.1.call-update
  29.2 141.0 %all-reduce.3.cloned.1.call-done = (bf16[1024,1024]{0,1:T(8,128)(2,1)}, bf16[1024,1024]{0,1:T(8,128)(2,1)}) async-done(((bf16[1024,1024]{0,1:T(8,128)(2,1)}, bf16[1024,1024]{0,1:T(8,128)(2,1)}), (bf16[1024,1024]{0,1:T(8,128)(2,1)}, bf16[1024,1024]{0,1:T(8,128)(2,1)})) %all-reduce.3.cloned.1.call-update) | async-done | bytes 4194320 | tf_op jit(solution)/shard_map/psum | solution.py:53
  170.2 2.2 collective-permute-start.4
  172.4 0.5 collective-permute-start
  172.9 0.2 convert_element_type.41
  173.1 0.7 fusion.35
  176.4 0.2 multiply_reduce_fusion
  176.6 0.2 collective-permute-start.2
  176.8 0.1 dynamic-slice.2
  176.9 0.7 fusion.34
  177.5 0.1 fusion.30
  177.6 0.6 fusion.37
  180.8 0.6 fusion.36
  181.4 8.4 %add_convert_fusion.2 = bf16[192,1024]{1,0:T(8,128)(2,1)S(1)} fusion(f32[]{:T(128)} %bitcast.17, f32[]{:T(128)} %bitcast.16, f32[]{:T(128)} %bitcast.15, f32[]{:T(128)} %bitcast.14, f32[]{:T(128)} %bitcast.13, f32[]{:T(128)} %bitcast.12, f32[]{:T(128)} %bitcast.11, f32[]{:T(128)} %bitcast.10, f32[]{:T(128)} %bitcast.9, f32[]{:T(128)} %bitcast.8, ...), kind=kOutput, calls=%fused_computation.43 | convolution fusion | flops 407371776 | bytes 2883648 | tf_op jit(solution)/shard_map/rd,md->rm/dot_general | solution.py:23
  189.8 0.0 slice-start.1
  189.8 8.6 %add_convert_fusion.1 = bf16[192,1024]{1,0:T(8,128)(2,1)S(1)} fusion(f32[]{:T(128)} %bitcast.17, f32[]{:T(128)} %bitcast.16, f32[]{:T(128)} %bitcast.15, f32[]{:T(128)} %bitcast.14, f32[]{:T(128)} %bitcast.13, f32[]{:T(128)} %bitcast.12, f32[]{:T(128)} %bitcast.11, f32[]{:T(128)} %bitcast.10, f32[]{:T(128)} %bitcast.9, f32[]{:T(128)} %bitcast.8, ...), kind=kOutput, calls=%fused_computation.42 | convolution fusion | flops 407371776 | bytes 2883648 | tf_op jit(solution)/shard_map/rd,md->rm/dot_general | solution.py:23
  198.4 0.3 maximum_select_fusion.5
  198.7 0.0 slice-start.2
  198.7 0.7 collective-permute-start.5
  199.4 6.8 %add_convert_fusion.4 = bf16[192,1024]{1,0:T(8,128)(2,1)S(1)} fusion(f32[]{:T(128)} %bitcast.17, f32[]{:T(128)} %bitcast.16, f32[]{:T(128)} %bitcast.15, f32[]{:T(128)} %bitcast.14, f32[]{:T(128)} %bitcast.13, f32[]{:T(128)} %bitcast.12, f32[]{:T(128)} %bitcast.11, f32[]{:T(128)} %bitcast.10, f32[]{:T(128)} %bitcast.9, f32[]{:T(128)} %bitcast.8, ...), kind=kOutput, calls=%fused_computation.45 | convolution fusion | flops 407371776 | bytes 2883648 | tf_op jit(solution)/shard_map/rd,md->rm/dot_general | solution.py:23
  206.2 0.0 slice-start.3
  206.2 6.8 %add_convert_fusion.3 = bf16[192,1024]{1,0:T(8,128)(2,1)S(1)} fusion(f32[]{:T(128)} %bitcast.17, f32[]{:T(128)} %bitcast.16, f32[]{:T(128)} %bitcast.15, f32[]{:T(128)} %bitcast.14, f32[]{:T(128)} %bitcast.13, f32[]{:T(128)} %bitcast.12, f32[]{:T(128)} %bitcast.11, f32[]{:T(128)} %bitcast.10, f32[]{:T(128)} %bitcast.9, f32[]{:T(128)} %bitcast.8, ...), kind=kOutput, calls=%fused_computation.44 | convolution fusion | flops 407371776 | bytes 2883648 | tf_op jit(solution)/shard_map/rd,md->rm/dot_general | solution.py:23
  213.1 0.3 maximum_select_fusion.4
  213.3 0.1 collective-permute-start.3
  213.5 3.4 %fusion = f32[384,2048]{1,0:T(8,128)S(1)} fusion(bf16[4096,2048]{1,0:T(8,128)(2,1)S(1)} %bitcast.33, bf16[192,2048]{1,0:T(8,128)(2,1)S(1)} %collective-permute-done.5, bf16[192,2048]{1,0:T(8,128)(2,1)S(1)} %maximum_select_fusion.5, pred[]{:T(512)S(6)} %eq.32), kind=kOutput, calls=%fused_computation | convolution fusion | flops 3228303360 | bytes 13107201 | tf_op jit(solution)/shard_map/dot_general | solution.py:75
  216.9 4.6 %add_convert_fusion = bf16[384,2048]{1,0:T(8,128)(2,1)} fusion(f32[384,2048]{1,0:T(8,128)S(1)} %fusion, bf16[4096,2048]{1,0:T(8,128)(2,1)S(1)} %bitcast.33, bf16[192,2048]{1,0:T(8,128)(2,1)S(1)} %collective-permute-done.3, bf16[192,2048]{1,0:T(8,128)(2,1)S(1)} %maximum_select_fusion.4, pred[]{:T(512)S(6)} %eq.32), kind=kOutput, calls=%fused_computation.18 | convolution fusion | flops 3229876224 | bytes 14680065 | tf_op jit(solution)/shard_map/dot_general | solution.py:75
  (30 shorter events, 0.1 us)
Async XLA Ops:
  6.5 163.7 %all-reduce.3.cloned.1.call-start = ((), (), s32[]{:S(2)}) async-start(), calls=%async_computation | async-start | bytes 8388608 | tf_op jit(solution)/shard_map/psum | solution.py:53
  7.4 7.5 %copy-start.4 = (s32[2]{0:T(128)S(1)}, s32[2]{0:T(128)}, u32[]{:S(2)}) copy-start(s32[2]{0:T(128)} %param.9) | copy-start | bytes 28
  25.3 2.0 copy-start.1
  29.2 143.2 %copy-start.2 = (f32[4]{0:T(128)S(1)}, f32[4]{0:T(128)}, u32[]{:S(2)}) copy-start(f32[4]{0:T(128)} %param.11) | copy-start | bytes 52
  29.2 143.2 %copy-start.3 = (f32[4]{0:T(128)S(1)}, f32[4]{0:T(128)}, u32[]{:S(2)}) copy-start(f32[4]{0:T(128)} %param.12) | copy-start | bytes 52
  29.2 143.7 %copy-start = (bf16[384,1024]{1,0:T(8,128)(2,1)S(1)}, bf16[384,1024]{1,0:T(8,128)(2,1)}, u32[]{:S(2)}) copy-start(bf16[384,1024]{1,0:T(8,128)(2,1)} %param.7) | copy-start | bytes 2359300
  170.2 19.6 %collective-permute-start.4 = (bf16[1024,1024]{0,1:T(8,128)(2,1)}, bf16[1024,1024]{0,1:T(8,128)(2,1)}, u32[]{:S(2)}, u32[]{:S(2)}) collective-permute-start(bf16[1024,1024]{0,1:T(8,128)(2,1)} %get-tuple-element.5), channel_id=1, source_target_pairs={{0,1},{1,0},{2,3},{3,2},{4,5},{5,4},{6,7},{7,6},{8,9},{9,8},{10,11... | collective-permute-start | bytes 6291464 | tf_op jit(solution)/shard_map/ppermute | solution.py:33
  172.4 5.2 %collective-permute-start.1 = (f32[4]{0:T(128)S(1)}, f32[4]{0:T(128)S(1)}, u32[]{:S(2)}, u32[]{:S(2)}) collective-permute-start(f32[4]{0:T(128)S(1)} %copy-done.2), channel_id=1, source_target_pairs={{0,1},{1,0},{2,3},{3,2},{4,5},{5,4},{6,7},{7,6},{8,9},{9,8},{10,11... | collective-permute-start | bytes 56 | tf_op jit(solution)/shard_map/ppermute | solution.py:33
  172.4 8.3 %collective-permute-start = (f32[4]{0:T(128)S(1)}, f32[4]{0:T(128)S(1)}, u32[]{:S(2)}, u32[]{:S(2)}) collective-permute-start(f32[4]{0:T(128)S(1)} %copy-done.3), channel_id=1, source_target_pairs={{0,1},{1,0},{2,3},{3,2},{4,5},{5,4},{6,7},{7,6},{8,9},{9,8},{10,11... | collective-permute-start | bytes 56 | tf_op jit(solution)/shard_map/ppermute | solution.py:33
  176.6 29.6 %collective-permute-start.2 = (bf16[1024,1024]{0,1:T(8,128)(2,1)}, bf16[1024,1024]{0,1:T(8,128)(2,1)S(1)}, u32[]{:S(2)}, u32[]{:S(2)}) collective-permute-start(bf16[1024,1024]{0,1:T(8,128)(2,1)} %get-tuple-element.6), channel_id=1, source_target_pairs={{0,1},{1,0},{2,3},{3,2},{4,5},{5,4},{6,7},{7,6},{8,9},{9,8},{10,11... | collective-permute-start | bytes 6291464 | tf_op jit(solution)/shard_map/ppermute | solution.py:33
  181.4 32.1 %slice-start = ((s8[16777216]{0:T(1024)(128)(4,1)}), s8[4194304]{0:T(1024)(128)(4,1)S(1)}, s32[]{:S(2)}) async-start(s8[16777216]{0:T(1024)(128)(4,1)} %bitcast.32), calls=%async_computation.1 | async-start | bytes 8388608
  189.8 9.6 %copy-start.5 = (bf16[1024,1024]{0,1:T(8,128)(2,1)S(1)}, bf16[1024,1024]{0,1:T(8,128)(2,1)}, u32[]{:S(2)}) copy-start(bf16[1024,1024]{0,1:T(8,128)(2,1)} %get-tuple-element.6) | copy-start | bytes 6291460
  189.8 23.7 %slice-start.1 = ((s8[16777216]{0:T(1024)(128)(4,1)}), s8[4194304]{0:T(1024)(128)(4,1)S(1)}, s32[]{:S(2)}) async-start(s8[16777216]{0:T(1024)(128)(4,1)} %bitcast.32), calls=%async_computation.2 | async-start | bytes 8388608
  198.7 14.8 %slice-start.2 = ((s8[16777216]{0:T(1024)(128)(4,1)}), s8[4194304]{0:T(1024)(128)(4,1)S(1)}, s32[]{:S(2)}) async-start(s8[16777216]{0:T(1024)(128)(4,1)} %bitcast.32), calls=%async_computation.3 | async-start | bytes 8388608
  198.7 14.7 %collective-permute-start.5 = (bf16[192,2048]{1,0:T(8,128)(2,1)S(1)}, bf16[192,2048]{1,0:T(8,128)(2,1)S(1)}, u32[]{:S(2)}, u32[]{:S(2)}) collective-permute-start(bf16[192,2048]{1,0:T(8,128)(2,1)S(1)} %maximum_select_fusion.5), channel_id=1, source_target_pairs={{0,1},{1,0},{2,3},{3,2},{4,5},{5,4},{6,7},{7,6},{8,9},{9,8},{10,11... | collective-permute-start | bytes 2359304 | tf_op jit(solution)/shard_map/ppermute | solution.py:33
  206.2 7.2 %slice-start.3 = ((s8[16777216]{0:T(1024)(128)(4,1)}), s8[4194304]{0:T(1024)(128)(4,1)S(1)}, s32[]{:S(2)}) async-start(s8[16777216]{0:T(1024)(128)(4,1)} %bitcast.32), calls=%async_computation.4 | async-start | bytes 8388608
  213.3 3.6 %collective-permute-start.3 = (bf16[192,2048]{1,0:T(8,128)(2,1)S(1)}, bf16[192,2048]{1,0:T(8,128)(2,1)S(1)}, u32[]{:S(2)}, u32[]{:S(2)}) collective-permute-start(bf16[192,2048]{1,0:T(8,128)(2,1)S(1)} %maximum_select_fusion.4), channel_id=1, source_target_pairs={{0,1},{1,0},{2,3},{3,2},{4,5},{5,4},{6,7},{7,6},{8,9},{9,8},{10,11... | collective-permute-start | bytes 2359304 | tf_op jit(solution)/shard_map/ppermute | solution.py:33
Sparse Core Ops, SparseCore 0:
  29.4 140.7 all-reduce.2

commit v7 on v6

--- a/solution.py
+++ b/solution.py
@@ -23,10 +23,11 @@
     return jnp.einsum("rd,md->rm", unit_rows, landmark, preferred_element_type=jnp.float32)
 
 
-def select_rows(rows, picks):
-    onehot = (picks[:, None] == lax.broadcasted_iota(jnp.int32, (picks.shape[0], rows.shape[0]), 1))
-    chosen = jnp.dot(onehot.astype(rows.dtype), rows, preferred_element_type=jnp.float32)
-    return chosen.astype(rows.dtype)
+def reorder_columns(kernel, picks):
+    natural = lax.broadcasted_iota(jnp.int32, (kernel.shape[1], picks.shape[0]), 0)
+    onehot = (picks[None, :] == natural).astype(kernel.dtype)
+    ordered = jnp.dot(kernel, onehot, preferred_element_type=jnp.float32)
+    return ordered.astype(kernel.dtype)
 
 
 def swap_cores(value):
@@ -46,8 +47,7 @@
     weights = jnp.concatenate([mixture, swap_cores(mixture)])
     pieces = []
     for number in range(block_count):
-        picks = lax.dynamic_slice_in_dim(landmark_picks[number], core * half, half)
-        chosen = normalize(select_rows(candidates, picks))
+        chosen = normalize(lax.dynamic_slice_in_dim(candidates, core * half, half, axis=0))
         chosen = jnp.where(here == block_owner[number], chosen, jnp.zeros_like(chosen))
         pieces.append(chosen)
     arrived = lax.psum(pieces, SPREAD)
@@ -65,6 +65,7 @@
             jnp.concatenate(parts, axis=1),
             jnp.concatenate(parts[::-1], axis=1),
         )
+        own_kernel = reorder_columns(own_kernel, landmark_picks[number])
         other_kernel = swap_cores(own_kernel)
         kernel = jnp.where(
             core == 0,

time: 229 us -> 222 us (0.969)
  matrix products: 54.6 us -> 47.6 us
    dot_general x2, matrix products: 16 us -> 7.77 us  [reorder_columns(): ordered = jnp.dot(kernel, onehot, preferred_element_type=jnp.float32)]
  transfers between devices with their start and end apart: 7 -> 7, of which waited for: 1 -> 1; matrix products, arithmetic and copies ran while one was open for 17% -> 21% of each run, Pallas kernels for 0% -> 0%
where the time goes in v7:
time: 222 us
  waiting for transfers between devices  139 us (63%)
  matrix products  47.6 us (21%)
  between operations  19.9 us (9%)
  other arithmetic  6.94 us (3%)
  starting transfers between devices  4.55 us (2%)
  local copies, waits for them, and re-layouts  3.97 us (2%)
    psum x1, waiting for transfers between devices, per_device(): arrived = lax.psum(pieces, SPREAD)  139 us
    dot_general x4, matrix products, inner_products(): jnp.einsum('rd,md->rm', unit_rows, landmark, preferred_element_type=jnp.f...  31.8 us
    dot_general x2, matrix products, per_device(): jnp.dot(kernel, rows, preferred_element_type=jnp.float32)  8.01 us
    dot_general x2, matrix products, reorder_columns(): ordered = jnp.dot(kernel, onehot, preferred_element_type=jnp.float32)  7.77 us
    ppermute x6, starting transfers between devices, swap_cores(): return lax.ppermute(value, 'bw', [(0, 1), (1, 0)])  4.55 us
  transfers between devices with their start and end apart: 7, of which 1 were waited for; matrix products, arithmetic and copies ran while one was open for 21% of the time, Pallas kernels for 0%

profile of v7, /device:TPU:1, one launch (start us, length us, event | category | flops | bytes accessed | tf_op | source)
XLA Modules:
  0.0 221.8 jit_solution(5466893475821726423)
XLA Ops:
  6.5 2.1 fusion.8
  8.6 0.6 fusion.48
  10.6 4.3 %broadcast_select_fusion.1 = (bf16[1024,1024]{1,0:T(8,128)(2,1)}, bf16[1024,1024]{1,0:T(8,128)(2,1)}) fusion(pred[]{:T(512)S(6)} %eq.33, f32[1024]{0:T(1024)S(1)} %add_rsqrt_fusion, bf16[2048,1024]{1,0:T(8,128)(2,1)} %param.8, s32[]{:T(128)S(6)} %select_n.49, pred[]{:T(512)S(6)} %eq.37), kind=kLoop, calls=%fused_computation.18 | loop fusion | flops 5242880 | bytes 6295558 | tf_op jit(solution)/shard_map/jit(_where)/select_n | solution.py:51
  14.9 0.0 all-reduce.3.cloned.1.call-update
  15.0 0.6 copy-done.2
  15.6 1.4 collective-permute-start.1
  17.0 0.0 collective-permute-start
  17.0 0.2 multiply_reduce_fusion
  17.2 138.7 %all-reduce.3.cloned.1.call-done = (bf16[1024,1024]{1,0:T(8,128)(2,1)}, bf16[1024,1024]{1,0:T(8,128)(2,1)}) async-done(((bf16[1024,1024]{1,0:T(8,128)(2,1)}, bf16[1024,1024]{1,0:T(8,128)(2,1)}), (bf16[1024,1024]{1,0:T(8,128)(2,1)}, bf16[1024,1024]{1,0:T(8,128)(2,1)})) %all-reduce.3.cloned.1.call-update) | async-done | bytes 4194320 | tf_op jit(solution)/shard_map/psum | solution.py:53
  155.9 2.2 %collective-permute-start.4 = (bf16[1024,1024]{1,0:T(8,128)(2,1)}, bf16[1024,1024]{1,0:T(8,128)(2,1)}, u32[]{:S(2)}, u32[]{:S(2)}) collective-permute-start(bf16[1024,1024]{1,0:T(8,128)(2,1)} %get-tuple-element.5), channel_id=1, source_target_pairs={{0,1},{1,0},{2,3},{3,2},{4,5},{5,4},{6,7},{7,6},{8,9},{9,8},{10,11... | collective-permute-start | bytes 6291464 | tf_op jit(solution)/shard_map/ppermute | solution.py:34
  158.2 0.7 fusion.45
  158.9 0.1 collective-permute-start.2
  159.0 0.7 fusion.44
  159.6 0.2 convert_element_type.37
  162.3 0.1 dynamic-slice
  162.4 0.1 fusion.26
  162.6 0.6 fusion.47
  165.7 0.6 fusion.46
  166.3 8.4 %add_convert_fusion.4 = bf16[192,1024]{1,0:T(8,128)(2,1)S(1)} fusion(f32[]{:T(128)} %bitcast.16, f32[]{:T(128)} %bitcast.15, f32[]{:T(128)} %bitcast.14, f32[]{:T(128)} %bitcast.13, f32[]{:T(128)} %bitcast.12, f32[]{:T(128)} %bitcast.11, f32[]{:T(128)} %bitcast.10, f32[]{:T(128)} %bitcast.9, f32[]{:T(128)} %bitcast.8, f32[]{:T(128)} %bitcast.7, ...), kind=kOutput, calls=%fused_computation.51 | convolution fusion | flops 407371776 | bytes 2883648 | tf_op jit(solution)/shard_map/rd,md->rm/dot_general | solution.py:23
  174.7 6.6 %add_convert_fusion.2 = bf16[192,1024]{1,0:T(8,128)(2,1)S(1)} fusion(f32[]{:T(128)} %bitcast.16, f32[]{:T(128)} %bitcast.15, f32[]{:T(128)} %bitcast.14, f32[]{:T(128)} %bitcast.13, f32[]{:T(128)} %bitcast.12, f32[]{:T(128)} %bitcast.11, f32[]{:T(128)} %bitcast.10, f32[]{:T(128)} %bitcast.9, f32[]{:T(128)} %bitcast.8, f32[]{:T(128)} %bitcast.7, ...), kind=kOutput, calls=%fused_computation.49 | convolution fusion | flops 407371776 | bytes 2883648 | tf_op jit(solution)/shard_map/rd,md->rm/dot_general | solution.py:23
  181.3 8.2 %add_convert_fusion.1 = bf16[192,1024]{1,0:T(8,128)(2,1)S(1)} fusion(f32[]{:T(128)} %bitcast.16, f32[]{:T(128)} %bitcast.15, f32[]{:T(128)} %bitcast.14, f32[]{:T(128)} %bitcast.13, f32[]{:T(128)} %bitcast.12, f32[]{:T(128)} %bitcast.11, f32[]{:T(128)} %bitcast.10, f32[]{:T(128)} %bitcast.9, f32[]{:T(128)} %bitcast.8, f32[]{:T(128)} %bitcast.7, ...), kind=kOutput, calls=%fused_computation.48 | convolution fusion | flops 407371776 | bytes 2883648 | tf_op jit(solution)/shard_map/rd,md->rm/dot_general | solution.py:23
  189.5 0.0 slice-start
  189.5 0.0 slice-start.1
  189.5 3.9 %fusion.12 = bf16[192,2048]{1,0:T(8,128)(2,1)S(1)} fusion(s32[2048]{0:T(1024)S(1)} %bitcast.29, bf16[192,1024]{1,0:T(8,128)(2,1)S(1)} %add_convert_fusion.1, bf16[192,1024]{1,0:T(8,128)(2,1)S(1)} %add_convert_fusion.2, pred[]{:T(512)S(6)} %eq.32), kind=kOutput, calls=%fused_computation.15 | convolution fusion | flops 1618739200 | bytes 1581057 | tf_op jit(solution)/shard_map/dot_general | solution.py:29
  193.4 0.0 slice-start.2
  193.5 0.8 collective-permute-start.5
  194.2 8.6 %add_convert_fusion.3 = bf16[192,1024]{1,0:T(8,128)(2,1)S(1)} fusion(f32[]{:T(128)} %bitcast.16, f32[]{:T(128)} %bitcast.15, f32[]{:T(128)} %bitcast.14, f32[]{:T(128)} %bitcast.13, f32[]{:T(128)} %bitcast.12, f32[]{:T(128)} %bitcast.11, f32[]{:T(128)} %bitcast.10, f32[]{:T(128)} %bitcast.9, f32[]{:T(128)} %bitcast.8, f32[]{:T(128)} %bitcast.7, ...), kind=kOutput, calls=%fused_computation.50 | convolution fusion | flops 407371776 | bytes 2883648 | tf_op jit(solution)/shard_map/rd,md->rm/dot_general | solution.py:23
  202.8 0.0 slice-start.3
  202.8 3.9 %fusion.13 = bf16[192,2048]{1,0:T(8,128)(2,1)S(1)} fusion(s32[2048]{0:T(1024)S(1)} %bitcast.28, bf16[192,1024]{1,0:T(8,128)(2,1)S(1)} %add_convert_fusion.3, bf16[192,1024]{1,0:T(8,128)(2,1)S(1)} %add_convert_fusion.4, pred[]{:T(512)S(6)} %eq.32), kind=kOutput, calls=%fused_computation.16 | convolution fusion | flops 1618739200 | bytes 1581057 | tf_op jit(solution)/shard_map/dot_general | solution.py:29
  206.7 0.1 collective-permute-start.3
  206.9 3.4 %fusion.2 = f32[384,2048]{1,0:T(8,128)S(1)} fusion(bf16[4096,2048]{1,0:T(8,128)(2,1)S(1)} %bitcast.31, bf16[192,2048]{1,0:T(8,128)(2,1)S(1)} %collective-permute-done.5, bf16[192,2048]{1,0:T(8,128)(2,1)S(1)} %fusion.12, pred[]{:T(512)S(6)} %eq.32), kind=kOutput, calls=%fused_computation.4 | convolution fusion | flops 3228303360 | bytes 13107201 | tf_op jit(solution)/shard_map/dot_general | solution.py:76
  210.3 4.6 %add_convert_fusion = bf16[384,2048]{1,0:T(8,128)(2,1)} fusion(f32[384,2048]{1,0:T(8,128)S(1)} %fusion.2, bf16[4096,2048]{1,0:T(8,128)(2,1)S(1)} %bitcast.31, bf16[192,2048]{1,0:T(8,128)(2,1)S(1)} %collective-permute-done.3, bf16[192,2048]{1,0:T(8,128)(2,1)S(1)} %fusion.13, pred[]{:T(512)S(6)} %eq.32), kind=kOutput, calls=%fused_computation.14 | convolution fusion | flops 3229876224 | bytes 14680065 | tf_op jit(solution)/shard_map/dot_general | solution.py:76
  (26 shorter events, 0.1 us)
Async XLA Ops:
  6.5 2.1 copy-start.4
  6.5 149.4 %all-reduce.3.cloned.1.call-start = ((), (), s32[]{:S(2)}) async-start(), calls=%async_computation | async-start | bytes 8388608 | tf_op jit(solution)/shard_map/psum | solution.py:53
  14.9 0.7 copy-start.2
  14.9 2.0 copy-start.3
  14.9 2.1 copy-start
  14.9 143.9 %copy-start.1 = (s32[2,2048]{1,0:T(2,128)S(1)}, s32[2,2048]{1,0:T(2,128)}, u32[]{:S(2)}) copy-start(s32[2,2048]{1,0:T(2,128)} %param.10) | copy-start | bytes 49156
  15.6 147.0 %collective-permute-start.1 = (f32[4]{0:T(128)S(1)}, f32[4]{0:T(128)S(1)}, u32[]{:S(2)}, u32[]{:S(2)}) collective-permute-start(f32[4]{0:T(128)S(1)} %copy-done.2), channel_id=1, source_target_pairs={{0,1},{1,0},{2,3},{3,2},{4,5},{5,4},{6,7},{7,6},{8,9},{9,8},{10,11... | collective-permute-start | bytes 56 | tf_op jit(solution)/shard_map/ppermute | solution.py:34
  17.0 148.7 %collective-permute-start = (f32[4]{0:T(128)S(1)}, f32[4]{0:T(128)S(1)}, u32[]{:S(2)}, u32[]{:S(2)}) collective-permute-start(f32[4]{0:T(128)S(1)} %copy-done.3), channel_id=1, source_target_pairs={{0,1},{1,0},{2,3},{3,2},{4,5},{5,4},{6,7},{7,6},{8,9},{9,8},{10,11... | collective-permute-start | bytes 56 | tf_op jit(solution)/shard_map/ppermute | solution.py:34
  155.9 25.3 %collective-permute-start.4 = (bf16[1024,1024]{1,0:T(8,128)(2,1)}, bf16[1024,1024]{1,0:T(8,128)(2,1)}, u32[]{:S(2)}, u32[]{:S(2)}) collective-permute-start(bf16[1024,1024]{1,0:T(8,128)(2,1)} %get-tuple-element.5), channel_id=1, source_target_pairs={{0,1},{1,0},{2,3},{3,2},{4,5},{5,4},{6,7},{7,6},{8,9},{9,8},{10,11... | collective-permute-start | bytes 6291464 | tf_op jit(solution)/shard_map/ppermute | solution.py:34
  158.9 35.3 %collective-permute-start.2 = (bf16[1024,1024]{1,0:T(8,128)(2,1)}, bf16[1024,1024]{1,0:T(8,128)(2,1)}, u32[]{:S(2)}, u32[]{:S(2)}) collective-permute-start(bf16[1024,1024]{1,0:T(8,128)(2,1)} %get-tuple-element.6), channel_id=1, source_target_pairs={{0,1},{1,0},{2,3},{3,2},{4,5},{5,4},{6,7},{7,6},{8,9},{9,8},{10,11... | collective-permute-start | bytes 6291464 | tf_op jit(solution)/shard_map/ppermute | solution.py:34
  166.3 8.4 %copy-start.5 = (bf16[1024,1024]{1,0:T(8,128)(2,1)S(1)}, bf16[1024,1024]{1,0:T(8,128)(2,1)}, u32[]{:S(2)}) copy-start(bf16[1024,1024]{1,0:T(8,128)(2,1)} %get-tuple-element.5) | copy-start | bytes 6291460
  189.5 17.3 %slice-start = ((s8[16777216]{0:T(1024)(128)(4,1)}), s8[4194304]{0:T(1024)(128)(4,1)S(1)}, s32[]{:S(2)}) async-start(s8[16777216]{0:T(1024)(128)(4,1)} %bitcast.30), calls=%async_computation.1 | async-start | bytes 8388608
  189.5 17.3 %slice-start.1 = ((s8[16777216]{0:T(1024)(128)(4,1)}), s8[4194304]{0:T(1024)(128)(4,1)S(1)}, s32[]{:S(2)}) async-start(s8[16777216]{0:T(1024)(128)(4,1)} %bitcast.30), calls=%async_computation.2 | async-start | bytes 8388608
  193.4 13.4 %slice-start.2 = ((s8[16777216]{0:T(1024)(128)(4,1)}), s8[4194304]{0:T(1024)(128)(4,1)S(1)}, s32[]{:S(2)}) async-start(s8[16777216]{0:T(1024)(128)(4,1)} %bitcast.30), calls=%async_computation.3 | async-start | bytes 8388608
  193.5 13.4 %collective-permute-start.5 = (bf16[192,2048]{1,0:T(8,128)(2,1)S(1)}, bf16[192,2048]{1,0:T(8,128)(2,1)S(1)}, u32[]{:S(2)}, u32[]{:S(2)}) collective-permute-start(bf16[192,2048]{1,0:T(8,128)(2,1)S(1)} %fusion.12), channel_id=1, source_target_pairs={{0,1},{1,0},{2,3},{3,2},{4,5},{5,4},{6,7},{7,6},{8,9},{9,8},{10,11... | collective-permute-start | bytes 2359304 | tf_op jit(solution)/shard_map/ppermute | solution.py:34
  202.8 4.0 %slice-start.3 = ((s8[16777216]{0:T(1024)(128)(4,1)}), s8[4194304]{0:T(1024)(128)(4,1)S(1)}, s32[]{:S(2)}) async-start(s8[16777216]{0:T(1024)(128)(4,1)} %bitcast.30), calls=%async_computation.4 | async-start | bytes 8388608
  206.7 3.6 %collective-permute-start.3 = (bf16[192,2048]{1,0:T(8,128)(2,1)S(1)}, bf16[192,2048]{1,0:T(8,128)(2,1)S(1)}, u32[]{:S(2)}, u32[]{:S(2)}) collective-permute-start(bf16[192,2048]{1,0:T(8,128)(2,1)S(1)} %fusion.13), channel_id=1, source_target_pairs={{0,1},{1,0},{2,3},{3,2},{4,5},{5,4},{6,7},{7,6},{8,9},{9,8},{10,11... | collective-permute-start | bytes 2359304 | tf_op jit(solution)/shard_map/ppermute | solution.py:34
Sparse Core Ops, SparseCore 0:
  15.1 140.8 all-reduce.2

commit v8 on v7

--- a/solution.py
+++ b/solution.py
@@ -50,6 +50,7 @@
         chosen = normalize(lax.dynamic_slice_in_dim(candidates, core * half, half, axis=0))
         chosen = jnp.where(here == block_owner[number], chosen, jnp.zeros_like(chosen))
         pieces.append(chosen)
+    pieces, widths, weights = lax.optimization_barrier((pieces, widths, weights))
     arrived = lax.psum(pieces, SPREAD)
     share = unit_rows.shape[0] // cores
     own_rows = lax.dynamic_slice_in_dim(unit_rows, core * share, share, axis=0)

time: 222 us -> 219 us (0.986)
  local copies, waits for them, and re-layouts: 3.97 us -> 1.45 us
  matrix products: 47.6 us -> 45.3 us
    dot_general x4, matrix products: 31.8 us -> 29.5 us  [inner_products(): jnp.einsum('rd,md->rm', unit_rows, landmark, preferred_element_type=jnp.f...]
  transfers between devices with their start and end apart: 7 -> 7, of which waited for: 1 -> 1; matrix products, arithmetic and copies ran while one was open for 21% -> 22% of each run, Pallas kernels for 0% -> 0%
where the time goes in v8:
time: 219 us; the launch traced here: 218 us
  waiting for transfers between devices  140 us (64%)
  matrix products  45.3 us (21%)
  between operations  19.8 us (9%)
  other arithmetic  7.08 us (3%)
  starting transfers between devices  4.58 us (2%)
    psum x1, waiting for transfers between devices, per_device(): arrived = lax.psum(pieces, SPREAD)  140 us
    dot_general x4, matrix products, inner_products(): jnp.einsum('rd,md->rm', unit_rows, landmark, preferred_element_type=jnp.f...  29.5 us
    dot_general x2, matrix products, per_device(): jnp.dot(kernel, rows, preferred_element_type=jnp.float32)  8.01 us
    dot_general x2, matrix products, reorder_columns(): ordered = jnp.dot(kernel, onehot, preferred_element_type=jnp.float32)  7.78 us
    ppermute x6, starting transfers between devices, swap_cores(): return lax.ppermute(value, 'bw', [(0, 1), (1, 0)])  4.58 us
  transfers between devices with their start and end apart: 7, of which 1 were waited for; matrix products, arithmetic and copies ran while one was open for 22% of the time, Pallas kernels for 0%

profile of v8, /device:TPU:1, one launch (start us, length us, event | category | flops | bytes accessed | tf_op | source)
XLA Modules:
  0.0 218.4 jit_solution(768811317819681349)
XLA Ops:
  6.5 1.4 collective-permute-start
  7.9 0.0 collective-permute-start.1
  7.9 2.1 fusion.8
  10.0 0.6 fusion.46
  11.9 0.0 copy-start.5
  11.9 0.0 copy-start.6
  11.9 4.3 %broadcast_select_fusion = (bf16[1024,1024]{1,0:T(8,128)(2,1)}, bf16[1024,1024]{1,0:T(8,128)(2,1)}) fusion(pred[]{:T(512)S(6)} %eq.34, f32[1024]{0:T(1024)S(1)} %add_rsqrt_fusion, bf16[2048,1024]{1,0:T(8,128)(2,1)} %param.8, s32[]{:T(128)S(6)} %select_n.48, pred[]{:T(512)S(6)} %eq.33), kind=kLoop, calls=%fused_computation.17 | loop fusion | flops 5242880 | bytes 6295558 | tf_op jit(solution)/shard_map/jit(_where)/select_n | solution.py:51
  16.3 0.1 pad_maximum_fusion
  16.3 0.1 pad_maximum_fusion.1
  16.4 0.0 all-reduce.3.cloned.1.call-update
  16.4 140.1 %all-reduce.3.cloned.1.call-done = (bf16[1024,1024]{1,0:T(8,128)(2,1)}, bf16[1024,1024]{1,0:T(8,128)(2,1)}) async-done(((bf16[1024,1024]{1,0:T(8,128)(2,1)}, bf16[1024,1024]{1,0:T(8,128)(2,1)}), (bf16[1024,1024]{1,0:T(8,128)(2,1)}, bf16[1024,1024]{1,0:T(8,128)(2,1)})) %all-reduce.3.cloned.1.call-update) | async-done | bytes 4194320 | tf_op jit(solution)/shard_map/psum | solution.py:54
  156.6 2.2 %collective-permute-start.4 = (bf16[1024,1024]{1,0:T(8,128)(2,1)}, bf16[1024,1024]{1,0:T(8,128)(2,1)}, u32[]{:S(2)}, u32[]{:S(2)}) collective-permute-start(bf16[1024,1024]{1,0:T(8,128)(2,1)} %get-tuple-element.13), channel_id=1, source_target_pairs={{0,1},{1,0},{2,3},{3,2},{4,5},{5,4},{6,7},{7,6},{8,9},{9,8},{10,11... | collective-permute-start | bytes 6291464 | tf_op jit(solution)/shard_map/ppermute | solution.py:34
  158.8 0.2 convert_element_type.39
  159.0 0.2 multiply_reduce_fusion
  159.2 0.1 dynamic-slice
  159.3 0.1 fusion.26
  159.4 0.1 collective-permute-start.2
  159.5 0.7 fusion.44
  165.2 7.0 %add_convert_fusion.4 = bf16[192,1024]{1,0:T(8,128)(2,1)S(1)} fusion(f32[]{:T(128)} %bitcast.17, f32[]{:T(128)} %bitcast.16, f32[]{:T(128)} %bitcast.15, f32[]{:T(128)} %bitcast.14, f32[]{:T(128)} %bitcast.13, f32[]{:T(128)} %bitcast.12, f32[]{:T(128)} %bitcast.11, f32[]{:T(128)} %bitcast.10, f32[]{:T(128)} %bitcast.9, f32[]{:T(128)} %bitcast.8, ...), kind=kOutput, calls=%fused_computation.51 | convolution fusion | flops 407371776 | bytes 2883648 | tf_op jit(solution)/shard_map/rd,md->rm/dot_general | solution.py:23
  172.2 6.8 %add_convert_fusion.2 = bf16[192,1024]{1,0:T(8,128)(2,1)S(1)} fusion(f32[]{:T(128)} %bitcast.17, f32[]{:T(128)} %bitcast.16, f32[]{:T(128)} %bitcast.15, f32[]{:T(128)} %bitcast.14, f32[]{:T(128)} %bitcast.13, f32[]{:T(128)} %bitcast.12, f32[]{:T(128)} %bitcast.11, f32[]{:T(128)} %bitcast.10, f32[]{:T(128)} %bitcast.9, f32[]{:T(128)} %bitcast.8, ...), kind=kOutput, calls=%fused_computation.49 | convolution fusion | flops 407371776 | bytes 2883648 | tf_op jit(solution)/shard_map/rd,md->rm/dot_general | solution.py:23
  179.1 8.5 %add_convert_fusion.1 = bf16[192,1024]{1,0:T(8,128)(2,1)S(1)} fusion(f32[]{:T(128)} %bitcast.17, f32[]{:T(128)} %bitcast.16, f32[]{:T(128)} %bitcast.15, f32[]{:T(128)} %bitcast.14, f32[]{:T(128)} %bitcast.13, f32[]{:T(128)} %bitcast.12, f32[]{:T(128)} %bitcast.11, f32[]{:T(128)} %bitcast.10, f32[]{:T(128)} %bitcast.9, f32[]{:T(128)} %bitcast.8, ...), kind=kOutput, calls=%fused_computation.48 | convolution fusion | flops 407371776 | bytes 2883648 | tf_op jit(solution)/shard_map/rd,md->rm/dot_general | solution.py:23
  187.5 0.0 slice-start
  187.5 0.0 slice-start.1
  187.5 3.9 %fusion.12 = bf16[192,2048]{1,0:T(8,128)(2,1)S(1)} fusion(s32[2048]{0:T(1024)S(1)} %bitcast.29, bf16[192,1024]{1,0:T(8,128)(2,1)S(1)} %add_convert_fusion.1, bf16[192,1024]{1,0:T(8,128)(2,1)S(1)} %add_convert_fusion.2, pred[]{:T(512)S(6)} %eq.32), kind=kOutput, calls=%fused_computation.15 | convolution fusion | flops 1618739200 | bytes 1581057 | tf_op jit(solution)/shard_map/dot_general | solution.py:29
  191.4 0.0 slice-start.2
  191.4 0.7 collective-permute-start.5
  192.2 7.2 %add_convert_fusion.3 = bf16[192,1024]{1,0:T(8,128)(2,1)S(1)} fusion(f32[]{:T(128)} %bitcast.17, f32[]{:T(128)} %bitcast.16, f32[]{:T(128)} %bitcast.15, f32[]{:T(128)} %bitcast.14, f32[]{:T(128)} %bitcast.13, f32[]{:T(128)} %bitcast.12, f32[]{:T(128)} %bitcast.11, f32[]{:T(128)} %bitcast.10, f32[]{:T(128)} %bitcast.9, f32[]{:T(128)} %bitcast.8, ...), kind=kOutput, calls=%fused_computation.50 | convolution fusion | flops 407371776 | bytes 2883648 | tf_op jit(solution)/shard_map/rd,md->rm/dot_general | solution.py:23
  199.4 0.0 slice-start.3
  199.4 3.9 %fusion.13 = bf16[192,2048]{1,0:T(8,128)(2,1)S(1)} fusion(s32[2048]{0:T(1024)S(1)} %bitcast.28, bf16[192,1024]{1,0:T(8,128)(2,1)S(1)} %add_convert_fusion.3, bf16[192,1024]{1,0:T(8,128)(2,1)S(1)} %add_convert_fusion.4, pred[]{:T(512)S(6)} %eq.32), kind=kOutput, calls=%fused_computation.16 | convolution fusion | flops 1618739200 | bytes 1581057 | tf_op jit(solution)/shard_map/dot_general | solution.py:29
  203.3 0.1 collective-permute-start.3
  203.5 3.4 %fusion.2 = f32[384,2048]{1,0:T(8,128)S(1)} fusion(bf16[4096,2048]{1,0:T(8,128)(2,1)S(1)} %bitcast.31, bf16[192,2048]{1,0:T(8,128)(2,1)S(1)} %collective-permute-done.5, bf16[192,2048]{1,0:T(8,128)(2,1)S(1)} %fusion.12, pred[]{:T(512)S(6)} %eq.32), kind=kOutput, calls=%fused_computation.4 | convolution fusion | flops 3228303360 | bytes 13107201 | tf_op jit(solution)/shard_map/dot_general | solution.py:77
  207.0 4.6 %add_convert_fusion = bf16[384,2048]{1,0:T(8,128)(2,1)} fusion(f32[384,2048]{1,0:T(8,128)S(1)} %fusion.2, bf16[4096,2048]{1,0:T(8,128)(2,1)S(1)} %bitcast.31, bf16[192,2048]{1,0:T(8,128)(2,1)S(1)} %collective-permute-done.3, bf16[192,2048]{1,0:T(8,128)(2,1)S(1)} %fusion.13, pred[]{:T(512)S(6)} %eq.32), kind=kOutput, calls=%fused_computation.14 | convolution fusion | flops 3229876224 | bytes 14680065 | tf_op jit(solution)/shard_map/dot_general | solution.py:77
  (27 shorter events, 0.1 us)
Async XLA Ops:
  6.5 3.5 %copy-start.2 = (s32[2]{0:T(128)S(1)}, s32[2]{0:T(128)}, u32[]{:S(2)}) copy-start(s32[2]{0:T(128)} %param.9) | copy-start | bytes 28
  6.5 150.0 %all-reduce.3.cloned.1.call-start = ((), (), s32[]{:S(2)}) async-start(), calls=%async_computation | async-start | bytes 8388608 | tf_op jit(solution)/shard_map/psum | solution.py:54
  6.5 9.7 %collective-permute-start = (f32[4]{0:T(128)}, f32[4]{0:T(128)S(1)}, u32[]{:S(2)}, u32[]{:S(2)}) collective-permute-start(f32[4]{0:T(128)} %param.11), channel_id=1, source_target_pairs={{0,1},{1,0},{2,3},{3,2},{4,5},{5,4},{6,7},{7,6},{8,9},{9,8},{10,11... | collective-permute-start | bytes 56 | tf_op jit(solution)/shard_map/ppermute | solution.py:34
  7.9 8.4 %collective-permute-start.1 = (f32[4]{0:T(128)}, f32[4]{0:T(128)S(1)}, u32[]{:S(2)}, u32[]{:S(2)}) collective-permute-start(f32[4]{0:T(128)} %param.12), channel_id=1, source_target_pairs={{0,1},{1,0},{2,3},{3,2},{4,5},{5,4},{6,7},{7,6},{8,9},{9,8},{10,11... | collective-permute-start | bytes 56 | tf_op jit(solution)/shard_map/ppermute | solution.py:34
  11.9 4.4 %copy-start.5 = (f32[4]{0:T(128)S(1)}, f32[4]{0:T(128)}, u32[]{:S(2)}) copy-start(f32[4]{0:T(128)} %param.11) | copy-start | bytes 52
  11.9 4.4 %copy-start.6 = (f32[4]{0:T(128)S(1)}, f32[4]{0:T(128)}, u32[]{:S(2)}) copy-start(f32[4]{0:T(128)} %param.12) | copy-start | bytes 52
  16.4 142.4 %copy-start = (bf16[384,1024]{1,0:T(8,128)(2,1)S(1)}, bf16[384,1024]{1,0:T(8,128)(2,1)}, u32[]{:S(2)}) copy-start(bf16[384,1024]{1,0:T(8,128)(2,1)} %param.7) | copy-start | bytes 2359300
  156.6 22.5 %collective-permute-start.4 = (bf16[1024,1024]{1,0:T(8,128)(2,1)}, bf16[1024,1024]{1,0:T(8,128)(2,1)}, u32[]{:S(2)}, u32[]{:S(2)}) collective-permute-start(bf16[1024,1024]{1,0:T(8,128)(2,1)} %get-tuple-element.13), channel_id=1, source_target_pairs={{0,1},{1,0},{2,3},{3,2},{4,5},{5,4},{6,7},{7,6},{8,9},{9,8},{10,11... | collective-permute-start | bytes 6291464 | tf_op jit(solution)/shard_map/ppermute | solution.py:34
  158.8 0.7 copy-start.1
  159.0 6.2 %copy-start.3 = (bf16[1024,1024]{1,0:T(8,128)(2,1)S(1)}, bf16[1024,1024]{1,0:T(8,128)(2,1)}, u32[]{:S(2)}) copy-start(bf16[1024,1024]{1,0:T(8,128)(2,1)} %get-tuple-element.14) | copy-start | bytes 6291460
  159.4 32.8 %collective-permute-start.2 = (bf16[1024,1024]{1,0:T(8,128)(2,1)}, bf16[1024,1024]{1,0:T(8,128)(2,1)S(1)}, u32[]{:S(2)}, u32[]{:S(2)}) collective-permute-start(bf16[1024,1024]{1,0:T(8,128)(2,1)} %get-tuple-element.14), channel_id=1, source_target_pairs={{0,1},{1,0},{2,3},{3,2},{4,5},{5,4},{6,7},{7,6},{8,9},{9,8},{10,11... | collective-permute-start | bytes 6291464 | tf_op jit(solution)/shard_map/ppermute | solution.py:34
  165.2 7.0 %copy-start.4 = (bf16[1024,1024]{1,0:T(8,128)(2,1)S(1)}, bf16[1024,1024]{1,0:T(8,128)(2,1)}, u32[]{:S(2)}) copy-start(bf16[1024,1024]{1,0:T(8,128)(2,1)} %get-tuple-element.13) | copy-start | bytes 6291460
  187.5 15.9 %slice-start = ((s8[16777216]{0:T(1024)(128)(4,1)}), s8[4194304]{0:T(1024)(128)(4,1)S(1)}, s32[]{:S(2)}) async-start(s8[16777216]{0:T(1024)(128)(4,1)} %bitcast.30), calls=%async_computation.1 | async-start | bytes 8388608
  187.5 15.9 %slice-start.1 = ((s8[16777216]{0:T(1024)(128)(4,1)}), s8[4194304]{0:T(1024)(128)(4,1)S(1)}, s32[]{:S(2)}) async-start(s8[16777216]{0:T(1024)(128)(4,1)} %bitcast.30), calls=%async_computation.2 | async-start | bytes 8388608
  191.4 12.0 %slice-start.2 = ((s8[16777216]{0:T(1024)(128)(4,1)}), s8[4194304]{0:T(1024)(128)(4,1)S(1)}, s32[]{:S(2)}) async-start(s8[16777216]{0:T(1024)(128)(4,1)} %bitcast.30), calls=%async_computation.3 | async-start | bytes 8388608
  191.4 12.0 %collective-permute-start.5 = (bf16[192,2048]{1,0:T(8,128)(2,1)S(1)}, bf16[192,2048]{1,0:T(8,128)(2,1)S(1)}, u32[]{:S(2)}, u32[]{:S(2)}) collective-permute-start(bf16[192,2048]{1,0:T(8,128)(2,1)S(1)} %fusion.12), channel_id=1, source_target_pairs={{0,1},{1,0},{2,3},{3,2},{4,5},{5,4},{6,7},{7,6},{8,9},{9,8},{10,11... | collective-permute-start | bytes 2359304 | tf_op jit(solution)/shard_map/ppermute | solution.py:34
  199.4 4.1 %slice-start.3 = ((s8[16777216]{0:T(1024)(128)(4,1)}), s8[4194304]{0:T(1024)(128)(4,1)S(1)}, s32[]{:S(2)}) async-start(s8[16777216]{0:T(1024)(128)(4,1)} %bitcast.30), calls=%async_computation.4 | async-start | bytes 8388608
  203.3 3.6 %collective-permute-start.3 = (bf16[192,2048]{1,0:T(8,128)(2,1)S(1)}, bf16[192,2048]{1,0:T(8,128)(2,1)S(1)}, u32[]{:S(2)}, u32[]{:S(2)}) collective-permute-start(bf16[192,2048]{1,0:T(8,128)(2,1)S(1)} %fusion.13), channel_id=1, source_target_pairs={{0,1},{1,0},{2,3},{3,2},{4,5},{5,4},{6,7},{7,6},{8,9},{9,8},{10,11... | collective-permute-start | bytes 2359304 | tf_op jit(solution)/shard_map/ppermute | solution.py:34
Sparse Core Ops, SparseCore 0:
  16.6 139.9 all-reduce.2

commit v9 on v8

--- a/solution.py
+++ b/solution.py
@@ -51,7 +51,8 @@
         chosen = jnp.where(here == block_owner[number], chosen, jnp.zeros_like(chosen))
         pieces.append(chosen)
     pieces, widths, weights = lax.optimization_barrier((pieces, widths, weights))
-    arrived = lax.psum(pieces, SPREAD)
+    orders = [SPREAD, SPREAD[::-1]]
+    arrived = [lax.psum(piece, orders[number % 2]) for number, piece in enumerate(pieces)]
     share = unit_rows.shape[0] // cores
     own_rows = lax.dynamic_slice_in_dim(unit_rows, core * share, share, axis=0)
     features = jnp.zeros((unit_rows.shape[0], whitening.shape[1]), jnp.float32)

time: 219 us -> 349 us (1.59)
  waiting for transfers between devices: 140 us -> 265 us
    psum x1 -> x2, waiting for transfers between devices: 140 us -> 264 us  [per_device(): lax.psum(piece, orders[number % 2])]
  transfers between devices with their start and end apart: 7 -> 8, of which waited for: 1 -> 2; matrix products, arithmetic and copies ran while one was open for 22% -> 15% of each run, Pallas kernels for 0% -> 0%
where the time goes in v9:
time: 349 us; the launch traced here: 348 us
  waiting for transfers between devices  265 us (76%)
  matrix products  46.8 us (13%)
  between operations  20 us (6%)
  starting transfers between devices  7.97 us (2%)
  other arithmetic  7.08 us (2%)
    psum x2, waiting for transfers between devices, per_device(): lax.psum(piece, orders[number % 2])  264 us
    dot_general x4, matrix products, inner_products(): jnp.einsum('rd,md->rm', unit_rows, landmark, preferred_element_type=jnp.f...  31 us
    dot_general x2, matrix products, per_device(): jnp.dot(kernel, rows, preferred_element_type=jnp.float32)  8.01 us
    ppermute x6, starting transfers between devices, swap_cores(): return lax.ppermute(value, 'bw', [(0, 1), (1, 0)])  7.92 us
    dot_general x2, matrix products, reorder_columns(): ordered = jnp.dot(kernel, onehot, preferred_element_type=jnp.float32)  7.78 us
  transfers between devices with their start and end apart: 8, of which 2 were waited for; matrix products, arithmetic and copies ran while one was open for 15% of the time, Pallas kernels for 0%

profile of v9, /device:TPU:1, one launch (start us, length us, event | category | flops | bytes accessed | tf_op | source)
XLA Modules:
  0.0 348.5 jit_solution(17720588510566206339)
XLA Ops:
  6.5 1.4 collective-permute-start
  7.9 2.1 fusion.8
  10.0 0.6 fusion.46
  12.0 0.0 copy-start.4
  12.0 4.3 %broadcast_select_fusion = (bf16[1024,1024]{1,0:T(8,128)(2,1)}, bf16[1024,1024]{1,0:T(8,128)(2,1)}) fusion(pred[]{:T(512)S(6)} %eq.34, f32[1024]{0:T(1024)S(1)} %add_rsqrt_fusion, bf16[2048,1024]{1,0:T(8,128)(2,1)} %param.8, s32[]{:T(128)S(6)} %select_n.48, pred[]{:T(512)S(6)} %eq.33), kind=kLoop, calls=%fused_computation.17 | loop fusion | flops 5242880 | bytes 6295558 | tf_op jit(solution)/shard_map/jit(_where)/select_n | solution.py:51
  16.3 0.1 pad_maximum_fusion
  16.4 0.1 pad_maximum_fusion.1
  16.5 0.0 all-reduce.5.cloned.1.call-update
  16.5 0.0 all-reduce.3.cloned.1.call-start
  16.6 0.7 all-reduce.3.cloned.1.call-update
  17.3 132.6 %all-reduce.5.cloned.1.call-done = bf16[1024,1024]{1,0:T(8,128)(2,1)} async-done(((bf16[1024,1024]{1,0:T(8,128)(2,1)}), bf16[1024,1024]{1,0:T(8,128)(2,1)}) %all-reduce.5.cloned.1.call-update) | async-done | bytes 2097168 | tf_op jit(solution)/shard_map/psum | solution.py:55
  149.9 2.8 collective-permute-start.4
  152.7 0.2 convert_element_type.39
  152.9 0.2 multiply_reduce_fusion
  153.1 0.1 dynamic-slice
  153.2 0.1 fusion.26
  153.3 131.7 %all-reduce.3.cloned.1.call-done = bf16[1024,1024]{1,0:T(8,128)(2,1)} async-done(((bf16[1024,1024]{1,0:T(8,128)(2,1)}), bf16[1024,1024]{1,0:T(8,128)(2,1)}) %all-reduce.3.cloned.1.call-update) | async-done | bytes 2097168 | tf_op jit(solution)/shard_map/psum | solution.py:55
  285.1 2.8 collective-permute-start.2
  287.9 0.7 fusion.44
  293.7 8.6 %add_convert_fusion.4 = bf16[192,1024]{1,0:T(8,128)(2,1)S(1)} fusion(f32[]{:T(128)} %bitcast.17, f32[]{:T(128)} %bitcast.16, f32[]{:T(128)} %bitcast.15, f32[]{:T(128)} %bitcast.14, f32[]{:T(128)} %bitcast.13, f32[]{:T(128)} %bitcast.12, f32[]{:T(128)} %bitcast.11, f32[]{:T(128)} %bitcast.10, f32[]{:T(128)} %bitcast.9, f32[]{:T(128)} %bitcast.8, ...), kind=kOutput, calls=%fused_computation.51 | convolution fusion | flops 407371776 | bytes 2883648 | tf_op jit(solution)/shard_map/rd,md->rm/dot_general | solution.py:23
  302.3 6.9 %add_convert_fusion.2 = bf16[192,1024]{1,0:T(8,128)(2,1)S(1)} fusion(f32[]{:T(128)} %bitcast.17, f32[]{:T(128)} %bitcast.16, f32[]{:T(128)} %bitcast.15, f32[]{:T(128)} %bitcast.14, f32[]{:T(128)} %bitcast.13, f32[]{:T(128)} %bitcast.12, f32[]{:T(128)} %bitcast.11, f32[]{:T(128)} %bitcast.10, f32[]{:T(128)} %bitcast.9, f32[]{:T(128)} %bitcast.8, ...), kind=kOutput, calls=%fused_computation.49 | convolution fusion | flops 407371776 | bytes 2883648 | tf_op jit(solution)/shard_map/rd,md->rm/dot_general | solution.py:23
  309.2 8.4 %add_convert_fusion.1 = bf16[192,1024]{1,0:T(8,128)(2,1)S(1)} fusion(f32[]{:T(128)} %bitcast.17, f32[]{:T(128)} %bitcast.16, f32[]{:T(128)} %bitcast.15, f32[]{:T(128)} %bitcast.14, f32[]{:T(128)} %bitcast.13, f32[]{:T(128)} %bitcast.12, f32[]{:T(128)} %bitcast.11, f32[]{:T(128)} %bitcast.10, f32[]{:T(128)} %bitcast.9, f32[]{:T(128)} %bitcast.8, ...), kind=kOutput, calls=%fused_computation.48 | convolution fusion | flops 407371776 | bytes 2883648 | tf_op jit(solution)/shard_map/rd,md->rm/dot_general | solution.py:23
  317.6 0.0 slice-start
  317.7 3.9 %fusion.12 = bf16[192,2048]{1,0:T(8,128)(2,1)S(1)} fusion(s32[2048]{0:T(1024)S(1)} %bitcast.29, bf16[192,1024]{1,0:T(8,128)(2,1)S(1)} %add_convert_fusion.1, bf16[192,1024]{1,0:T(8,128)(2,1)S(1)} %add_convert_fusion.2, pred[]{:T(512)S(6)} %eq.32), kind=kOutput, calls=%fused_computation.15 | convolution fusion | flops 1618739200 | bytes 1581057 | tf_op jit(solution)/shard_map/dot_general | solution.py:29
  321.6 0.0 slice-start.2
  321.6 0.3 collective-permute-start.5
  321.9 7.2 %add_convert_fusion.3 = bf16[192,1024]{1,0:T(8,128)(2,1)S(1)} fusion(f32[]{:T(128)} %bitcast.17, f32[]{:T(128)} %bitcast.16, f32[]{:T(128)} %bitcast.15, f32[]{:T(128)} %bitcast.14, f32[]{:T(128)} %bitcast.13, f32[]{:T(128)} %bitcast.12, f32[]{:T(128)} %bitcast.11, f32[]{:T(128)} %bitcast.10, f32[]{:T(128)} %bitcast.9, f32[]{:T(128)} %bitcast.8, ...), kind=kOutput, calls=%fused_computation.50 | convolution fusion | flops 407371776 | bytes 2883648 | tf_op jit(solution)/shard_map/rd,md->rm/dot_general | solution.py:23
  329.0 0.0 slice-start.3
  329.0 3.9 %fusion.13 = bf16[192,2048]{1,0:T(8,128)(2,1)S(1)} fusion(s32[2048]{0:T(1024)S(1)} %bitcast.28, bf16[192,1024]{1,0:T(8,128)(2,1)S(1)} %add_convert_fusion.3, bf16[192,1024]{1,0:T(8,128)(2,1)S(1)} %add_convert_fusion.4, pred[]{:T(512)S(6)} %eq.32), kind=kOutput, calls=%fused_computation.16 | convolution fusion | flops 1618739200 | bytes 1581057 | tf_op jit(solution)/shard_map/dot_general | solution.py:29
  332.9 0.6 collective-permute-start.3
  333.6 3.4 fusion.2
  337.1 4.6 %add_convert_fusion = bf16[384,2048]{1,0:T(8,128)(2,1)} fusion(f32[384,2048]{1,0:T(8,128)S(1)} %fusion.2, bf16[4096,2048]{1,0:T(8,128)(2,1)S(1)} %bitcast.31, bf16[192,2048]{1,0:T(8,128)(2,1)S(1)} %collective-permute-done.3, bf16[192,2048]{1,0:T(8,128)(2,1)S(1)} %fusion.13, pred[]{:T(512)S(6)} %eq.32), kind=kOutput, calls=%fused_computation.14 | convolution fusion | flops 3229876224 | bytes 14680065 | tf_op jit(solution)/shard_map/dot_general | solution.py:78
  (28 shorter events, 0.1 us)
Async XLA Ops:
  6.5 3.5 copy-start.2
  6.5 143.3 %all-reduce.5.cloned.1.call-start = ((), (), s32[]{:S(2)}) async-start(), calls=%async_computation.1 | async-start | bytes 4194304 | tf_op jit(solution)/shard_map/psum | solution.py:55
  6.5 9.8 %collective-permute-start = (f32[4]{0:T(128)}, f32[4]{0:T(128)S(1)}, u32[]{:S(2)}, u32[]{:S(2)}) collective-permute-start(f32[4]{0:T(128)} %param.11), channel_id=1, source_target_pairs={{0,1},{1,0},{2,3},{3,2},{4,5},{5,4},{6,7},{7,6},{8,9},{9,8},{10,11... | collective-permute-start | bytes 56 | tf_op jit(solution)/shard_map/ppermute | solution.py:34
  7.9 8.5 %collective-permute-start.1 = (f32[4]{0:T(128)}, f32[4]{0:T(128)S(1)}, u32[]{:S(2)}, u32[]{:S(2)}) collective-permute-start(f32[4]{0:T(128)} %param.12), channel_id=1, source_target_pairs={{0,1},{1,0},{2,3},{3,2},{4,5},{5,4},{6,7},{7,6},{8,9},{9,8},{10,11... | collective-permute-start | bytes 56 | tf_op jit(solution)/shard_map/ppermute | solution.py:34
  12.0 4.4 %copy-start.4 = (f32[4]{0:T(128)S(1)}, f32[4]{0:T(128)}, u32[]{:S(2)}) copy-start(f32[4]{0:T(128)} %param.11) | copy-start | bytes 52
  12.0 4.4 %copy-start.5 = (f32[4]{0:T(128)S(1)}, f32[4]{0:T(128)}, u32[]{:S(2)}) copy-start(f32[4]{0:T(128)} %param.12) | copy-start | bytes 52
  16.5 136.2 %copy-start = (bf16[384,1024]{1,0:T(8,128)(2,1)S(1)}, bf16[384,1024]{1,0:T(8,128)(2,1)}, u32[]{:S(2)}) copy-start(bf16[384,1024]{1,0:T(8,128)(2,1)} %param.7) | copy-start | bytes 2359300
  16.5 268.6 %all-reduce.3.cloned.1.call-start = ((), (), s32[]{:S(2)}) async-start(), calls=%async_computation | async-start | bytes 4194304 | tf_op jit(solution)/shard_map/psum | solution.py:55
  149.9 159.3 %collective-permute-start.4 = (bf16[1024,1024]{1,0:T(8,128)(2,1)}, bf16[1024,1024]{1,0:T(8,128)(2,1)}, u32[]{:S(2)}, u32[]{:S(2)}) collective-permute-start(bf16[1024,1024]{1,0:T(8,128)(2,1)} %all-reduce.5.cloned.1.call-done), channel_id=1, source_target_pairs={{0,1},{1,0},{2,3},{3,2},{4,5},{5,4},{6,7},{7,6},{8,9},{9,8},{10,11... | collective-permute-start | bytes 6291464 | tf_op jit(solution)/shard_map/ppermute | solution.py:34
  152.7 135.2 %copy-start.1 = (s32[2,2048]{1,0:T(2,128)S(1)}, s32[2,2048]{1,0:T(2,128)}, u32[]{:S(2)}) copy-start(s32[2,2048]{1,0:T(2,128)} %param.10) | copy-start | bytes 49156
  285.1 36.8 %collective-permute-start.2 = (bf16[1024,1024]{1,0:T(8,128)(2,1)}, bf16[1024,1024]{1,0:T(8,128)(2,1)S(1)}, u32[]{:S(2)}, u32[]{:S(2)}) collective-permute-start(bf16[1024,1024]{1,0:T(8,128)(2,1)} %all-reduce.3.cloned.1.call-done), channel_id=1, source_target_pairs={{0,1},{1,0},{2,3},{3,2},{4,5},{5,4},{6,7},{7,6},{8,9},{9,8},{10,11... | collective-permute-start | bytes 6291464 | tf_op jit(solution)/shard_map/ppermute | solution.py:34
  293.7 8.6 %copy-start.3 = (bf16[1024,1024]{1,0:T(8,128)(2,1)S(1)}, bf16[1024,1024]{1,0:T(8,128)(2,1)}, u32[]{:S(2)}) copy-start(bf16[1024,1024]{1,0:T(8,128)(2,1)} %all-reduce.5.cloned.1.call-done) | copy-start | bytes 6291460
  317.6 15.9 %slice-start = ((s8[16777216]{0:T(1024)(128)(4,1)}), s8[4194304]{0:T(1024)(128)(4,1)S(1)}, s32[]{:S(2)}) async-start(s8[16777216]{0:T(1024)(128)(4,1)} %bitcast.30), calls=%async_computation.2 | async-start | bytes 8388608
  317.6 15.9 %slice-start.1 = ((s8[16777216]{0:T(1024)(128)(4,1)}), s8[4194304]{0:T(1024)(128)(4,1)S(1)}, s32[]{:S(2)}) async-start(s8[16777216]{0:T(1024)(128)(4,1)} %bitcast.30), calls=%async_computation.3 | async-start | bytes 8388608
  321.6 12.0 %slice-start.2 = ((s8[16777216]{0:T(1024)(128)(4,1)}), s8[4194304]{0:T(1024)(128)(4,1)S(1)}, s32[]{:S(2)}) async-start(s8[16777216]{0:T(1024)(128)(4,1)} %bitcast.30), calls=%async_computation.4 | async-start | bytes 8388608
  321.6 12.0 %collective-permute-start.5 = (bf16[192,2048]{1,0:T(8,128)(2,1)S(1)}, bf16[192,2048]{1,0:T(8,128)(2,1)S(1)}, u32[]{:S(2)}, u32[]{:S(2)}) collective-permute-start(bf16[192,2048]{1,0:T(8,128)(2,1)S(1)} %fusion.12), channel_id=1, source_target_pairs={{0,1},{1,0},{2,3},{3,2},{4,5},{5,4},{6,7},{7,6},{8,9},{9,8},{10,11... | collective-permute-start | bytes 2359304 | tf_op jit(solution)/shard_map/ppermute | solution.py:34
  329.0 4.5 %slice-start.3 = ((s8[16777216]{0:T(1024)(128)(4,1)}), s8[4194304]{0:T(1024)(128)(4,1)S(1)}, s32[]{:S(2)}) async-start(s8[16777216]{0:T(1024)(128)(4,1)} %bitcast.30), calls=%async_computation.5 | async-start | bytes 8388608
  332.9 4.1 %collective-permute-start.3 = (bf16[192,2048]{1,0:T(8,128)(2,1)S(1)}, bf16[192,2048]{1,0:T(8,128)(2,1)S(1)}, u32[]{:S(2)}, u32[]{:S(2)}) collective-permute-start(bf16[192,2048]{1,0:T(8,128)(2,1)S(1)} %fusion.13), channel_id=1, source_target_pairs={{0,1},{1,0},{2,3},{3,2},{4,5},{5,4},{6,7},{7,6},{8,9},{9,8},{10,11... | collective-permute-start | bytes 2359304 | tf_op jit(solution)/shard_map/ppermute | solution.py:34
Sparse Core Ops, SparseCore 0:
  16.6 133.2 all-reduce.4
  154.7 130.2 all-reduce.2

commit v10 on v7

--- a/solution.py
+++ b/solution.py
@@ -45,12 +45,21 @@
     here = lax.axis_index(SPREAD)
     widths = jnp.concatenate([inverse_width, swap_cores(inverse_width)])
     weights = jnp.concatenate([mixture, swap_cores(mixture)])
-    pieces = []
-    for number in range(block_count):
-        chosen = normalize(lax.dynamic_slice_in_dim(candidates, core * half, half, axis=0))
-        chosen = jnp.where(here == block_owner[number], chosen, jnp.zeros_like(chosen))
-        pieces.append(chosen)
-    arrived = lax.psum(pieces, SPREAD)
+    count = lax.axis_size(SPREAD)
+    chosen = normalize(lax.dynamic_slice_in_dim(candidates, core * half, half, axis=0))
+    chosen, widths, weights = lax.optimization_barrier((chosen, widths, weights))
+    pieces = chosen.reshape(count, half // count, chosen.shape[1])
+    spread = lax.all_to_all(pieces, SPREAD, 0, 0, tiled=True)
+    kept = jnp.stack(
+        [
+            lax.dynamic_index_in_dim(spread, block_owner[number], 0, keepdims=False)
+            for number in range(block_count)
+        ]
+    )
+    gathered = lax.all_to_all(
+        jnp.broadcast_to(kept[None], (count,) + kept.shape), SPREAD, 0, 0, tiled=True
+    )
+    arrived = [gathered[:, number].reshape(half, chosen.shape[1]) for number in range(block_count)]
     share = unit_rows.shape[0] // cores
     own_rows = lax.dynamic_slice_in_dim(unit_rows, core * share, share, axis=0)
     features = jnp.zeros((unit_rows.shape[0], whitening.shape[1]), jnp.float32)

time: 222 us -> 166 us (0.75)
  waiting for transfers between devices: 139 us -> 23.5 us
  blocking collectives: 0 us -> 57.9 us
  starting transfers between devices: 4.55 us -> 16.4 us
  between operations: 19.9 us -> 9 us
    psum x1 -> x0, waiting for transfers between devices: 139 us -> none  [per_device(): arrived = lax.psum(pieces, SPREAD)]
    all_to_all x0 -> x1, blocking collectives: none -> 57.9 us  [per_device(): lax.all_to_all(jnp.broadcast_to(kept[None], (count,) + kept.shape), SPREA...]
    all_to_all x0 -> x1, waiting for transfers between devices: none -> 23.5 us  [per_device(): spread = lax.all_to_all(pieces, SPREAD, 0, 0, tiled=True)]
    all_to_all x0 -> x1, starting transfers between devices: none -> 11.4 us  [per_device(): spread = lax.all_to_all(pieces, SPREAD, 0, 0, tiled=True)]
    select_n x1 -> x0, other arithmetic: 4.35 us -> none  [per_device(): jnp.where(here == block_owner[number], chosen, jnp.zeros_like(chosen))]
    convert_element_type x1 -> x2, other arithmetic: 0.11 us -> 3.45 us  [normalize(): return (widened * scale).astype(jnp.bfloat16)]
    slice x0 -> x1, local copies, waits for them, and re-layouts: none -> 2.39 us  [per_device(): gathered[:, number].reshape(half, chosen.shape[1])]
  transfers between devices with their start and end apart: 7 -> 7, of which waited for: 1 -> 1; matrix products, arithmetic and copies ran while one was open for 21% -> 30% of each run, Pallas kernels for 0% -> 0%
where the time goes in v10:
time: 166 us; the launch traced here: 164 us
  blocking collectives  57.9 us (35%)
  matrix products  46.8 us (28%)
  waiting for transfers between devices  23.5 us (14%)
  starting transfers between devices  16.4 us (10%)
  between operations  9 us (5%)
  other arithmetic  6.09 us (4%)
  local copies, waits for them, and re-layouts  4.41 us (3%)
    all_to_all x1, blocking collectives, per_device(): lax.all_to_all(jnp.broadcast_to(kept[None], (count,) + kept.shape), SPREA...  57.9 us
    dot_general x4, matrix products, inner_products(): jnp.einsum('rd,md->rm', unit_rows, landmark, preferred_element_type=jnp.f...  31 us
    all_to_all x1, waiting for transfers between devices, per_device(): spread = lax.all_to_all(pieces, SPREAD, 0, 0, tiled=True)  23.5 us
    all_to_all x1, starting transfers between devices, per_device(): spread = lax.all_to_all(pieces, SPREAD, 0, 0, tiled=True)  11.4 us
    dot_general x2, matrix products, per_device(): jnp.dot(kernel, rows, preferred_element_type=jnp.float32)  8 us
    dot_general x2, matrix products, reorder_columns(): ordered = jnp.dot(kernel, onehot, preferred_element_type=jnp.float32)  7.78 us
    ppermute x6, starting transfers between devices, swap_cores(): return lax.ppermute(value, 'bw', [(0, 1), (1, 0)])  5.01 us
    convert_element_type x2, other arithmetic, normalize(): return (widened * scale).astype(jnp.bfloat16)  3.45 us
  transfers between devices with their start and end apart: 7, of which 1 were waited for; matrix products, arithmetic and copies ran while one was open for 30% of the time, Pallas kernels for 0%

profile of v10, /device:TPU:1, one launch (start us, length us, event | category | flops | bytes accessed | tf_op | source)
XLA Modules:
  0.0 164.1 jit_solution(12270364909222387447)
XLA Ops:
  0.0 1.4 collective-permute-start
  1.4 2.1 %fusion.8 = f32[1024]{0:T(1024)S(1)} fusion(bf16[2048,1024]{1,0:T(8,128)(2,1)} %param.8, s32[]{:T(128)S(6)} %select_n.39), kind=kLoop, calls=%fused_computation.12 | loop fusion | flops 3144704 | bytes 2101252 | tf_op jit(solution)/shard_map/reduce_sum | solution.py:11
  3.5 0.0 copy-start.5
  3.5 3.3 %fusion.9 = bf16[1024,1024]{1,0:T(8,128)(2,1)} fusion(f32[1024]{0:T(1024)S(1)} %add_rsqrt_fusion, bf16[2048,1024]{1,0:T(8,128)(2,1)} %param.8, s32[]{:T(128)S(6)} %select_n.39), kind=kLoop, calls=%fused_computation.13 | loop fusion | flops 3145728 | bytes 4198404 | tf_op jit(solution)/shard_map/convert_element_type | solution.py:12
  6.8 0.1 pad_maximum_fusion.1
  6.9 0.1 pad_maximum_fusion.2
  7.0 11.4 %all-to-all-start = ((bf16[64,16,1024]{2,1,0:T(8,128)(2,1)}), bf16[64,16,1024]{2,1,0:T(8,128)(2,1)S(1)}, u32[]{:S(2)}, u32[]{:S(2)}) async-start(bf16[64,16,1024]{2,1,0:T(8,128)(2,1)} %bitcast.2), calls=%async_computation | async-start | bytes 4194304 | tf_op jit(solution)/shard_map/all_to_all | solution.py:52
  18.4 0.6 fusion.47
  22.8 23.5 %all-to-all-done = bf16[64,16,1024]{2,1,0:T(8,128)(2,1)S(1)} async-done(((bf16[64,16,1024]{2,1,0:T(8,128)(2,1)}), bf16[64,16,1024]{2,1,0:T(8,128)(2,1)S(1)}, u32[]{:S(2)}, u32[]{:S(2)}) %all-to-all-start) | async-done | bytes 2097184 | tf_op jit(solution)/shard_map/all_to_all | solution.py:52
  46.4 0.5 broadcast_in_dim.2
  46.9 57.9 %all_to_all.10 = bf16[64,2,16,1024]{3,2,1,0:T(8,128)(2,1)S(1)} all-to-all(bf16[64,2,16,1024]{3,2,1,0:T(8,128)(2,1)S(1)} %broadcast_in_dim.2), channel_id=1, replica_groups=mesh['row'=8,'lmk'=8,'bw'=2] {'row','lmk'}, dimensions={0} | all-to-all | bytes 8388608 | tf_op jit(solution)/shard_map/all_to_all | solution.py:59
  104.8 2.4 %fusion.43 = (bf16[64,1,16,1024]{3,2,1,0:T(8,128)(2,1)}, bf16[64,1,16,1024]{3,2,1,0:T(8,128)(2,1)}) fusion(bf16[64,2,16,1024]{3,2,1,0:T(8,128)(2,1)S(1)} %all_to_all.10), kind=kLoop, calls=%fused_computation.63 | loop fusion | bytes 8388608 | tf_op jit(solution)/shard_map/slice | solution.py:62
  107.2 2.5 %collective-permute-start.4 = (bf16[1024,1024]{1,0:T(8,128)(2,1)}, bf16[1024,1024]{1,0:T(8,128)(2,1)}, u32[]{:S(2)}, u32[]{:S(2)}) collective-permute-start(bf16[1024,1024]{1,0:T(8,128)(2,1)} %bitcast.21), channel_id=1, source_target_pairs={{0,1},{1,0},{2,3},{3,2},{4,5},{5,4},{6,7},{7,6},{8,9},{9,8},{10,11... | collective-permute-start | bytes 6291464 | tf_op jit(solution)/shard_map/ppermute | solution.py:34
  109.7 0.2 convert_element_type.37
  109.9 0.2 multiply_reduce_fusion
  110.1 0.1 dynamic-slice
  110.2 0.1 fusion.26
  110.3 0.3 collective-permute-start.2
  110.7 0.7 fusion.45
  116.3 6.8 %add_convert_fusion.4 = bf16[192,1024]{1,0:T(8,128)(2,1)S(1)} fusion(f32[]{:T(128)} %bitcast.19, f32[]{:T(128)} %bitcast.18, f32[]{:T(128)} %bitcast.17, f32[]{:T(128)} %bitcast.16, f32[]{:T(128)} %bitcast.15, f32[]{:T(128)} %bitcast.14, f32[]{:T(128)} %bitcast.13, f32[]{:T(128)} %bitcast.12, f32[]{:T(128)} %bitcast.11, f32[]{:T(128)} %bitcast.10, ...), kind=kOutput, calls=%fused_computation.49 | convolution fusion | flops 407371776 | bytes 2883648 | tf_op jit(solution)/shard_map/rd,md->rm/dot_general | solution.py:23
  123.1 8.4 %add_convert_fusion.2 = bf16[192,1024]{1,0:T(8,128)(2,1)S(1)} fusion(f32[]{:T(128)} %bitcast.19, f32[]{:T(128)} %bitcast.18, f32[]{:T(128)} %bitcast.17, f32[]{:T(128)} %bitcast.16, f32[]{:T(128)} %bitcast.15, f32[]{:T(128)} %bitcast.14, f32[]{:T(128)} %bitcast.13, f32[]{:T(128)} %bitcast.12, f32[]{:T(128)} %bitcast.11, f32[]{:T(128)} %bitcast.10, ...), kind=kOutput, calls=%fused_computation.47 | convolution fusion | flops 407371776 | bytes 2883648 | tf_op jit(solution)/shard_map/rd,md->rm/dot_general | solution.py:23
  131.6 8.5 %add_convert_fusion.1 = bf16[192,1024]{1,0:T(8,128)(2,1)S(1)} fusion(f32[]{:T(128)} %bitcast.19, f32[]{:T(128)} %bitcast.18, f32[]{:T(128)} %bitcast.17, f32[]{:T(128)} %bitcast.16, f32[]{:T(128)} %bitcast.15, f32[]{:T(128)} %bitcast.14, f32[]{:T(128)} %bitcast.13, f32[]{:T(128)} %bitcast.12, f32[]{:T(128)} %bitcast.11, f32[]{:T(128)} %bitcast.10, ...), kind=kOutput, calls=%fused_computation.46 | convolution fusion | flops 407371776 | bytes 2883648 | tf_op jit(solution)/shard_map/rd,md->rm/dot_general | solution.py:23
  140.1 0.0 slice-start
  140.1 3.9 %fusion.12 = bf16[192,2048]{1,0:T(8,128)(2,1)S(1)} fusion(s32[2048]{0:T(1024)S(1)} %bitcast.34, bf16[192,1024]{1,0:T(8,128)(2,1)S(1)} %add_convert_fusion.1, bf16[192,1024]{1,0:T(8,128)(2,1)S(1)} %add_convert_fusion.2, pred[]{:T(512)S(6)} %eq.26), kind=kOutput, calls=%fused_computation.15 | convolution fusion | flops 1618739200 | bytes 1581057 | tf_op jit(solution)/shard_map/dot_general | solution.py:29
  144.0 0.0 slice-start.2
  144.0 0.8 collective-permute-start.5
  144.8 7.2 %add_convert_fusion.3 = bf16[192,1024]{1,0:T(8,128)(2,1)S(1)} fusion(f32[]{:T(128)} %bitcast.19, f32[]{:T(128)} %bitcast.18, f32[]{:T(128)} %bitcast.17, f32[]{:T(128)} %bitcast.16, f32[]{:T(128)} %bitcast.15, f32[]{:T(128)} %bitcast.14, f32[]{:T(128)} %bitcast.13, f32[]{:T(128)} %bitcast.12, f32[]{:T(128)} %bitcast.11, f32[]{:T(128)} %bitcast.10, ...), kind=kOutput, calls=%fused_computation.48 | convolution fusion | flops 407371776 | bytes 2883648 | tf_op jit(solution)/shard_map/rd,md->rm/dot_general | solution.py:23
  152.0 0.0 slice-start.3
  152.0 3.9 %fusion.13 = bf16[192,2048]{1,0:T(8,128)(2,1)S(1)} fusion(s32[2048]{0:T(1024)S(1)} %bitcast.33, bf16[192,1024]{1,0:T(8,128)(2,1)S(1)} %add_convert_fusion.3, bf16[192,1024]{1,0:T(8,128)(2,1)S(1)} %add_convert_fusion.4, pred[]{:T(512)S(6)} %eq.26), kind=kOutput, calls=%fused_computation.16 | convolution fusion | flops 1618739200 | bytes 1581057 | tf_op jit(solution)/shard_map/dot_general | solution.py:29
  155.9 0.1 collective-permute-start.3
  156.1 3.4 %fusion.2 = f32[384,2048]{1,0:T(8,128)S(1)} fusion(bf16[4096,2048]{1,0:T(8,128)(2,1)S(1)} %bitcast.36, bf16[192,2048]{1,0:T(8,128)(2,1)S(1)} %collective-permute-done.5, bf16[192,2048]{1,0:T(8,128)(2,1)S(1)} %fusion.12, pred[]{:T(512)S(6)} %eq.26), kind=kOutput, calls=%fused_computation.4 | convolution fusion | flops 3228303360 | bytes 13107201 | tf_op jit(solution)/shard_map/dot_general | solution.py:85
  159.6 4.6 %add_convert_fusion = bf16[384,2048]{1,0:T(8,128)(2,1)} fusion(f32[384,2048]{1,0:T(8,128)S(1)} %fusion.2, bf16[4096,2048]{1,0:T(8,128)(2,1)S(1)} %bitcast.36, bf16[192,2048]{1,0:T(8,128)(2,1)S(1)} %collective-permute-done.3, bf16[192,2048]{1,0:T(8,128)(2,1)S(1)} %fusion.13, pred[]{:T(512)S(6)} %eq.26), kind=kOutput, calls=%fused_computation.14 | convolution fusion | flops 3229876224 | bytes 14680065 | tf_op jit(solution)/shard_map/dot_general | solution.py:85
  (29 shorter events, 0.1 us)
Async XLA Ops:
  0.0 6.8 %collective-permute-start = (f32[4]{0:T(128)}, f32[4]{0:T(128)S(1)}, u32[]{:S(2)}, u32[]{:S(2)}) collective-permute-start(f32[4]{0:T(128)} %param.11), channel_id=1, source_target_pairs={{0,1},{1,0},{2,3},{3,2},{4,5},{5,4},{6,7},{7,6},{8,9},{9,8},{10,11... | collective-permute-start | bytes 56 | tf_op jit(solution)/shard_map/ppermute | solution.py:34
  1.4 5.5 %collective-permute-start.1 = (f32[4]{0:T(128)}, f32[4]{0:T(128)S(1)}, u32[]{:S(2)}, u32[]{:S(2)}) collective-permute-start(f32[4]{0:T(128)} %param.12), channel_id=1, source_target_pairs={{0,1},{1,0},{2,3},{3,2},{4,5},{5,4},{6,7},{7,6},{8,9},{9,8},{10,11... | collective-permute-start | bytes 56 | tf_op jit(solution)/shard_map/ppermute | solution.py:34
  3.5 3.4 %copy-start.4 = (f32[4]{0:T(128)S(1)}, f32[4]{0:T(128)}, u32[]{:S(2)}) copy-start(f32[4]{0:T(128)} %param.11) | copy-start | bytes 52
  3.5 3.4 %copy-start.5 = (f32[4]{0:T(128)S(1)}, f32[4]{0:T(128)}, u32[]{:S(2)}) copy-start(f32[4]{0:T(128)} %param.12) | copy-start | bytes 52
  7.0 11.4 %copy-start.3 = (s32[2]{0:T(128)S(1)}, s32[2]{0:T(128)}, u32[]{:S(2)}) copy-start(s32[2]{0:T(128)} %param.9) | copy-start | bytes 28
  7.0 39.4 %all-to-all-start = ((bf16[64,16,1024]{2,1,0:T(8,128)(2,1)}), bf16[64,16,1024]{2,1,0:T(8,128)(2,1)S(1)}, u32[]{:S(2)}, u32[]{:S(2)}) async-start(bf16[64,16,1024]{2,1,0:T(8,128)(2,1)} %bitcast.2), calls=%async_computation | async-start | bytes 4194304 | tf_op jit(solution)/shard_map/all_to_all | solution.py:52
  104.8 4.9 %copy-start = (bf16[384,1024]{1,0:T(8,128)(2,1)S(1)}, bf16[384,1024]{1,0:T(8,128)(2,1)}, u32[]{:S(2)}) copy-start(bf16[384,1024]{1,0:T(8,128)(2,1)} %param.7) | copy-start | bytes 2359300
  107.2 24.4 %collective-permute-start.4 = (bf16[1024,1024]{1,0:T(8,128)(2,1)}, bf16[1024,1024]{1,0:T(8,128)(2,1)}, u32[]{:S(2)}, u32[]{:S(2)}) collective-permute-start(bf16[1024,1024]{1,0:T(8,128)(2,1)} %bitcast.21), channel_id=1, source_target_pairs={{0,1},{1,0},{2,3},{3,2},{4,5},{5,4},{6,7},{7,6},{8,9},{9,8},{10,11... | collective-permute-start | bytes 6291464 | tf_op jit(solution)/shard_map/ppermute | solution.py:34
  109.7 0.9 copy-start.2
  109.9 6.4 %copy-start.1 = (bf16[64,1,16,1024]{3,2,1,0:T(8,128)(2,1)S(1)}, bf16[64,1,16,1024]{3,2,1,0:T(8,128)(2,1)}, u32[]{:S(2)}) copy-start(bf16[64,1,16,1024]{3,2,1,0:T(8,128)(2,1)} %get-tuple-element.11) | copy-start | bytes 6291460
  110.3 34.4 %collective-permute-start.2 = (bf16[1024,1024]{1,0:T(8,128)(2,1)}, bf16[1024,1024]{1,0:T(8,128)(2,1)S(1)}, u32[]{:S(2)}, u32[]{:S(2)}) collective-permute-start(bf16[1024,1024]{1,0:T(8,128)(2,1)} %bitcast.31), channel_id=1, source_target_pairs={{0,1},{1,0},{2,3},{3,2},{4,5},{5,4},{6,7},{7,6},{8,9},{9,8},{10,11... | collective-permute-start | bytes 6291464 | tf_op jit(solution)/shard_map/ppermute | solution.py:34
  140.1 16.0 %slice-start = ((s8[16777216]{0:T(1024)(128)(4,1)}), s8[4194304]{0:T(1024)(128)(4,1)S(1)}, s32[]{:S(2)}) async-start(s8[16777216]{0:T(1024)(128)(4,1)} %bitcast.35), calls=%async_computation.2 | async-start | bytes 8388608
  140.1 16.0 %slice-start.1 = ((s8[16777216]{0:T(1024)(128)(4,1)}), s8[4194304]{0:T(1024)(128)(4,1)S(1)}, s32[]{:S(2)}) async-start(s8[16777216]{0:T(1024)(128)(4,1)} %bitcast.35), calls=%async_computation.3 | async-start | bytes 8388608
  144.0 12.1 %slice-start.2 = ((s8[16777216]{0:T(1024)(128)(4,1)}), s8[4194304]{0:T(1024)(128)(4,1)S(1)}, s32[]{:S(2)}) async-start(s8[16777216]{0:T(1024)(128)(4,1)} %bitcast.35), calls=%async_computation.4 | async-start | bytes 8388608
  144.0 12.0 %collective-permute-start.5 = (bf16[192,2048]{1,0:T(8,128)(2,1)S(1)}, bf16[192,2048]{1,0:T(8,128)(2,1)S(1)}, u32[]{:S(2)}, u32[]{:S(2)}) collective-permute-start(bf16[192,2048]{1,0:T(8,128)(2,1)S(1)} %fusion.12), channel_id=1, source_target_pairs={{0,1},{1,0},{2,3},{3,2},{4,5},{5,4},{6,7},{7,6},{8,9},{9,8},{10,11... | collective-permute-start | bytes 2359304 | tf_op jit(solution)/shard_map/ppermute | solution.py:34
  152.0 4.0 %slice-start.3 = ((s8[16777216]{0:T(1024)(128)(4,1)}), s8[4194304]{0:T(1024)(128)(4,1)S(1)}, s32[]{:S(2)}) async-start(s8[16777216]{0:T(1024)(128)(4,1)} %bitcast.35), calls=%async_computation.5 | async-start | bytes 8388608
  155.9 3.6 %collective-permute-start.3 = (bf16[192,2048]{1,0:T(8,128)(2,1)S(1)}, bf16[192,2048]{1,0:T(8,128)(2,1)S(1)}, u32[]{:S(2)}, u32[]{:S(2)}) collective-permute-start(bf16[192,2048]{1,0:T(8,128)(2,1)S(1)} %fusion.13), channel_id=1, source_target_pairs={{0,1},{1,0},{2,3},{3,2},{4,5},{5,4},{6,7},{7,6},{8,9},{9,8},{10,11... | collective-permute-start | bytes 2359304 | tf_op jit(solution)/shard_map/ppermute | solution.py:34

commit v11 on v10

--- a/solution.py
+++ b/solution.py
@@ -46,16 +46,16 @@
     widths = jnp.concatenate([inverse_width, swap_cores(inverse_width)])
     weights = jnp.concatenate([mixture, swap_cores(mixture)])
     count = lax.axis_size(SPREAD)
-    chosen = normalize(lax.dynamic_slice_in_dim(candidates, core * half, half, axis=0))
-    chosen, widths, weights = lax.optimization_barrier((chosen, widths, weights))
+    chosen = lax.dynamic_slice_in_dim(candidates, core * half, half, axis=0)
     pieces = chosen.reshape(count, half // count, chosen.shape[1])
     spread = lax.all_to_all(pieces, SPREAD, 0, 0, tiled=True)
     kept = jnp.stack(
         [
-            lax.dynamic_index_in_dim(spread, block_owner[number], 0, keepdims=False)
+            normalize(lax.dynamic_index_in_dim(spread, block_owner[number], 0, keepdims=False))
             for number in range(block_count)
         ]
     )
+    kept, widths, weights = lax.optimization_barrier((kept, widths, weights))
     gathered = lax.all_to_all(
         jnp.broadcast_to(kept[None], (count,) + kept.shape), SPREAD, 0, 0, tiled=True
     )

time: 166 us -> 166 us (level)
  other arithmetic: 6.09 us -> 0.89 us
  local copies, waits for them, and re-layouts: 4.41 us -> 8.09 us
  matrix products: 46.8 us -> 49.5 us
    convert_element_type x2, other arithmetic: 3.45 us -> 0.19 us  [normalize(): return (widened * scale).astype(jnp.bfloat16)]
    dynamic_slice x1, local copies, waits for them, and re-layouts: 0.01 us -> 3.1 us  [per_device(): chosen = lax.dynamic_slice_in_dim(candidates, core * half, half, axis=0)]
    dot_general x4, matrix products: 31 us -> 33.8 us  [inner_products(): jnp.einsum('rd,md->rm', unit_rows, landmark, preferred_element_type=jnp.f...]
    reduce_sum x2, other arithmetic: 2.3 us -> 0.36 us  [normalize(): jnp.sum(widened * widened, axis=-1, keepdims=True) + 1e-06]
  transfers between devices with their start and end apart: 7 -> 7, of which waited for: 1 -> 1; matrix products, arithmetic and copies ran while one was open for 30% -> 29% of each run, Pallas kernels for 0% -> 0%
where the time goes in v11:
time: 166 us; the launch traced here: 165 us
  blocking collectives  57.6 us (35%)
  matrix products  49.5 us (30%)
  waiting for transfers between devices  22.7 us (14%)
  starting transfers between devices  16.8 us (10%)
  between operations  8.86 us (5%)
  local copies, waits for them, and re-layouts  8.09 us (5%)
    all_to_all x1, blocking collectives, per_device(): lax.all_to_all(jnp.broadcast_to(kept[None], (count,) + kept.shape), SPREA...  57.6 us
    dot_general x4, matrix products, inner_products(): jnp.einsum('rd,md->rm', unit_rows, landmark, preferred_element_type=jnp.f...  33.8 us
    all_to_all x1, waiting for transfers between devices, per_device(): spread = lax.all_to_all(pieces, SPREAD, 0, 0, tiled=True)  22.7 us
    all_to_all x1, starting transfers between devices, per_device(): spread = lax.all_to_all(pieces, SPREAD, 0, 0, tiled=True)  12.1 us
    dot_general x2, matrix products, per_device(): jnp.dot(kernel, rows, preferred_element_type=jnp.float32)  8.01 us
    dot_general x2, matrix products, reorder_columns(): ordered = jnp.dot(kernel, onehot, preferred_element_type=jnp.float32)  7.78 us
    ppermute x6, starting transfers between devices, swap_cores(): return lax.ppermute(value, 'bw', [(0, 1), (1, 0)])  4.76 us
  transfers between devices with their start and end apart: 7, of which 1 were waited for; matrix products, arithmetic and copies ran while one was open for 29% of the time, Pallas kernels for 0%

profile of v11, /device:TPU:1, one launch (start us, length us, event | category | flops | bytes accessed | tf_op | source)
XLA Modules:
  0.0 164.5 jit_solution(2250309120153350890)
XLA Ops:
  0.0 3.1 %constant_dynamic-slice_fusion = bf16[1024,1024]{1,0:T(8,128)(2,1)} fusion(bf16[2048,1024]{1,0:T(8,128)(2,1)} %param.8, s32[]{:T(128)S(6)} %select_n.39), kind=kLoop, calls=%fused_computation.58 | loop fusion | bytes 4194308 | tf_op jit(solution)/shard_map/dynamic_slice | solution.py:49
  3.1 12.1 %all-to-all-start = ((bf16[64,16,1024]{2,1,0:T(8,128)(2,1)}), bf16[64,16,1024]{2,1,0:T(8,128)(2,1)S(1)}, u32[]{:S(2)}, u32[]{:S(2)}) async-start(bf16[64,16,1024]{2,1,0:T(8,128)(2,1)} %bitcast), calls=%async_computation | async-start | bytes 4194304 | tf_op jit(solution)/shard_map/all_to_all | solution.py:51
  15.2 1.0 collective-permute-start
  16.2 0.1 collective-permute-start.1
  16.3 0.6 fusion.49
  20.6 0.1 pad_maximum_fusion.1
  20.7 0.1 pad_maximum_fusion.2
  20.7 22.7 %all-to-all-done = bf16[64,16,1024]{2,1,0:T(8,128)(2,1)S(1)} async-done(((bf16[64,16,1024]{2,1,0:T(8,128)(2,1)}), bf16[64,16,1024]{2,1,0:T(8,128)(2,1)S(1)}, u32[]{:S(2)}, u32[]{:S(2)}) %all-to-all-start) | async-done | bytes 2097184 | tf_op jit(solution)/shard_map/all_to_all | solution.py:51
  43.4 0.1 fusion.37
  43.5 0.1 fusion.38
  43.6 0.5 broadcast_in_dim.2
  44.2 57.6 %all_to_all.10 = bf16[64,2,16,1024]{3,2,1,0:T(8,128)(2,1)S(1)} all-to-all(bf16[64,2,16,1024]{3,2,1,0:T(8,128)(2,1)S(1)} %broadcast_in_dim.2), channel_id=1, replica_groups=mesh['row'=8,'lmk'=8,'bw'=2] {'row','lmk'}, dimensions={0} | all-to-all | bytes 8388608 | tf_op jit(solution)/shard_map/all_to_all | solution.py:59
  101.8 2.4 %fusion.45 = (bf16[64,1,16,1024]{3,2,1,0:T(8,128)(2,1)}, bf16[64,1,16,1024]{3,2,1,0:T(8,128)(2,1)}) fusion(bf16[64,2,16,1024]{3,2,1,0:T(8,128)(2,1)S(1)} %all_to_all.10), kind=kLoop, calls=%fused_computation.67 | loop fusion | bytes 8388608 | tf_op jit(solution)/shard_map/slice | solution.py:62
  104.2 2.5 %collective-permute-start.4 = (bf16[1024,1024]{1,0:T(8,128)(2,1)}, bf16[1024,1024]{1,0:T(8,128)(2,1)}, u32[]{:S(2)}, u32[]{:S(2)}) collective-permute-start(bf16[1024,1024]{1,0:T(8,128)(2,1)} %bitcast.21), channel_id=1, source_target_pairs={{0,1},{1,0},{2,3},{3,2},{4,5},{5,4},{6,7},{7,6},{8,9},{9,8},{10,11... | collective-permute-start | bytes 6291464 | tf_op jit(solution)/shard_map/ppermute | solution.py:34
  106.7 0.2 multiply_reduce_fusion
  106.9 0.3 collective-permute-start.2
  107.2 0.2 convert_element_type.51
  107.4 0.1 dynamic-slice
  107.4 0.1 fusion.24
  107.6 0.7 fusion.48
  113.2 0.7 fusion.47
  113.9 8.3 %add_convert_fusion.4 = bf16[192,1024]{1,0:T(8,128)(2,1)S(1)} fusion(f32[]{:T(128)} %bitcast.19, f32[]{:T(128)} %bitcast.18, f32[]{:T(128)} %bitcast.17, f32[]{:T(128)} %bitcast.16, f32[]{:T(128)} %bitcast.15, f32[]{:T(128)} %bitcast.14, f32[]{:T(128)} %bitcast.13, f32[]{:T(128)} %bitcast.12, f32[]{:T(128)} %bitcast.11, f32[]{:T(128)} %bitcast.10, ...), kind=kOutput, calls=%fused_computation.45 | convolution fusion | flops 407371776 | bytes 2883648 | tf_op jit(solution)/shard_map/rd,md->rm/dot_general | solution.py:23
  122.2 8.3 %add_convert_fusion.2 = bf16[192,1024]{1,0:T(8,128)(2,1)S(1)} fusion(f32[]{:T(128)} %bitcast.19, f32[]{:T(128)} %bitcast.18, f32[]{:T(128)} %bitcast.17, f32[]{:T(128)} %bitcast.16, f32[]{:T(128)} %bitcast.15, f32[]{:T(128)} %bitcast.14, f32[]{:T(128)} %bitcast.13, f32[]{:T(128)} %bitcast.12, f32[]{:T(128)} %bitcast.11, f32[]{:T(128)} %bitcast.10, ...), kind=kOutput, calls=%fused_computation.43 | convolution fusion | flops 407371776 | bytes 2883648 | tf_op jit(solution)/shard_map/rd,md->rm/dot_general | solution.py:23
  130.6 8.3 %add_convert_fusion.1 = bf16[192,1024]{1,0:T(8,128)(2,1)S(1)} fusion(f32[]{:T(128)} %bitcast.19, f32[]{:T(128)} %bitcast.18, f32[]{:T(128)} %bitcast.17, f32[]{:T(128)} %bitcast.16, f32[]{:T(128)} %bitcast.15, f32[]{:T(128)} %bitcast.14, f32[]{:T(128)} %bitcast.13, f32[]{:T(128)} %bitcast.12, f32[]{:T(128)} %bitcast.11, f32[]{:T(128)} %bitcast.10, ...), kind=kOutput, calls=%fused_computation.42 | convolution fusion | flops 407371776 | bytes 2883648 | tf_op jit(solution)/shard_map/rd,md->rm/dot_general | solution.py:23
  139.0 3.9 %fusion.10 = bf16[192,2048]{1,0:T(8,128)(2,1)S(1)} fusion(s32[2048]{0:T(1024)S(1)} %bitcast.32, bf16[192,1024]{1,0:T(8,128)(2,1)S(1)} %add_convert_fusion.1, bf16[192,1024]{1,0:T(8,128)(2,1)S(1)} %add_convert_fusion.2, pred[]{:T(512)S(6)} %eq.26), kind=kOutput, calls=%fused_computation.11 | convolution fusion | flops 1618739200 | bytes 1581057 | tf_op jit(solution)/shard_map/dot_general | solution.py:29
  142.9 0.8 collective-permute-start.5
  143.7 8.7 %add_convert_fusion.3 = bf16[192,1024]{1,0:T(8,128)(2,1)S(1)} fusion(f32[]{:T(128)} %bitcast.19, f32[]{:T(128)} %bitcast.18, f32[]{:T(128)} %bitcast.17, f32[]{:T(128)} %bitcast.16, f32[]{:T(128)} %bitcast.15, f32[]{:T(128)} %bitcast.14, f32[]{:T(128)} %bitcast.13, f32[]{:T(128)} %bitcast.12, f32[]{:T(128)} %bitcast.11, f32[]{:T(128)} %bitcast.10, ...), kind=kOutput, calls=%fused_computation.44 | convolution fusion | flops 407371776 | bytes 2883648 | tf_op jit(solution)/shard_map/rd,md->rm/dot_general | solution.py:23
  152.4 0.0 slice-start.3
  152.4 3.9 %fusion.11 = bf16[192,2048]{1,0:T(8,128)(2,1)S(1)} fusion(s32[2048]{0:T(1024)S(1)} %bitcast.31, bf16[192,1024]{1,0:T(8,128)(2,1)S(1)} %add_convert_fusion.3, bf16[192,1024]{1,0:T(8,128)(2,1)S(1)} %add_convert_fusion.4, pred[]{:T(512)S(6)} %eq.26), kind=kOutput, calls=%fused_computation.12 | convolution fusion | flops 1618739200 | bytes 1581057 | tf_op jit(solution)/shard_map/dot_general | solution.py:29
  156.3 0.1 collective-permute-start.3
  156.5 3.4 %fusion.2 = f32[384,2048]{1,0:T(8,128)S(1)} fusion(bf16[4096,2048]{1,0:T(8,128)(2,1)S(1)} %bitcast.34, bf16[192,2048]{1,0:T(8,128)(2,1)S(1)} %collective-permute-done.5, bf16[192,2048]{1,0:T(8,128)(2,1)S(1)} %fusion.10, pred[]{:T(512)S(6)} %eq.26), kind=kOutput, calls=%fused_computation.4 | convolution fusion | flops 3228303360 | bytes 13107201 | tf_op jit(solution)/shard_map/dot_general | solution.py:85
  159.9 4.6 %add_convert_fusion = bf16[384,2048]{1,0:T(8,128)(2,1)} fusion(f32[384,2048]{1,0:T(8,128)S(1)} %fusion.2, bf16[4096,2048]{1,0:T(8,128)(2,1)S(1)} %bitcast.34, bf16[192,2048]{1,0:T(8,128)(2,1)S(1)} %collective-permute-done.3, bf16[192,2048]{1,0:T(8,128)(2,1)S(1)} %fusion.11, pred[]{:T(512)S(6)} %eq.26), kind=kOutput, calls=%fused_computation.10 | convolution fusion | flops 3229876224 | bytes 14680065 | tf_op jit(solution)/shard_map/dot_general | solution.py:85
  (28 shorter events, 0.1 us)
Async XLA Ops:
  3.1 12.1 %copy-start.3 = (f32[4]{0:T(128)S(1)}, f32[4]{0:T(128)}, u32[]{:S(2)}) copy-start(f32[4]{0:T(128)} %param.11) | copy-start | bytes 52
  3.1 13.1 %copy-start.4 = (f32[4]{0:T(128)S(1)}, f32[4]{0:T(128)}, u32[]{:S(2)}) copy-start(f32[4]{0:T(128)} %param.12) | copy-start | bytes 52
  3.1 13.2 %copy-start.2 = (s32[2]{0:T(128)S(1)}, s32[2]{0:T(128)}, u32[]{:S(2)}) copy-start(s32[2]{0:T(128)} %param.9) | copy-start | bytes 28
  3.1 40.3 %all-to-all-start = ((bf16[64,16,1024]{2,1,0:T(8,128)(2,1)}), bf16[64,16,1024]{2,1,0:T(8,128)(2,1)S(1)}, u32[]{:S(2)}, u32[]{:S(2)}) async-start(bf16[64,16,1024]{2,1,0:T(8,128)(2,1)} %bitcast), calls=%async_computation | async-start | bytes 4194304 | tf_op jit(solution)/shard_map/all_to_all | solution.py:51
  15.2 5.4 %collective-permute-start = (f32[4]{0:T(128)S(1)}, f32[4]{0:T(128)S(1)}, u32[]{:S(2)}, u32[]{:S(2)}) collective-permute-start(f32[4]{0:T(128)S(1)} %copy-done.3), channel_id=1, source_target_pairs={{0,1},{1,0},{2,3},{3,2},{4,5},{5,4},{6,7},{7,6},{8,9},{9,8},{10,11... | collective-permute-start | bytes 56 | tf_op jit(solution)/shard_map/ppermute | solution.py:34
  16.2 4.4 %collective-permute-start.1 = (f32[4]{0:T(128)S(1)}, f32[4]{0:T(128)S(1)}, u32[]{:S(2)}, u32[]{:S(2)}) collective-permute-start(f32[4]{0:T(128)S(1)} %copy-done.4), channel_id=1, source_target_pairs={{0,1},{1,0},{2,3},{3,2},{4,5},{5,4},{6,7},{7,6},{8,9},{9,8},{10,11... | collective-permute-start | bytes 56 | tf_op jit(solution)/shard_map/ppermute | solution.py:34
  101.8 4.9 %copy-start = (bf16[384,1024]{1,0:T(8,128)(2,1)S(1)}, bf16[384,1024]{1,0:T(8,128)(2,1)}, u32[]{:S(2)}) copy-start(bf16[384,1024]{1,0:T(8,128)(2,1)} %param.7) | copy-start | bytes 2359300
  101.8 5.1 %copy-start.1 = (s32[2,2048]{1,0:T(2,128)S(1)}, s32[2,2048]{1,0:T(2,128)}, u32[]{:S(2)}) copy-start(s32[2,2048]{1,0:T(2,128)} %param.10) | copy-start | bytes 49156
  104.2 26.4 %collective-permute-start.4 = (bf16[1024,1024]{1,0:T(8,128)(2,1)}, bf16[1024,1024]{1,0:T(8,128)(2,1)}, u32[]{:S(2)}, u32[]{:S(2)}) collective-permute-start(bf16[1024,1024]{1,0:T(8,128)(2,1)} %bitcast.21), channel_id=1, source_target_pairs={{0,1},{1,0},{2,3},{3,2},{4,5},{5,4},{6,7},{7,6},{8,9},{9,8},{10,11... | collective-permute-start | bytes 6291464 | tf_op jit(solution)/shard_map/ppermute | solution.py:34
  106.9 36.8 %collective-permute-start.2 = (bf16[1024,1024]{1,0:T(8,128)(2,1)}, bf16[1024,1024]{1,0:T(8,128)(2,1)}, u32[]{:S(2)}, u32[]{:S(2)}) collective-permute-start(bf16[1024,1024]{1,0:T(8,128)(2,1)} %bitcast.5), channel_id=1, source_target_pairs={{0,1},{1,0},{2,3},{3,2},{4,5},{5,4},{6,7},{7,6},{8,9},{9,8},{10,11... | collective-permute-start | bytes 6291464 | tf_op jit(solution)/shard_map/ppermute | solution.py:34
  138.9 17.5 %slice-start = ((s8[16777216]{0:T(1024)(128)(4,1)}), s8[4194304]{0:T(1024)(128)(4,1)S(1)}, s32[]{:S(2)}) async-start(s8[16777216]{0:T(1024)(128)(4,1)} %bitcast.33), calls=%async_computation.2 | async-start | bytes 8388608
  139.0 17.5 %slice-start.1 = ((s8[16777216]{0:T(1024)(128)(4,1)}), s8[4194304]{0:T(1024)(128)(4,1)S(1)}, s32[]{:S(2)}) async-start(s8[16777216]{0:T(1024)(128)(4,1)} %bitcast.33), calls=%async_computation.3 | async-start | bytes 8388608
  142.9 13.6 %slice-start.2 = ((s8[16777216]{0:T(1024)(128)(4,1)}), s8[4194304]{0:T(1024)(128)(4,1)S(1)}, s32[]{:S(2)}) async-start(s8[16777216]{0:T(1024)(128)(4,1)} %bitcast.33), calls=%async_computation.4 | async-start | bytes 8388608
  142.9 13.5 %collective-permute-start.5 = (bf16[192,2048]{1,0:T(8,128)(2,1)S(1)}, bf16[192,2048]{1,0:T(8,128)(2,1)S(1)}, u32[]{:S(2)}, u32[]{:S(2)}) collective-permute-start(bf16[192,2048]{1,0:T(8,128)(2,1)S(1)} %fusion.10), channel_id=1, source_target_pairs={{0,1},{1,0},{2,3},{3,2},{4,5},{5,4},{6,7},{7,6},{8,9},{9,8},{10,11... | collective-permute-start | bytes 2359304 | tf_op jit(solution)/shard_map/ppermute | solution.py:34
  152.4 4.0 %slice-start.3 = ((s8[16777216]{0:T(1024)(128)(4,1)}), s8[4194304]{0:T(1024)(128)(4,1)S(1)}, s32[]{:S(2)}) async-start(s8[16777216]{0:T(1024)(128)(4,1)} %bitcast.33), calls=%async_computation.5 | async-start | bytes 8388608
  156.3 3.6 %collective-permute-start.3 = (bf16[192,2048]{1,0:T(8,128)(2,1)S(1)}, bf16[192,2048]{1,0:T(8,128)(2,1)S(1)}, u32[]{:S(2)}, u32[]{:S(2)}) collective-permute-start(bf16[192,2048]{1,0:T(8,128)(2,1)S(1)} %fusion.11), channel_id=1, source_target_pairs={{0,1},{1,0},{2,3},{3,2},{4,5},{5,4},{6,7},{7,6},{8,9},{9,8},{10,11... | collective-permute-start | bytes 2359304 | tf_op jit(solution)/shard_map/ppermute | solution.py:34

commit v12 on v10

--- a/solution.py
+++ b/solution.py
@@ -56,14 +56,19 @@
             for number in range(block_count)
         ]
     )
-    gathered = lax.all_to_all(
-        jnp.broadcast_to(kept[None], (count,) + kept.shape), SPREAD, 0, 0, tiled=True
-    )
-    arrived = [gathered[:, number].reshape(half, chosen.shape[1]) for number in range(block_count)]
+    arrived = [
+        lax.all_to_all(
+            jnp.broadcast_to(kept[number][None], (count,) + kept.shape[1:]), SPREAD, 0, 0, tiled=True
+        ).reshape(half, chosen.shape[1])
+        for number in range(block_count)
+    ]
     share = unit_rows.shape[0] // cores
     own_rows = lax.dynamic_slice_in_dim(unit_rows, core * share, share, axis=0)
     features = jnp.zeros((unit_rows.shape[0], whitening.shape[1]), jnp.float32)
-    for number, mine in enumerate(arrived):
+    for number in range(block_count):
+        mine = arrived[number]
+        if number > 0:
+            mine, features = lax.optimization_barrier((mine, features))
         other = swap_cores(mine)
         parts = [
             kernel_of(inner_products(own_rows, landmark), widths, weights).astype(jnp.bfloat16)

time: 166 us -> 160 us (0.964)
  blocking collectives: 57.9 us -> 35.1 us
  matrix products: 46.8 us -> 54.1 us
  starting transfers between devices: 16.4 us -> 23.6 us
  waiting for transfers between devices: 23.5 us -> 27.7 us
    all_to_all x1, blocking collectives: 57.9 us -> 35.1 us  [per_device(): lax.all_to_all(jnp.broadcast_to(kept[number][None], (count,) + kept.shape...]
    dot_general x2, matrix products: 8 us -> 16.4 us  [per_device(): jnp.dot(kernel, rows, preferred_element_type=jnp.float32)]
    all_to_all x0 -> x1, starting transfers between devices: none -> 6.79 us  [per_device(): lax.all_to_all(jnp.broadcast_to(kept[number][None], (count,) + kept.shape...]
    ppermute x6, waiting for transfers between devices: 0.02 us -> 4.07 us  [swap_cores(): return lax.ppermute(value, 'bw', [(0, 1), (1, 0)])]
    slice x1 -> x0, local copies, waits for them, and re-layouts: 2.39 us -> none  [per_device(): gathered[:, number].reshape(half, chosen.shape[1])]
  transfers between devices with their start and end apart: 7 -> 8, of which waited for: 1 -> 3; matrix products, arithmetic and copies ran while one was open for 30% -> 28% of each run, Pallas kernels for 0% -> 0%
where the time goes in v12:
time: 160 us; the launch traced here: 159 us
  matrix products  54.1 us (34%)
  blocking collectives  35.1 us (22%)
  waiting for transfers between devices  27.7 us (17%)
  starting transfers between devices  23.6 us (15%)
  between operations  8.94 us (6%)
  other arithmetic  6.09 us (4%)
  local copies, waits for them, and re-layouts  3.39 us (2%)
    all_to_all x1, blocking collectives, per_device(): lax.all_to_all(jnp.broadcast_to(kept[number][None], (count,) + kept.shape...  35.1 us
    dot_general x4, matrix products, inner_products(): jnp.einsum('rd,md->rm', unit_rows, landmark, preferred_element_type=jnp.f...  29.9 us
    all_to_all x1, waiting for transfers between devices, per_device(): spread = lax.all_to_all(pieces, SPREAD, 0, 0, tiled=True)  23.6 us
    dot_general x2, matrix products, per_device(): jnp.dot(kernel, rows, preferred_element_type=jnp.float32)  16.4 us
    all_to_all x1, starting transfers between devices, per_device(): spread = lax.all_to_all(pieces, SPREAD, 0, 0, tiled=True)  11.4 us
    dot_general x2, matrix products, reorder_columns(): ordered = jnp.dot(kernel, onehot, preferred_element_type=jnp.float32)  7.79 us
    all_to_all x1, starting transfers between devices, per_device(): lax.all_to_all(jnp.broadcast_to(kept[number][None], (count,) + kept.shape...  6.79 us
    ppermute x6, starting transfers between devices, swap_cores(): return lax.ppermute(value, 'bw', [(0, 1), (1, 0)])  5.47 us
  transfers between devices with their start and end apart: 8, of which 3 were waited for; matrix products, arithmetic and copies ran while one was open for 28% of the time, Pallas kernels for 0%

profile of v12, /device:TPU:1, one launch (start us, length us, event | category | flops | bytes accessed | tf_op | source)
XLA Modules:
  0.0 158.9 jit_solution(8008134539386341991)
XLA Ops:
  0.0 1.4 collective-permute-start
  1.4 2.1 %fusion.8 = f32[1024]{0:T(1024)S(1)} fusion(bf16[2048,1024]{1,0:T(8,128)(2,1)} %param.8, s32[]{:T(128)S(6)} %select_n.37), kind=kLoop, calls=%fused_computation.12 | loop fusion | flops 3144704 | bytes 2101252 | tf_op jit(solution)/shard_map/reduce_sum | solution.py:11
  3.5 3.3 %fusion.9 = bf16[1024,1024]{1,0:T(8,128)(2,1)} fusion(f32[1024]{0:T(1024)S(1)} %add_rsqrt_fusion, bf16[2048,1024]{1,0:T(8,128)(2,1)} %param.8, s32[]{:T(128)S(6)} %select_n.37), kind=kLoop, calls=%fused_computation.13 | loop fusion | flops 3145728 | bytes 4198404 | tf_op jit(solution)/shard_map/convert_element_type | solution.py:12
  6.8 0.1 pad_maximum_fusion
  6.9 0.1 pad_maximum_fusion.1
  7.0 11.4 %all-to-all-start = ((bf16[64,16,1024]{2,1,0:T(8,128)(2,1)}), bf16[64,16,1024]{2,1,0:T(8,128)(2,1)S(1)}, u32[]{:S(2)}, u32[]{:S(2)}) async-start(bf16[64,16,1024]{2,1,0:T(8,128)(2,1)} %bitcast), calls=%async_computation | async-start | bytes 4194304 | tf_op jit(solution)/shard_map/all_to_all | solution.py:52
  18.4 0.6 fusion.46
  22.8 23.6 %all-to-all-done = bf16[64,16,1024]{2,1,0:T(8,128)(2,1)S(1)} async-done(((bf16[64,16,1024]{2,1,0:T(8,128)(2,1)}), bf16[64,16,1024]{2,1,0:T(8,128)(2,1)S(1)}, u32[]{:S(2)}, u32[]{:S(2)}) %all-to-all-start) | async-done | bytes 2097184 | tf_op jit(solution)/shard_map/all_to_all | solution.py:52
  46.4 0.3 broadcast_in_dim.19
  46.6 35.1 %all_to_all.15 = bf16[64,16,1024]{2,1,0:T(8,128)(2,1)} all-to-all(bf16[64,16,1024]{2,1,0:T(8,128)(2,1)S(1)} %broadcast_in_dim.19), channel_id=1, replica_groups=mesh['row'=8,'lmk'=8,'bw'=2] {'row','lmk'}, dimensions={0} | all-to-all | bytes 4194304 | tf_op jit(solution)/shard_map/all_to_all | solution.py:60
  81.7 3.1 %collective-permute-start.2 = (bf16[1024,1024]{1,0:T(8,128)(2,1)}, bf16[1024,1024]{1,0:T(8,128)(2,1)}, u32[]{:S(2)}, u32[]{:S(2)}) collective-permute-start(bf16[1024,1024]{1,0:T(8,128)(2,1)} %bitcast.8), channel_id=1, source_target_pairs={{0,1},{1,0},{2,3},{3,2},{4,5},{5,4},{6,7},{7,6},{8,9},{9,8},{10,11... | collective-permute-start | bytes 6291464 | tf_op jit(solution)/shard_map/ppermute | solution.py:34
  84.8 0.2 convert_element_type.37
  85.0 0.2 multiply_reduce_fusion
  85.3 0.1 dynamic-slice
  85.3 0.1 fusion.26
  85.5 0.1 copy-done.1
  85.6 0.7 fusion.44
  91.3 1.6 %broadcast_in_dim.17 = bf16[64,16,1024]{2,1,0:T(8,128)(2,1)} broadcast(bf16[16,1024]{1,0:T(8,128)(2,1)S(1)} %get-tuple-element.16), dimensions={1,2} | broadcast | bytes 2129920 | tf_op jit(solution)/shard_map/broadcast_in_dim | solution.py:61
  92.9 6.8 %all-to-all-start.1 = ((bf16[64,16,1024]{2,1,0:T(8,128)(2,1)}), bf16[64,16,1024]{2,1,0:T(8,128)(2,1)S(1)}, u32[]{:S(2)}, u32[]{:S(2)}) async-start(bf16[64,16,1024]{2,1,0:T(8,128)(2,1)} %broadcast_in_dim.17), calls=%async_computation.1 | async-start | bytes 4194304 | tf_op jit(solution)/shard_map/all_to_all | solution.py:60
  99.7 8.3 %add_convert_fusion.4 = bf16[192,1024]{1,0:T(8,128)(2,1)S(1)} fusion(f32[]{:T(128)} %bitcast.22, f32[]{:T(128)} %bitcast.21, f32[]{:T(128)} %bitcast.20, f32[]{:T(128)} %bitcast.19, f32[]{:T(128)} %bitcast.18, f32[]{:T(128)} %bitcast.17, f32[]{:T(128)} %bitcast.16, f32[]{:T(128)} %bitcast.15, f32[]{:T(128)} %bitcast.14, f32[]{:T(128)} %bitcast.13, ...), kind=kOutput, calls=%fused_computation.49 | convolution fusion | flops 407371776 | bytes 2883648 | tf_op jit(solution)/shard_map/rd,md->rm/dot_general | solution.py:23
  108.0 8.3 %add_convert_fusion.3 = bf16[192,1024]{1,0:T(8,128)(2,1)S(1)} fusion(f32[]{:T(128)} %bitcast.22, f32[]{:T(128)} %bitcast.21, f32[]{:T(128)} %bitcast.20, f32[]{:T(128)} %bitcast.19, f32[]{:T(128)} %bitcast.18, f32[]{:T(128)} %bitcast.17, f32[]{:T(128)} %bitcast.16, f32[]{:T(128)} %bitcast.15, f32[]{:T(128)} %bitcast.14, f32[]{:T(128)} %bitcast.13, ...), kind=kOutput, calls=%fused_computation.48 | convolution fusion | flops 407371776 | bytes 2883648 | tf_op jit(solution)/shard_map/rd,md->rm/dot_general | solution.py:23
  116.3 3.9 %fusion.13 = bf16[192,2048]{1,0:T(8,128)(2,1)S(1)} fusion(s32[2048]{0:T(1024)S(1)} %bitcast.38, bf16[192,1024]{1,0:T(8,128)(2,1)S(1)} %add_convert_fusion.3, bf16[192,1024]{1,0:T(8,128)(2,1)S(1)} %add_convert_fusion.4, pred[]{:T(512)S(6)} %eq.26), kind=kOutput, calls=%fused_computation.16 | convolution fusion | flops 1618739200 | bytes 1581057 | tf_op jit(solution)/shard_map/dot_general | solution.py:29
  120.2 0.4 collective-permute-start.3
  120.5 2.0 %collective-permute-done.3 = bf16[192,2048]{1,0:T(8,128)(2,1)S(1)} collective-permute-done((bf16[192,2048]{1,0:T(8,128)(2,1)S(1)}, bf16[192,2048]{1,0:T(8,128)(2,1)S(1)}, u32[]{:S(2)}, u32[]{:S(2)}) %collective-permute-start.3) | collective-permute-done | bytes 786464 | tf_op jit(solution)/shard_map/ppermute | solution.py:34
  122.6 8.5 %fusion.5 = f32[384,2048]{1,0:T(8,128)} fusion(bf16[4096,2048]{1,0:T(8,128)(2,1)} %param.13, bf16[192,2048]{1,0:T(8,128)(2,1)S(1)} %collective-permute-done.3, bf16[192,2048]{1,0:T(8,128)(2,1)S(1)} %fusion.13, pred[]{:T(512)S(6)} %eq.26), kind=kOutput, calls=%fused_computation.7 | convolution fusion | flops 3228303360 | bytes 13107201 | tf_op jit(solution)/shard_map/dot_general | solution.py:90
  131.0 0.3 collective-permute-start.4
  131.3 6.7 %add_convert_fusion.2 = bf16[192,1024]{1,0:T(8,128)(2,1)S(1)} fusion(f32[]{:T(128)} %bitcast.22, f32[]{:T(128)} %bitcast.21, f32[]{:T(128)} %bitcast.20, f32[]{:T(128)} %bitcast.19, f32[]{:T(128)} %bitcast.18, f32[]{:T(128)} %bitcast.17, f32[]{:T(128)} %bitcast.16, f32[]{:T(128)} %bitcast.15, f32[]{:T(128)} %bitcast.14, f32[]{:T(128)} %bitcast.13, ...), kind=kOutput, calls=%fused_computation.47 | convolution fusion | flops 407371776 | bytes 2883648 | tf_op jit(solution)/shard_map/rd,md->rm/dot_general | solution.py:23
  138.0 6.7 %add_convert_fusion.1 = bf16[192,1024]{1,0:T(8,128)(2,1)S(1)} fusion(f32[]{:T(128)} %bitcast.22, f32[]{:T(128)} %bitcast.21, f32[]{:T(128)} %bitcast.20, f32[]{:T(128)} %bitcast.19, f32[]{:T(128)} %bitcast.18, f32[]{:T(128)} %bitcast.17, f32[]{:T(128)} %bitcast.16, f32[]{:T(128)} %bitcast.15, f32[]{:T(128)} %bitcast.14, f32[]{:T(128)} %bitcast.13, ...), kind=kOutput, calls=%fused_computation.46 | convolution fusion | flops 407371776 | bytes 2883648 | tf_op jit(solution)/shard_map/rd,md->rm/dot_general | solution.py:23
  144.7 3.9 %fusion.12 = bf16[192,2048]{1,0:T(8,128)(2,1)S(1)} fusion(s32[2048]{0:T(1024)S(1)} %bitcast.37, bf16[192,1024]{1,0:T(8,128)(2,1)S(1)} %add_convert_fusion.1, bf16[192,1024]{1,0:T(8,128)(2,1)S(1)} %add_convert_fusion.2, pred[]{:T(512)S(6)} %eq.26), kind=kOutput, calls=%fused_computation.15 | convolution fusion | flops 1618739200 | bytes 1581057 | tf_op jit(solution)/shard_map/dot_general | solution.py:29
  148.5 0.3 collective-permute-start.5
  148.9 2.0 %collective-permute-done.5 = bf16[192,2048]{1,0:T(8,128)(2,1)S(1)} collective-permute-done((bf16[192,2048]{1,0:T(8,128)(2,1)S(1)}, bf16[192,2048]{1,0:T(8,128)(2,1)S(1)}, u32[]{:S(2)}, u32[]{:S(2)}) %collective-permute-start.5) | collective-permute-done | bytes 786464 | tf_op jit(solution)/shard_map/ppermute | solution.py:34
  150.9 7.9 %add_convert_fusion = bf16[384,2048]{1,0:T(8,128)(2,1)} fusion(f32[384,2048]{1,0:T(8,128)S(1)} %copy-done.5, bf16[4096,2048]{1,0:T(8,128)(2,1)} %param.13, bf16[192,2048]{1,0:T(8,128)(2,1)S(1)} %collective-permute-done.5, bf16[192,2048]{1,0:T(8,128)(2,1)S(1)} %fusion.12, pred[]{:T(512)S(6)} %eq.26), kind=kOutput, calls=%fused_computation.14 | convolution fusion | flops 3229876224 | bytes 14680065 | tf_op jit(solution)/shard_map/dot_general | solution.py:90
  (21 shorter events, 0.1 us)
Async XLA Ops:
  0.0 6.8 %collective-permute-start = (f32[4]{0:T(128)}, f32[4]{0:T(128)S(1)}, u32[]{:S(2)}, u32[]{:S(2)}) collective-permute-start(f32[4]{0:T(128)} %param.11), channel_id=1, source_target_pairs={{0,1},{1,0},{2,3},{3,2},{4,5},{5,4},{6,7},{7,6},{8,9},{9,8},{10,11... | collective-permute-start | bytes 56 | tf_op jit(solution)/shard_map/ppermute | solution.py:34
  1.4 5.5 %collective-permute-start.1 = (f32[4]{0:T(128)}, f32[4]{0:T(128)S(1)}, u32[]{:S(2)}, u32[]{:S(2)}) collective-permute-start(f32[4]{0:T(128)} %param.12), channel_id=1, source_target_pairs={{0,1},{1,0},{2,3},{3,2},{4,5},{5,4},{6,7},{7,6},{8,9},{9,8},{10,11... | collective-permute-start | bytes 56 | tf_op jit(solution)/shard_map/ppermute | solution.py:34
  3.5 3.4 %copy-start.3 = (f32[4]{0:T(128)S(1)}, f32[4]{0:T(128)}, u32[]{:S(2)}) copy-start(f32[4]{0:T(128)} %param.11) | copy-start | bytes 52
  3.5 3.4 %copy-start.4 = (f32[4]{0:T(128)S(1)}, f32[4]{0:T(128)}, u32[]{:S(2)}) copy-start(f32[4]{0:T(128)} %param.12) | copy-start | bytes 52
  7.0 11.4 %copy-start.2 = (s32[2]{0:T(128)S(1)}, s32[2]{0:T(128)}, u32[]{:S(2)}) copy-start(s32[2]{0:T(128)} %param.9) | copy-start | bytes 28
  7.0 39.4 %all-to-all-start = ((bf16[64,16,1024]{2,1,0:T(8,128)(2,1)}), bf16[64,16,1024]{2,1,0:T(8,128)(2,1)S(1)}, u32[]{:S(2)}, u32[]{:S(2)}) async-start(bf16[64,16,1024]{2,1,0:T(8,128)(2,1)} %bitcast), calls=%async_computation | async-start | bytes 4194304 | tf_op jit(solution)/shard_map/all_to_all | solution.py:52
  46.6 38.2 %copy-start = (bf16[384,1024]{1,0:T(8,128)(2,1)S(1)}, bf16[384,1024]{1,0:T(8,128)(2,1)}, u32[]{:S(2)}) copy-start(bf16[384,1024]{1,0:T(8,128)(2,1)} %param.7) | copy-start | bytes 2359300
  81.7 26.3 %collective-permute-start.2 = (bf16[1024,1024]{1,0:T(8,128)(2,1)}, bf16[1024,1024]{1,0:T(8,128)(2,1)}, u32[]{:S(2)}, u32[]{:S(2)}) collective-permute-start(bf16[1024,1024]{1,0:T(8,128)(2,1)} %bitcast.8), channel_id=1, source_target_pairs={{0,1},{1,0},{2,3},{3,2},{4,5},{5,4},{6,7},{7,6},{8,9},{9,8},{10,11... | collective-permute-start | bytes 6291464 | tf_op jit(solution)/shard_map/ppermute | solution.py:34
  84.8 0.7 copy-start.1
  92.9 38.1 %all-to-all-start.1 = ((bf16[64,16,1024]{2,1,0:T(8,128)(2,1)}), bf16[64,16,1024]{2,1,0:T(8,128)(2,1)S(1)}, u32[]{:S(2)}, u32[]{:S(2)}) async-start(bf16[64,16,1024]{2,1,0:T(8,128)(2,1)} %broadcast_in_dim.17), calls=%async_computation.1 | async-start | bytes 4194304 | tf_op jit(solution)/shard_map/all_to_all | solution.py:60
  120.2 2.4 %collective-permute-start.3 = (bf16[192,2048]{1,0:T(8,128)(2,1)S(1)}, bf16[192,2048]{1,0:T(8,128)(2,1)S(1)}, u32[]{:S(2)}, u32[]{:S(2)}) collective-permute-start(bf16[192,2048]{1,0:T(8,128)(2,1)S(1)} %fusion.13), channel_id=1, source_target_pairs={{0,1},{1,0},{2,3},{3,2},{4,5},{5,4},{6,7},{7,6},{8,9},{9,8},{10,11... | collective-permute-start | bytes 2359304 | tf_op jit(solution)/shard_map/ppermute | solution.py:34
  131.0 6.9 %collective-permute-start.4 = (bf16[1024,1024]{1,0:T(8,128)(2,1)S(1)}, bf16[1024,1024]{1,0:T(8,128)(2,1)S(1)}, u32[]{:S(2)}, u32[]{:S(2)}) collective-permute-start(bf16[1024,1024]{1,0:T(8,128)(2,1)S(1)} %bitcast.35), channel_id=1, source_target_pairs={{0,1},{1,0},{2,3},{3,2},{4,5},{5,4},{6,7},{7,6},{8,9},{9,8},{10,11... | collective-permute-start | bytes 6291464 | tf_op jit(solution)/shard_map/ppermute | solution.py:34
  144.6 6.3 %copy-start.5 = (f32[384,2048]{1,0:T(8,128)S(1)}, f32[384,2048]{1,0:T(8,128)}, u32[]{:S(2)}) copy-start(f32[384,2048]{1,0:T(8,128)} %fusion.5) | copy-start | bytes 9437188
  148.5 2.4 %collective-permute-start.5 = (bf16[192,2048]{1,0:T(8,128)(2,1)S(1)}, bf16[192,2048]{1,0:T(8,128)(2,1)S(1)}, u32[]{:S(2)}, u32[]{:S(2)}) collective-permute-start(bf16[192,2048]{1,0:T(8,128)(2,1)S(1)} %fusion.12), channel_id=1, source_target_pairs={{0,1},{1,0},{2,3},{3,2},{4,5},{5,4},{6,7},{7,6},{8,9},{9,8},{10,11... | collective-permute-start | bytes 2359304 | tf_op jit(solution)/shard_map/ppermute | solution.py:34

commit v13 on v10

--- a/solution.py
+++ b/solution.py
@@ -23,11 +23,9 @@
     return jnp.einsum("rd,md->rm", unit_rows, landmark, preferred_element_type=jnp.float32)
 
 
-def reorder_columns(kernel, picks):
-    natural = lax.broadcasted_iota(jnp.int32, (kernel.shape[1], picks.shape[0]), 0)
-    onehot = (picks[None, :] == natural).astype(kernel.dtype)
-    ordered = jnp.dot(kernel, onehot, preferred_element_type=jnp.float32)
-    return ordered.astype(kernel.dtype)
+def reorder_columns(kernel, natural, picks):
+    onehot = (picks[None, :] == natural[:, None]).astype(kernel.dtype)
+    return jnp.dot(kernel, onehot, preferred_element_type=jnp.float32)
 
 
 def swap_cores(value):
@@ -56,33 +54,51 @@
             for number in range(block_count)
         ]
     )
-    gathered = lax.all_to_all(
-        jnp.broadcast_to(kept[None], (count,) + kept.shape), SPREAD, 0, 0, tiled=True
-    )
-    arrived = [gathered[:, number].reshape(half, chosen.shape[1]) for number in range(block_count)]
+    piece_rows = half // count
+    splits = 2
+    part = piece_rows // splits
     share = unit_rows.shape[0] // cores
     own_rows = lax.dynamic_slice_in_dim(unit_rows, core * share, share, axis=0)
+
+    def natural_rows(which, chunk):
+        piece = lax.broadcasted_iota(jnp.int32, (count, part), 0)
+        inner = lax.broadcasted_iota(jnp.int32, (count, part), 1)
+        return (which * half + piece * piece_rows + chunk * part + inner).reshape(-1)
+
+    units = [(number, chunk) for number in range(block_count) for chunk in range(splits)]
+    gathered = [
+        lax.all_to_all(
+            jnp.broadcast_to(
+                kept[number, chunk * part:(chunk + 1) * part][None], (count, part, kept.shape[2])
+            ),
+            SPREAD, 0, 0, tiled=True,
+        ).reshape(count * part, kept.shape[2])
+        for number, chunk in units
+    ]
     features = jnp.zeros((unit_rows.shape[0], whitening.shape[1]), jnp.float32)
-    for number, mine in enumerate(arrived):
+    ordered = jnp.zeros((share, block_rows), jnp.float32)
+    for step, (number, chunk) in enumerate(units):
+        mine = gathered[step]
+        if step > 0:
+            mine, features, ordered = lax.optimization_barrier((mine, features, ordered))
         other = swap_cores(mine)
-        parts = [
-            kernel_of(inner_products(own_rows, landmark), widths, weights).astype(jnp.bfloat16)
-            for landmark in (mine, other)
-        ]
-        own_kernel = jnp.where(
-            core == 0,
-            jnp.concatenate(parts, axis=1),
-            jnp.concatenate(parts[::-1], axis=1),
-        )
-        own_kernel = reorder_columns(own_kernel, landmark_picks[number])
-        other_kernel = swap_cores(own_kernel)
-        kernel = jnp.where(
-            core == 0,
-            jnp.concatenate([own_kernel, other_kernel], axis=0),
-            jnp.concatenate([other_kernel, own_kernel], axis=0),
-        )
-        rows = lax.dynamic_slice_in_dim(whitening, number * block_rows, block_rows, axis=0)
-        features = features + jnp.dot(kernel, rows, preferred_element_type=jnp.float32)
+        kernel = kernel_of(
+            inner_products(own_rows, jnp.concatenate([mine, other], axis=0)), widths, weights
+        ).astype(jnp.bfloat16)
+        kernel = lax.optimization_barrier(kernel)
+        natural = jnp.concatenate([natural_rows(core, chunk), natural_rows(1 - core, chunk)])
+        ordered = ordered + reorder_columns(kernel, natural, landmark_picks[number])
+        if chunk == splits - 1:
+            own_kernel = ordered.astype(jnp.bfloat16)
+            other_kernel = swap_cores(own_kernel)
+            kernel = jnp.where(
+                core == 0,
+                jnp.concatenate([own_kernel, other_kernel], axis=0),
+                jnp.concatenate([other_kernel, own_kernel], axis=0),
+            )
+            rows = lax.dynamic_slice_in_dim(whitening, number * block_rows, block_rows, axis=0)
+            features = features + jnp.dot(kernel, rows, preferred_element_type=jnp.float32)
+            ordered = jnp.zeros((share, block_rows), jnp.float32)
     return features.astype(jnp.bfloat16)
 
 

time: 166 us -> 190 us (1.14)
  blocking collectives: 57.9 us -> 0 us
  waiting for transfers between devices: 23.5 us -> 60.7 us
  starting transfers between devices: 16.4 us -> 48.9 us
  matrix products: 46.8 us -> 56 us
  local copies, waits for them, and re-layouts: 4.41 us -> 7.63 us
    all_to_all x1 -> x0, blocking collectives: 57.9 us -> none  [per_device(): lax.all_to_all(jnp.broadcast_to(kept[None], (count,) + kept.shape), SPREA...]
    all_to_all x0 -> x4, waiting for transfers between devices: none -> 31 us  [per_device(): lax.all_to_all(jnp.broadcast_to(kept[number, chunk * part:(chunk + 1) * p...]
    all_to_all x0 -> x4, starting transfers between devices: none -> 25.7 us  [per_device(): lax.all_to_all(jnp.broadcast_to(kept[number, chunk * part:(chunk + 1) * p...]
    dot_general x2, matrix products: 8 us -> 16.4 us  [per_device(): jnp.dot(kernel, rows, preferred_element_type=jnp.float32)]
    ppermute x6 -> x8, starting transfers between devices: 5.01 us -> 11.6 us  [swap_cores(): return lax.ppermute(value, 'bw', [(0, 1), (1, 0)])]
    ppermute x6 -> x8, waiting for transfers between devices: 0.02 us -> 6.35 us  [swap_cores(): return lax.ppermute(value, 'bw', [(0, 1), (1, 0)])]
    broadcast_in_dim x1 -> x7, local copies, waits for them, and re-layouts: 0.52 us -> 5.74 us  [the longest x5 5.22 us: per_device(): jnp.broadcast_to(kept[number, chunk * part:(chunk + 1) * part][None], (co...]
    slice x2 -> x1, local copies, waits for them, and re-layouts: 2.4 us -> 0.01 us  [per_device(): ordered = ordered + reorder_columns(kernel, natural, landmark_picks[number])]
  transfers between devices with their start and end apart: 7 -> 13, of which waited for: 1 -> 8; matrix products, arithmetic and copies ran while one was open for 30% -> 22% of each run, Pallas kernels for 0% -> 0%
where the time goes in v13:
time: 190 us; the launch traced here: 189 us
  waiting for transfers between devices  60.7 us (32%)
  matrix products  56 us (29%)
  starting transfers between devices  48.9 us (26%)
  between operations  9.19 us (5%)
  local copies, waits for them, and re-layouts  7.63 us (4%)
  other arithmetic  6.37 us (3%)
    all_to_all x4, waiting for transfers between devices, per_device(): lax.all_to_all(jnp.broadcast_to(kept[number, chunk * part:(chunk + 1) * p...  31 us
    dot_general x4, matrix products, inner_products(): jnp.einsum('rd,md->rm', unit_rows, landmark, preferred_element_type=jnp.f...  30.3 us
    all_to_all x4, starting transfers between devices, per_device(): lax.all_to_all(jnp.broadcast_to(kept[number, chunk * part:(chunk + 1) * p...  25.7 us
    all_to_all x1, waiting for transfers between devices, per_device(): spread = lax.all_to_all(pieces, SPREAD, 0, 0, tiled=True)  23.3 us
    dot_general x2, matrix products, per_device(): jnp.dot(kernel, rows, preferred_element_type=jnp.float32)  16.4 us
    all_to_all x1, starting transfers between devices, per_device(): spread = lax.all_to_all(pieces, SPREAD, 0, 0, tiled=True)  11.6 us
    ppermute x8, starting transfers between devices, swap_cores(): return lax.ppermute(value, 'bw', [(0, 1), (1, 0)])  11.6 us
    dot_general x4, matrix products, reorder_columns(): return jnp.dot(kernel, onehot, preferred_element_type=jnp.float32)  9.29 us
  transfers between devices with their start and end apart: 13, of which 8 were waited for; matrix products, arithmetic and copies ran while one was open for 22% of the time, Pallas kernels for 0%

profile of v13, /device:TPU:1, one launch (start us, length us, event | category | flops | bytes accessed | tf_op | source)
XLA Modules:
  0.0 188.8 jit_solution(5523604889423176860)
XLA Ops:
  0.0 1.4 collective-permute-start
  1.4 2.1 %fusion.12 = f32[1024]{0:T(1024)S(1)} fusion(bf16[2048,1024]{1,0:T(8,128)(2,1)} %param.8, s32[]{:T(128)S(6)} %select_n.25), kind=kLoop, calls=%fused_computation.14 | loop fusion | flops 3144704 | bytes 2101252 | tf_op jit(solution)/shard_map/reduce_sum | solution.py:11
  3.5 3.3 %fusion.13 = bf16[1024,1024]{1,0:T(8,128)(2,1)} fusion(f32[1024]{0:T(1024)S(1)} %add_rsqrt_fusion, bf16[2048,1024]{1,0:T(8,128)(2,1)} %param.8, s32[]{:T(128)S(6)} %select_n.25), kind=kLoop, calls=%fused_computation.15 | loop fusion | flops 3145728 | bytes 4198404 | tf_op jit(solution)/shard_map/convert_element_type | solution.py:12
  7.0 11.6 %all-to-all-start = ((bf16[64,16,1024]{2,1,0:T(8,128)(2,1)}), bf16[64,16,1024]{2,1,0:T(8,128)(2,1)}, u32[]{:S(2)}, u32[]{:S(2)}) async-start(bf16[64,16,1024]{2,1,0:T(8,128)(2,1)} %bitcast), calls=%async_computation | async-start | bytes 4194304 | tf_op jit(solution)/shard_map/all_to_all | solution.py:50
  23.1 23.3 %all-to-all-done = bf16[64,16,1024]{2,1,0:T(8,128)(2,1)} async-done(((bf16[64,16,1024]{2,1,0:T(8,128)(2,1)}), bf16[64,16,1024]{2,1,0:T(8,128)(2,1)}, u32[]{:S(2)}, u32[]{:S(2)}) %all-to-all-start) | async-done | bytes 2097184 | tf_op jit(solution)/shard_map/all_to_all | solution.py:50
  47.2 1.1 broadcast_in_dim.48
  48.3 7.3 %all-to-all-start.4 = ((bf16[64,8,1024]{2,1,0:T(8,128)(2,1)}), bf16[64,8,1024]{2,1,0:T(8,128)(2,1)S(1)}, u32[]{:S(2)}, u32[]{:S(2)}) async-start(bf16[64,8,1024]{2,1,0:T(8,128)(2,1)} %broadcast_in_dim.48), calls=%async_computation.4 | async-start | bytes 2097152 | tf_op jit(solution)/shard_map/all_to_all | solution.py:70
  56.3 15.7 %all-to-all-done.4 = bf16[64,8,1024]{2,1,0:T(8,128)(2,1)S(1)} async-done(((bf16[64,8,1024]{2,1,0:T(8,128)(2,1)}), bf16[64,8,1024]{2,1,0:T(8,128)(2,1)S(1)}, u32[]{:S(2)}, u32[]{:S(2)}) %all-to-all-start.4) | async-done | bytes 1048608 | tf_op jit(solution)/shard_map/all_to_all | solution.py:70
  71.9 3.2 %collective-permute-start.2 = (bf16[512,1024]{1,0:T(8,128)(2,1)S(1)}, bf16[512,1024]{1,0:T(8,128)(2,1)}, u32[]{:S(2)}, u32[]{:S(2)}) collective-permute-start(bf16[512,1024]{1,0:T(8,128)(2,1)S(1)} %bitcast.41), channel_id=1, source_target_pairs={{0,1},{1,0},{2,3},{3,2},{4,5},{5,4},{6,7},{7,6},{8,9},{9,8},{10,11... | collective-permute-start | bytes 3145736 | tf_op jit(solution)/shard_map/ppermute | solution.py:32
  75.2 1.1 broadcast_in_dim.45
  76.3 5.5 %all-to-all-start.3 = ((bf16[64,8,1024]{2,1,0:T(8,128)(2,1)}), bf16[64,8,1024]{2,1,0:T(8,128)(2,1)}, u32[]{:S(2)}, u32[]{:S(2)}) async-start(bf16[64,8,1024]{2,1,0:T(8,128)(2,1)} %broadcast_in_dim.45), calls=%async_computation.3 | async-start | bytes 2097152 | tf_op jit(solution)/shard_map/all_to_all | solution.py:70
  88.0 7.9 %add_convert_fusion.4 = bf16[192,1024]{1,0:T(8,128)(2,1)S(1)} fusion(bf16[192,1024]{1,0:T(8,128)(2,1)S(1)} %fusion.70, bf16[512,1024]{1,0:T(8,128)(2,1)} %collective-permute-done.2, bf16[512,1024]{1,0:T(8,128)(2,1)S(1)} %bitcast.42, f32[]{:T(128)} %bitcast.26, f32[]{:T(128)} %bitcast.25, f32[]{:T(128)} %bitcast.24, f32[]{:T(128)} %bitcast.23, f32[]{:T(128)} %bitcast.22, ...), kind=kOutput, calls=%fused_computation.67 | convolution fusion | flops 411566080 | bytes 2883648 | tf_op jit(solution)/shard_map/rd,md->rm/dot_general | solution.py:23
  95.9 2.8 %fusion.10 = f32[192,2048]{1,0:T(8,128)} fusion(bf16[192,1024]{1,0:T(8,128)(2,1)S(1)} %add_convert_fusion.4, s32[2048]{0:T(1024)S(1)} %bitcast.49, s32[1024]{0:T(1024)S(1)} %pad_add_fusion), kind=kOutput, calls=%fused_computation.10 | convolution fusion | flops 807403520 | bytes 1978368 | tf_op jit(solution)/shard_map/dot_general | solution.py:28
  99.4 1.6 collective-permute-start.3
  101.3 2.1 %collective-permute-done.3 = bf16[512,1024]{1,0:T(8,128)(2,1)S(1)} collective-permute-done((bf16[512,1024]{1,0:T(8,128)(2,1)}, bf16[512,1024]{1,0:T(8,128)(2,1)S(1)}, u32[]{:S(2)}, u32[]{:S(2)}) %collective-permute-start.3) | collective-permute-done | bytes 1048608 | tf_op jit(solution)/shard_map/ppermute | solution.py:32
  103.5 7.9 %add_convert_fusion.3 = bf16[192,1024]{1,0:T(8,128)(2,1)S(1)} fusion(bf16[192,1024]{1,0:T(8,128)(2,1)S(1)} %fusion.70, bf16[512,1024]{1,0:T(8,128)(2,1)S(1)} %collective-permute-done.3, bf16[512,1024]{1,0:T(8,128)(2,1)} %bitcast.8, f32[]{:T(128)} %bitcast.26, f32[]{:T(128)} %bitcast.25, f32[]{:T(128)} %bitcast.24, f32[]{:T(128)} %bitcast.23, f32[]{:T(128)} %bitcast.22, ...), kind=kOutput, calls=%fused_computation.66 | convolution fusion | flops 411566080 | bytes 2883648 | tf_op jit(solution)/shard_map/rd,md->rm/dot_general | solution.py:23
  111.4 1.8 fusion.39
  114.7 7.8 %all-to-all-start.2 = ((bf16[64,8,1024]{2,1,0:T(8,128)(2,1)}), bf16[64,8,1024]{2,1,0:T(8,128)(2,1)S(1)}, u32[]{:S(2)}, u32[]{:S(2)}) async-start(bf16[64,8,1024]{2,1,0:T(8,128)(2,1)} %broadcast_in_dim.43), calls=%async_computation.2 | async-start | bytes 2097152 | tf_op jit(solution)/shard_map/all_to_all | solution.py:70
  122.9 8.4 %fusion.22 = f32[384,2048]{1,0:T(8,128)} fusion(f32[384,2048]{1,0:T(8,128)S(1)} %broadcast_in_dim.46, bf16[4096,2048]{1,0:T(8,128)(2,1)} %param.13, bf16[192,2048]{1,0:T(8,128)(2,1)S(1)} %collective-permute-done.4, bf16[192,2048]{1,0:T(8,128)(2,1)S(1)} %fusion.39, pred[]{:T(512)S(6)} %eq.26), kind=kOutput, calls=%fused_computation.25 | convolution fusion | flops 3229089792 | bytes 16252929 | tf_op jit(solution)/shard_map/dot_general | solution.py:100
  131.4 8.3 %all-to-all-done.2 = bf16[64,8,1024]{2,1,0:T(8,128)(2,1)S(1)} async-done(((bf16[64,8,1024]{2,1,0:T(8,128)(2,1)}), bf16[64,8,1024]{2,1,0:T(8,128)(2,1)S(1)}, u32[]{:S(2)}, u32[]{:S(2)}) %all-to-all-start.2) | async-done | bytes 1048608 | tf_op jit(solution)/shard_map/all_to_all | solution.py:70
  139.6 2.4 %collective-permute-start.5 = (bf16[512,1024]{1,0:T(8,128)(2,1)S(1)}, bf16[512,1024]{1,0:T(8,128)(2,1)}, u32[]{:S(2)}, u32[]{:S(2)}) collective-permute-start(bf16[512,1024]{1,0:T(8,128)(2,1)S(1)} %bitcast.45), channel_id=1, source_target_pairs={{0,1},{1,0},{2,3},{3,2},{4,5},{5,4},{6,7},{7,6},{8,9},{9,8},{10,11... | collective-permute-start | bytes 3145736 | tf_op jit(solution)/shard_map/ppermute | solution.py:32
  142.0 1.1 broadcast_in_dim.41
  143.2 5.0 %all-to-all-start.1 = ((bf16[64,8,1024]{2,1,0:T(8,128)(2,1)}), bf16[64,8,1024]{2,1,0:T(8,128)(2,1)S(1)}, u32[]{:S(2)}, u32[]{:S(2)}) async-start(bf16[64,8,1024]{2,1,0:T(8,128)(2,1)} %broadcast_in_dim.41), calls=%async_computation.1 | async-start | bytes 2097152 | tf_op jit(solution)/shard_map/all_to_all | solution.py:70
  148.3 7.9 %add_convert_fusion.2 = bf16[192,1024]{1,0:T(8,128)(2,1)S(1)} fusion(bf16[192,1024]{1,0:T(8,128)(2,1)S(1)} %copy-done.2, bf16[512,1024]{1,0:T(8,128)(2,1)} %collective-permute-done.5, bf16[512,1024]{1,0:T(8,128)(2,1)S(1)} %bitcast.46, f32[]{:T(128)} %bitcast.26, f32[]{:T(128)} %bitcast.25, f32[]{:T(128)} %bitcast.24, f32[]{:T(128)} %bitcast.23, ...), kind=kOutput, calls=%fused_computation.65 | convolution fusion | flops 411566080 | bytes 2883648 | tf_op jit(solution)/shard_map/rd,md->rm/dot_general | solution.py:23
  156.3 2.9 %fusion.30 = f32[192,2048]{1,0:T(8,128)} fusion(f32[192,2048]{1,0:T(8,128)S(1)} %broadcast_in_dim.49, bf16[192,1024]{1,0:T(8,128)(2,1)S(1)} %add_convert_fusion.2, s32[2048]{0:T(1024)S(1)} %bitcast.47, s32[1024]{0:T(1024)S(1)} %pad_add_fusion), kind=kOutput, calls=%fused_computation.27 | convolution fusion | flops 807796736 | bytes 3551232 | tf_op jit(solution)/shard_map/dot_general | solution.py:28
  159.2 6.4 %all-to-all-done.1 = bf16[64,8,1024]{2,1,0:T(8,128)(2,1)S(1)} async-done(((bf16[64,8,1024]{2,1,0:T(8,128)(2,1)}), bf16[64,8,1024]{2,1,0:T(8,128)(2,1)S(1)}, u32[]{:S(2)}, u32[]{:S(2)}) %all-to-all-start.1) | async-done | bytes 1048608 | tf_op jit(solution)/shard_map/all_to_all | solution.py:70
  165.6 2.1 %collective-permute-start.6 = (bf16[512,1024]{1,0:T(8,128)(2,1)S(1)}, bf16[512,1024]{1,0:T(8,128)(2,1)S(1)}, u32[]{:S(2)}, u32[]{:S(2)}) collective-permute-start(bf16[512,1024]{1,0:T(8,128)(2,1)S(1)} %bitcast.43), channel_id=1, source_target_pairs={{0,1},{1,0},{2,3},{3,2},{4,5},{5,4},{6,7},{7,6},{8,9},{9,8},{10,11... | collective-permute-start | bytes 3145736 | tf_op jit(solution)/shard_map/ppermute | solution.py:32
  167.7 2.3 %collective-permute-done.6 = bf16[512,1024]{1,0:T(8,128)(2,1)S(1)} collective-permute-done((bf16[512,1024]{1,0:T(8,128)(2,1)S(1)}, bf16[512,1024]{1,0:T(8,128)(2,1)S(1)}, u32[]{:S(2)}, u32[]{:S(2)}) %collective-permute-start.6) | collective-permute-done | bytes 1048608 | tf_op jit(solution)/shard_map/ppermute | solution.py:32
  170.0 6.7 %add_convert_fusion.1 = bf16[192,1024]{1,0:T(8,128)(2,1)S(1)} fusion(bf16[192,1024]{1,0:T(8,128)(2,1)S(1)} %copy-done.2, bf16[512,1024]{1,0:T(8,128)(2,1)S(1)} %collective-permute-done.6, bf16[512,1024]{1,0:T(8,128)(2,1)S(1)} %bitcast.44, f32[]{:T(128)} %bitcast.26, f32[]{:T(128)} %bitcast.25, f32[]{:T(128)} %bitcast.24, f32[]{:T(128)} %bitcast.23, ...), kind=kOutput, calls=%fused_computation.64 | convolution fusion | flops 411566080 | bytes 2883648 | tf_op jit(solution)/shard_map/rd,md->rm/dot_general | solution.py:23
  176.7 1.8 fusion.36
  178.9 1.9 %collective-permute-done.7 = bf16[192,2048]{1,0:T(8,128)(2,1)S(1)} collective-permute-done((bf16[192,2048]{1,0:T(8,128)(2,1)S(1)}, bf16[192,2048]{1,0:T(8,128)(2,1)S(1)}, u32[]{:S(2)}, u32[]{:S(2)}) %collective-permute-start.7) | collective-permute-done | bytes 786464 | tf_op jit(solution)/shard_map/ppermute | solution.py:32
  180.8 7.9 %add_convert_fusion = bf16[384,2048]{1,0:T(8,128)(2,1)} fusion(f32[384,2048]{1,0:T(8,128)S(1)} %copy-done.9, bf16[4096,2048]{1,0:T(8,128)(2,1)} %param.13, bf16[192,2048]{1,0:T(8,128)(2,1)S(1)} %collective-permute-done.7, bf16[192,2048]{1,0:T(8,128)(2,1)S(1)} %fusion.36, pred[]{:T(512)S(6)} %eq.26), kind=kOutput, calls=%fused_computation.24 | convolution fusion | flops 3229876224 | bytes 14680065 | tf_op jit(solution)/shard_map/dot_general | solution.py:100
  (56 shorter events, 6.8 us)
Async XLA Ops:
  0.0 6.8 %collective-permute-start = (f32[4]{0:T(128)}, f32[4]{0:T(128)S(1)}, u32[]{:S(2)}, u32[]{:S(2)}) collective-permute-start(f32[4]{0:T(128)} %param.11), channel_id=1, source_target_pairs={{0,1},{1,0},{2,3},{3,2},{4,5},{5,4},{6,7},{7,6},{8,9},{9,8},{10,11... | collective-permute-start | bytes 56 | tf_op jit(solution)/shard_map/ppermute | solution.py:32
  1.4 5.5 %collective-permute-start.1 = (f32[4]{0:T(128)}, f32[4]{0:T(128)S(1)}, u32[]{:S(2)}, u32[]{:S(2)}) collective-permute-start(f32[4]{0:T(128)} %param.12), channel_id=1, source_target_pairs={{0,1},{1,0},{2,3},{3,2},{4,5},{5,4},{6,7},{7,6},{8,9},{9,8},{10,11... | collective-permute-start | bytes 56 | tf_op jit(solution)/shard_map/ppermute | solution.py:32
  3.5 3.3 %copy-start.5 = (f32[4]{0:T(128)S(1)}, f32[4]{0:T(128)}, u32[]{:S(2)}) copy-start(f32[4]{0:T(128)} %param.11) | copy-start | bytes 52
  3.5 3.4 %copy-start.6 = (f32[4]{0:T(128)S(1)}, f32[4]{0:T(128)}, u32[]{:S(2)}) copy-start(f32[4]{0:T(128)} %param.12) | copy-start | bytes 52
  7.0 11.7 %copy-start.4 = (s32[2]{0:T(128)S(1)}, s32[2]{0:T(128)}, u32[]{:S(2)}) copy-start(s32[2]{0:T(128)} %param.9) | copy-start | bytes 28
  7.0 39.5 %all-to-all-start = ((bf16[64,16,1024]{2,1,0:T(8,128)(2,1)}), bf16[64,16,1024]{2,1,0:T(8,128)(2,1)}, u32[]{:S(2)}, u32[]{:S(2)}) async-start(bf16[64,16,1024]{2,1,0:T(8,128)(2,1)} %bitcast), calls=%async_computation | async-start | bytes 4194304 | tf_op jit(solution)/shard_map/all_to_all | solution.py:50
  18.6 37.4 %copy-start = (bf16[384,1024]{1,0:T(8,128)(2,1)S(1)}, bf16[384,1024]{1,0:T(8,128)(2,1)}, u32[]{:S(2)}) copy-start(bf16[384,1024]{1,0:T(8,128)(2,1)} %param.7) | copy-start | bytes 2359300
  23.1 52.1 %copy-start.3 = (s32[2,2048]{1,0:T(2,128)S(1)}, s32[2,2048]{1,0:T(2,128)}, u32[]{:S(2)}) copy-start(s32[2,2048]{1,0:T(2,128)} %param.10) | copy-start | bytes 49156
  48.3 23.6 %all-to-all-start.4 = ((bf16[64,8,1024]{2,1,0:T(8,128)(2,1)}), bf16[64,8,1024]{2,1,0:T(8,128)(2,1)S(1)}, u32[]{:S(2)}, u32[]{:S(2)}) async-start(bf16[64,8,1024]{2,1,0:T(8,128)(2,1)} %broadcast_in_dim.48), calls=%async_computation.4 | async-start | bytes 2097152 | tf_op jit(solution)/shard_map/all_to_all | solution.py:70
  71.9 16.1 %collective-permute-start.2 = (bf16[512,1024]{1,0:T(8,128)(2,1)S(1)}, bf16[512,1024]{1,0:T(8,128)(2,1)}, u32[]{:S(2)}, u32[]{:S(2)}) collective-permute-start(bf16[512,1024]{1,0:T(8,128)(2,1)S(1)} %bitcast.41), channel_id=1, source_target_pairs={{0,1},{1,0},{2,3},{3,2},{4,5},{5,4},{6,7},{7,6},{8,9},{9,8},{10,11... | collective-permute-start | bytes 3145736 | tf_op jit(solution)/shard_map/ppermute | solution.py:32
  76.3 23.1 %all-to-all-start.3 = ((bf16[64,8,1024]{2,1,0:T(8,128)(2,1)}), bf16[64,8,1024]{2,1,0:T(8,128)(2,1)}, u32[]{:S(2)}, u32[]{:S(2)}) async-start(bf16[64,8,1024]{2,1,0:T(8,128)(2,1)} %broadcast_in_dim.45), calls=%async_computation.3 | async-start | bytes 2097152 | tf_op jit(solution)/shard_map/all_to_all | solution.py:70
  82.2 21.3 %copy-start.1 = (bf16[192,1024]{1,0:T(8,128)(2,1)}, bf16[192,1024]{1,0:T(8,128)(2,1)S(1)}, u32[]{:S(2)}) copy-start(bf16[192,1024]{1,0:T(8,128)(2,1)S(1)} %fusion.70) | copy-start | bytes 1179652
  99.4 4.1 %collective-permute-start.3 = (bf16[512,1024]{1,0:T(8,128)(2,1)}, bf16[512,1024]{1,0:T(8,128)(2,1)S(1)}, u32[]{:S(2)}, u32[]{:S(2)}) collective-permute-start(bf16[512,1024]{1,0:T(8,128)(2,1)} %bitcast.8), channel_id=1, source_target_pairs={{0,1},{1,0},{2,3},{3,2},{4,5},{5,4},{6,7},{7,6},{8,9},{9,8},{10,11... | collective-permute-start | bytes 3145736 | tf_op jit(solution)/shard_map/ppermute | solution.py:32
  101.3 10.0 %copy-start.8 = (f32[192,2048]{1,0:T(8,128)S(1)}, f32[192,2048]{1,0:T(8,128)}, u32[]{:S(2)}) copy-start(f32[192,2048]{1,0:T(8,128)} %fusion.10) | copy-start | bytes 4718596
  113.2 9.4 %collective-permute-start.4 = (bf16[192,2048]{1,0:T(8,128)(2,1)S(1)}, bf16[192,2048]{1,0:T(8,128)(2,1)S(1)}, u32[]{:S(2)}, u32[]{:S(2)}) collective-permute-start(bf16[192,2048]{1,0:T(8,128)(2,1)S(1)} %fusion.39), channel_id=1, source_target_pairs={{0,1},{1,0},{2,3},{3,2},{4,5},{5,4},{6,7},{7,6},{8,9},{9,8},{10,11... | collective-permute-start | bytes 2359304 | tf_op jit(solution)/shard_map/ppermute | solution.py:32
  114.7 24.9 %all-to-all-start.2 = ((bf16[64,8,1024]{2,1,0:T(8,128)(2,1)}), bf16[64,8,1024]{2,1,0:T(8,128)(2,1)S(1)}, u32[]{:S(2)}, u32[]{:S(2)}) async-start(bf16[64,8,1024]{2,1,0:T(8,128)(2,1)} %broadcast_in_dim.43), calls=%async_computation.2 | async-start | bytes 2097152 | tf_op jit(solution)/shard_map/all_to_all | solution.py:70
  131.4 16.9 %copy-start.2 = (bf16[192,1024]{1,0:T(8,128)(2,1)S(1)}, bf16[192,1024]{1,0:T(8,128)(2,1)}, u32[]{:S(2)}) copy-start(bf16[192,1024]{1,0:T(8,128)(2,1)} %copy-done.1) | copy-start | bytes 1179652
  139.6 8.6 %collective-permute-start.5 = (bf16[512,1024]{1,0:T(8,128)(2,1)S(1)}, bf16[512,1024]{1,0:T(8,128)(2,1)}, u32[]{:S(2)}, u32[]{:S(2)}) collective-permute-start(bf16[512,1024]{1,0:T(8,128)(2,1)S(1)} %bitcast.45), channel_id=1, source_target_pairs={{0,1},{1,0},{2,3},{3,2},{4,5},{5,4},{6,7},{7,6},{8,9},{9,8},{10,11... | collective-permute-start | bytes 3145736 | tf_op jit(solution)/shard_map/ppermute | solution.py:32
  143.2 22.4 %all-to-all-start.1 = ((bf16[64,8,1024]{2,1,0:T(8,128)(2,1)}), bf16[64,8,1024]{2,1,0:T(8,128)(2,1)S(1)}, u32[]{:S(2)}, u32[]{:S(2)}) async-start(bf16[64,8,1024]{2,1,0:T(8,128)(2,1)} %broadcast_in_dim.41), calls=%async_computation.1 | async-start | bytes 2097152 | tf_op jit(solution)/shard_map/all_to_all | solution.py:70
  165.6 11.1 %copy-start.7 = (f32[192,2048]{1,0:T(8,128)S(1)}, f32[192,2048]{1,0:T(8,128)}, u32[]{:S(2)}) copy-start(f32[192,2048]{1,0:T(8,128)} %fusion.30) | copy-start | bytes 4718596
  165.6 4.4 %collective-permute-start.6 = (bf16[512,1024]{1,0:T(8,128)(2,1)S(1)}, bf16[512,1024]{1,0:T(8,128)(2,1)S(1)}, u32[]{:S(2)}, u32[]{:S(2)}) collective-permute-start(bf16[512,1024]{1,0:T(8,128)(2,1)S(1)} %bitcast.43), channel_id=1, source_target_pairs={{0,1},{1,0},{2,3},{3,2},{4,5},{5,4},{6,7},{7,6},{8,9},{9,8},{10,11... | collective-permute-start | bytes 3145736 | tf_op jit(solution)/shard_map/ppermute | solution.py:32
  176.7 4.2 %copy-start.9 = (f32[384,2048]{1,0:T(8,128)S(1)}, f32[384,2048]{1,0:T(8,128)}, u32[]{:S(2)}) copy-start(f32[384,2048]{1,0:T(8,128)} %fusion.22) | copy-start | bytes 9437188
  178.5 2.4 %collective-permute-start.7 = (bf16[192,2048]{1,0:T(8,128)(2,1)S(1)}, bf16[192,2048]{1,0:T(8,128)(2,1)S(1)}, u32[]{:S(2)}, u32[]{:S(2)}) collective-permute-start(bf16[192,2048]{1,0:T(8,128)(2,1)S(1)} %fusion.36), channel_id=1, source_target_pairs={{0,1},{1,0},{2,3},{3,2},{4,5},{5,4},{6,7},{7,6},{8,9},{9,8},{10,11... | collective-permute-start | bytes 2359304 | tf_op jit(solution)/shard_map/ppermute | solution.py:32

commit v14 on v12

--- a/solution.py
+++ b/solution.py
@@ -64,11 +64,14 @@
     ]
     share = unit_rows.shape[0] // cores
     own_rows = lax.dynamic_slice_in_dim(unit_rows, core * share, share, axis=0)
-    features = jnp.zeros((unit_rows.shape[0], whitening.shape[1]), jnp.float32)
+    own_features = jnp.zeros((share, whitening.shape[1]), jnp.float32)
+    other_features = jnp.zeros((share, whitening.shape[1]), jnp.float32)
     for number in range(block_count):
         mine = arrived[number]
         if number > 0:
-            mine, features = lax.optimization_barrier((mine, features))
+            mine, own_features, other_features = lax.optimization_barrier(
+                (mine, own_features, other_features)
+            )
         other = swap_cores(mine)
         parts = [
             kernel_of(inner_products(own_rows, landmark), widths, weights).astype(jnp.bfloat16)
@@ -81,13 +84,16 @@
         )
         own_kernel = reorder_columns(own_kernel, landmark_picks[number])
         other_kernel = swap_cores(own_kernel)
-        kernel = jnp.where(
-            core == 0,
-            jnp.concatenate([own_kernel, other_kernel], axis=0),
-            jnp.concatenate([other_kernel, own_kernel], axis=0),
+        rows = lax.dynamic_slice_in_dim(whitening, number * block_rows, block_rows, axis=0)
+        own_features = own_features + jnp.dot(own_kernel, rows, preferred_element_type=jnp.float32)
+        other_features = other_features + jnp.dot(
+            other_kernel, rows, preferred_element_type=jnp.float32
         )
-        rows = lax.dynamic_slice_in_dim(whitening, number * block_rows, block_rows, axis=0)
-        features = features + jnp.dot(kernel, rows, preferred_element_type=jnp.float32)
+    features = jnp.where(
+        core == 0,
+        jnp.concatenate([own_features, other_features], axis=0),
+        jnp.concatenate([other_features, own_features], axis=0),
+    )
     return features.astype(jnp.bfloat16)
 
 

time: 160 us -> 159 us (level)
  waiting for transfers between devices: 27.7 us -> 23.6 us
  other arithmetic: 6.09 us -> 7.89 us
    ppermute x6, waiting for transfers between devices: 4.07 us -> 0.02 us  [swap_cores(): return lax.ppermute(value, 'bw', [(0, 1), (1, 0)])]
    convert_element_type x0 -> x1, other arithmetic: none -> 1.8 us  [per_device(): return features.astype(jnp.bfloat16)]
    dot_general x2 -> x4, matrix products: 16.4 us -> 16.9 us  [the longest x2 12 us: per_device(): jnp.dot(own_kernel, rows, preferred_element_type=jnp.float32)]
  transfers between devices with their start and end apart: 8 -> 8, of which waited for: 3 -> 1; matrix products, arithmetic and copies ran while one was open for 28% -> 33% of each run, Pallas kernels for 0% -> 0%
where the time goes in v14:
time: 159 us; the launch traced here: 158 us
  matrix products  55.3 us (35%)
  blocking collectives  35.1 us (22%)
  starting transfers between devices  23.6 us (15%)
  waiting for transfers between devices  23.6 us (15%)
  between operations  9.08 us (6%)
  other arithmetic  7.89 us (5%)
  local copies, waits for them, and re-layouts  3.46 us (2%)
    all_to_all x1, blocking collectives, per_device(): lax.all_to_all(jnp.broadcast_to(kept[number][None], (count,) + kept.shape...  35.1 us
    dot_general x4, matrix products, inner_products(): jnp.einsum('rd,md->rm', unit_rows, landmark, preferred_element_type=jnp.f...  30.6 us
    all_to_all x1, waiting for transfers between devices, per_device(): spread = lax.all_to_all(pieces, SPREAD, 0, 0, tiled=True)  23.6 us
    dot_general x2, matrix products, per_device(): jnp.dot(own_kernel, rows, preferred_element_type=jnp.float32)  12 us
    all_to_all x1, starting transfers between devices, per_device(): spread = lax.all_to_all(pieces, SPREAD, 0, 0, tiled=True)  11.4 us
    dot_general x2, matrix products, reorder_columns(): ordered = jnp.dot(kernel, onehot, preferred_element_type=jnp.float32)  7.78 us
    all_to_all x1, starting transfers between devices, per_device(): lax.all_to_all(jnp.broadcast_to(kept[number][None], (count,) + kept.shape...  6.79 us
    ppermute x6, starting transfers between devices, swap_cores(): return lax.ppermute(value, 'bw', [(0, 1), (1, 0)])  5.47 us
  transfers between devices with their start and end apart: 8, of which 1 were waited for; matrix products, arithmetic and copies ran while one was open for 33% of the time, Pallas kernels for 0%

profile of v14, /device:TPU:1, one launch (start us, length us, event | category | flops | bytes accessed | tf_op | source)
XLA Modules:
  0.0 158.0 jit_solution(3153158738497084949)
XLA Ops:
  0.0 1.4 collective-permute-start
  1.4 2.1 %fusion.12 = f32[1024]{0:T(1024)S(1)} fusion(bf16[2048,1024]{1,0:T(8,128)(2,1)} %param.8, s32[]{:T(128)S(6)} %select_n.34), kind=kLoop, calls=%fused_computation.16 | loop fusion | flops 3144704 | bytes 2101252 | tf_op jit(solution)/shard_map/reduce_sum | solution.py:11
  3.5 3.4 %fusion.13 = bf16[1024,1024]{1,0:T(8,128)(2,1)} fusion(f32[1024]{0:T(1024)S(1)} %add_rsqrt_fusion, bf16[2048,1024]{1,0:T(8,128)(2,1)} %param.8, s32[]{:T(128)S(6)} %select_n.34), kind=kLoop, calls=%fused_computation.17 | loop fusion | flops 3145728 | bytes 4198404 | tf_op jit(solution)/shard_map/convert_element_type | solution.py:12
  6.9 0.1 pad_maximum_fusion.1
  7.0 11.4 %all-to-all-start = ((bf16[64,16,1024]{2,1,0:T(8,128)(2,1)}), bf16[64,16,1024]{2,1,0:T(8,128)(2,1)S(1)}, u32[]{:S(2)}, u32[]{:S(2)}) async-start(bf16[64,16,1024]{2,1,0:T(8,128)(2,1)} %bitcast), calls=%async_computation | async-start | bytes 4194304 | tf_op jit(solution)/shard_map/all_to_all | solution.py:52
  18.4 0.6 fusion.41
  22.8 23.6 %all-to-all-done = bf16[64,16,1024]{2,1,0:T(8,128)(2,1)S(1)} async-done(((bf16[64,16,1024]{2,1,0:T(8,128)(2,1)}), bf16[64,16,1024]{2,1,0:T(8,128)(2,1)S(1)}, u32[]{:S(2)}, u32[]{:S(2)}) %all-to-all-start) | async-done | bytes 2097184 | tf_op jit(solution)/shard_map/all_to_all | solution.py:52
  46.4 0.3 broadcast_in_dim.19
  46.6 35.1 %all_to_all.15 = bf16[64,16,1024]{2,1,0:T(8,128)(2,1)} all-to-all(bf16[64,16,1024]{2,1,0:T(8,128)(2,1)S(1)} %broadcast_in_dim.19), channel_id=1, replica_groups=mesh['row'=8,'lmk'=8,'bw'=2] {'row','lmk'}, dimensions={0} | all-to-all | bytes 4194304 | tf_op jit(solution)/shard_map/all_to_all | solution.py:60
  81.7 3.1 %collective-permute-start.2 = (bf16[1024,1024]{1,0:T(8,128)(2,1)}, bf16[1024,1024]{1,0:T(8,128)(2,1)}, u32[]{:S(2)}, u32[]{:S(2)}) collective-permute-start(bf16[1024,1024]{1,0:T(8,128)(2,1)} %bitcast.8), channel_id=1, source_target_pairs={{0,1},{1,0},{2,3},{3,2},{4,5},{5,4},{6,7},{7,6},{8,9},{9,8},{10,11... | collective-permute-start | bytes 6291464 | tf_op jit(solution)/shard_map/ppermute | solution.py:34
  84.8 0.2 convert_element_type.37
  85.0 0.2 multiply_reduce_fusion
  85.3 0.1 dynamic-slice
  85.3 0.1 fusion.23
  85.5 0.1 copy-done.1
  85.6 0.7 fusion.39
  91.2 1.6 %broadcast_in_dim.17 = bf16[64,16,1024]{2,1,0:T(8,128)(2,1)} broadcast(bf16[16,1024]{1,0:T(8,128)(2,1)S(1)} %get-tuple-element.18), dimensions={1,2} | broadcast | bytes 2129920 | tf_op jit(solution)/shard_map/broadcast_in_dim | solution.py:61
  92.9 6.8 %all-to-all-start.1 = ((bf16[64,16,1024]{2,1,0:T(8,128)(2,1)}), bf16[64,16,1024]{2,1,0:T(8,128)(2,1)S(1)}, u32[]{:S(2)}, u32[]{:S(2)}) async-start(bf16[64,16,1024]{2,1,0:T(8,128)(2,1)} %broadcast_in_dim.17), calls=%async_computation.1 | async-start | bytes 4194304 | tf_op jit(solution)/shard_map/all_to_all | solution.py:60
  99.7 8.3 %add_convert_fusion.3 = bf16[192,1024]{1,0:T(8,128)(2,1)S(1)} fusion(f32[]{:T(128)} %bitcast.22, f32[]{:T(128)} %bitcast.21, f32[]{:T(128)} %bitcast.20, f32[]{:T(128)} %bitcast.19, f32[]{:T(128)} %bitcast.18, f32[]{:T(128)} %bitcast.17, f32[]{:T(128)} %bitcast.16, f32[]{:T(128)} %bitcast.15, f32[]{:T(128)} %bitcast.14, f32[]{:T(128)} %bitcast.13, ...), kind=kOutput, calls=%fused_computation.42 | convolution fusion | flops 407371776 | bytes 2883648 | tf_op jit(solution)/shard_map/rd,md->rm/dot_general | solution.py:23
  108.0 8.6 %add_convert_fusion.2 = bf16[192,1024]{1,0:T(8,128)(2,1)S(1)} fusion(f32[]{:T(128)} %bitcast.22, f32[]{:T(128)} %bitcast.21, f32[]{:T(128)} %bitcast.20, f32[]{:T(128)} %bitcast.19, f32[]{:T(128)} %bitcast.18, f32[]{:T(128)} %bitcast.17, f32[]{:T(128)} %bitcast.16, f32[]{:T(128)} %bitcast.15, f32[]{:T(128)} %bitcast.14, f32[]{:T(128)} %bitcast.13, ...), kind=kOutput, calls=%fused_computation.41 | convolution fusion | flops 407371776 | bytes 2883648 | tf_op jit(solution)/shard_map/rd,md->rm/dot_general | solution.py:23
  116.7 3.9 %fusion.22 = bf16[192,2048]{1,0:T(8,128)(2,1)S(1)} fusion(s32[2048]{0:T(1024)S(1)} %bitcast.42, bf16[192,1024]{1,0:T(8,128)(2,1)S(1)} %add_convert_fusion.2, bf16[192,1024]{1,0:T(8,128)(2,1)S(1)} %add_convert_fusion.3, pred[]{:T(512)S(6)} %eq.25), kind=kOutput, calls=%fused_computation.23 | convolution fusion | flops 1618739200 | bytes 1581057 | tf_op jit(solution)/shard_map/dot_general | solution.py:29
  120.6 0.4 collective-permute-start.3
  120.9 6.6 %fusion.10 = f32[192,2048]{1,0:T(8,128)} fusion(bf16[192,2048]{1,0:T(8,128)(2,1)S(1)} %fusion.22, bf16[4096,2048]{1,0:T(8,128)(2,1)} %param.13), kind=kOutput, calls=%fused_computation.12 | convolution fusion | flops 1610612736 | bytes 10747904 | tf_op jit(solution)/shard_map/dot_general | solution.py:88
  127.6 3.0 %fusion.8 = f32[192,2048]{1,0:T(8,128)} fusion(bf16[192,2048]{1,0:T(8,128)(2,1)S(1)} %collective-permute-done.3, bf16[4096,2048]{1,0:T(8,128)(2,1)S(1)} %bitcast.44), kind=kOutput, calls=%fused_computation.10 | convolution fusion | flops 1610612736 | bytes 10747904 | tf_op jit(solution)/shard_map/dot_general | solution.py:89
  130.6 0.2 collective-permute-start.4
  130.8 6.7 %add_convert_fusion.1 = bf16[192,1024]{1,0:T(8,128)(2,1)S(1)} fusion(f32[]{:T(128)} %bitcast.22, f32[]{:T(128)} %bitcast.21, f32[]{:T(128)} %bitcast.20, f32[]{:T(128)} %bitcast.19, f32[]{:T(128)} %bitcast.18, f32[]{:T(128)} %bitcast.17, f32[]{:T(128)} %bitcast.16, f32[]{:T(128)} %bitcast.15, f32[]{:T(128)} %bitcast.14, f32[]{:T(128)} %bitcast.13, ...), kind=kOutput, calls=%fused_computation.40 | convolution fusion | flops 407371776 | bytes 2883648 | tf_op jit(solution)/shard_map/rd,md->rm/dot_general | solution.py:23
  137.5 7.0 %add_convert_fusion = bf16[192,1024]{1,0:T(8,128)(2,1)S(1)} fusion(f32[]{:T(128)} %bitcast.22, f32[]{:T(128)} %bitcast.21, f32[]{:T(128)} %bitcast.20, f32[]{:T(128)} %bitcast.19, f32[]{:T(128)} %bitcast.18, f32[]{:T(128)} %bitcast.17, f32[]{:T(128)} %bitcast.16, f32[]{:T(128)} %bitcast.15, f32[]{:T(128)} %bitcast.14, f32[]{:T(128)} %bitcast.13, ...), kind=kOutput, calls=%fused_computation.39 | convolution fusion | flops 407371776 | bytes 2883648 | tf_op jit(solution)/shard_map/rd,md->rm/dot_general | solution.py:23
  144.5 3.9 %fusion.21 = bf16[192,2048]{1,0:T(8,128)(2,1)S(1)} fusion(s32[2048]{0:T(1024)S(1)} %bitcast.41, bf16[192,1024]{1,0:T(8,128)(2,1)S(1)} %add_convert_fusion, bf16[192,1024]{1,0:T(8,128)(2,1)S(1)} %add_convert_fusion.1, pred[]{:T(512)S(6)} %eq.25), kind=kOutput, calls=%fused_computation.22 | convolution fusion | flops 1618739200 | bytes 1581057 | tf_op jit(solution)/shard_map/dot_general | solution.py:29
  148.5 0.4 collective-permute-start.5
  148.8 5.4 %fusion.15 = bf16[192,2048]{1,0:T(8,128)(2,1)S(1)} fusion(f32[192,2048]{1,0:T(8,128)S(1)} %copy-done.6, bf16[192,2048]{1,0:T(8,128)(2,1)S(1)} %fusion.21, bf16[4096,2048]{1,0:T(8,128)(2,1)} %param.13), kind=kOutput, calls=%fused_computation.20 | convolution fusion | flops 1611399168 | bytes 11534336 | tf_op jit(solution)/shard_map/dot_general | solution.py:88
  154.4 1.9 %fusion.18 = bf16[192,2048]{1,0:T(8,128)(2,1)S(1)} fusion(f32[192,2048]{1,0:T(8,128)S(1)} %copy-done.5, bf16[192,2048]{1,0:T(8,128)(2,1)S(1)} %collective-permute-done.5, bf16[4096,2048]{1,0:T(8,128)(2,1)S(1)} %bitcast.46), kind=kOutput, calls=%fused_computation.21 | convolution fusion | flops 1611399168 | bytes 11534336 | tf_op jit(solution)/shard_map/dot_general | solution.py:89
  156.2 1.8 %fusion.14 = bf16[384,2048]{1,0:T(8,128)(2,1)} fusion(bf16[192,2048]{1,0:T(8,128)(2,1)S(1)} %fusion.18, bf16[192,2048]{1,0:T(8,128)(2,1)S(1)} %fusion.15, pred[]{:T(512)S(6)} %eq.25), kind=kLoop, calls=%fused_computation.19 | loop fusion | flops 7077888 | bytes 3145729 | tf_op jit(solution)/shard_map/convert_element_type | solution.py:97
  (44 shorter events, 0.2 us)
Async XLA Ops:
  0.0 6.8 %collective-permute-start = (f32[4]{0:T(128)}, f32[4]{0:T(128)S(1)}, u32[]{:S(2)}, u32[]{:S(2)}) collective-permute-start(f32[4]{0:T(128)} %param.11), channel_id=1, source_target_pairs={{0,1},{1,0},{2,3},{3,2},{4,5},{5,4},{6,7},{7,6},{8,9},{9,8},{10,11... | collective-permute-start | bytes 56 | tf_op jit(solution)/shard_map/ppermute | solution.py:34
  1.4 5.5 %collective-permute-start.1 = (f32[4]{0:T(128)}, f32[4]{0:T(128)S(1)}, u32[]{:S(2)}, u32[]{:S(2)}) collective-permute-start(f32[4]{0:T(128)} %param.12), channel_id=1, source_target_pairs={{0,1},{1,0},{2,3},{3,2},{4,5},{5,4},{6,7},{7,6},{8,9},{9,8},{10,11... | collective-permute-start | bytes 56 | tf_op jit(solution)/shard_map/ppermute | solution.py:34
  3.5 3.4 %copy-start.3 = (f32[4]{0:T(128)S(1)}, f32[4]{0:T(128)}, u32[]{:S(2)}) copy-start(f32[4]{0:T(128)} %param.11) | copy-start | bytes 52
  3.5 3.5 %copy-start.4 = (f32[4]{0:T(128)S(1)}, f32[4]{0:T(128)}, u32[]{:S(2)}) copy-start(f32[4]{0:T(128)} %param.12) | copy-start | bytes 52
  7.0 11.4 %copy-start.2 = (s32[2]{0:T(128)S(1)}, s32[2]{0:T(128)}, u32[]{:S(2)}) copy-start(s32[2]{0:T(128)} %param.9) | copy-start | bytes 28
  7.0 39.4 %all-to-all-start = ((bf16[64,16,1024]{2,1,0:T(8,128)(2,1)}), bf16[64,16,1024]{2,1,0:T(8,128)(2,1)S(1)}, u32[]{:S(2)}, u32[]{:S(2)}) async-start(bf16[64,16,1024]{2,1,0:T(8,128)(2,1)} %bitcast), calls=%async_computation | async-start | bytes 4194304 | tf_op jit(solution)/shard_map/all_to_all | solution.py:52
  46.6 38.2 %copy-start = (bf16[384,1024]{1,0:T(8,128)(2,1)S(1)}, bf16[384,1024]{1,0:T(8,128)(2,1)}, u32[]{:S(2)}) copy-start(bf16[384,1024]{1,0:T(8,128)(2,1)} %param.7) | copy-start | bytes 2359300
  81.7 26.3 %collective-permute-start.2 = (bf16[1024,1024]{1,0:T(8,128)(2,1)}, bf16[1024,1024]{1,0:T(8,128)(2,1)}, u32[]{:S(2)}, u32[]{:S(2)}) collective-permute-start(bf16[1024,1024]{1,0:T(8,128)(2,1)} %bitcast.8), channel_id=1, source_target_pairs={{0,1},{1,0},{2,3},{3,2},{4,5},{5,4},{6,7},{7,6},{8,9},{9,8},{10,11... | collective-permute-start | bytes 6291464 | tf_op jit(solution)/shard_map/ppermute | solution.py:34
  84.8 0.7 copy-start.1
  92.9 37.7 %all-to-all-start.1 = ((bf16[64,16,1024]{2,1,0:T(8,128)(2,1)}), bf16[64,16,1024]{2,1,0:T(8,128)(2,1)S(1)}, u32[]{:S(2)}, u32[]{:S(2)}) async-start(bf16[64,16,1024]{2,1,0:T(8,128)(2,1)} %broadcast_in_dim.17), calls=%async_computation.1 | async-start | bytes 4194304 | tf_op jit(solution)/shard_map/all_to_all | solution.py:60
  108.0 19.5 %slice-start = ((s8[16777216]{0:T(1024)(128)(4,1)}), s8[4194304]{0:T(1024)(128)(4,1)S(1)}, s32[]{:S(2)}) async-start(s8[16777216]{0:T(1024)(128)(4,1)} %bitcast.43), calls=%async_computation.3 | async-start | bytes 8388608
  116.6 10.9 %slice-start.1 = ((s8[16777216]{0:T(1024)(128)(4,1)}), s8[4194304]{0:T(1024)(128)(4,1)S(1)}, s32[]{:S(2)}) async-start(s8[16777216]{0:T(1024)(128)(4,1)} %bitcast.43), calls=%async_computation.4 | async-start | bytes 8388608
  116.6 10.9 %slice-start.2 = ((s8[16777216]{0:T(1024)(128)(4,1)}), s8[4194304]{0:T(1024)(128)(4,1)S(1)}, s32[]{:S(2)}) async-start(s8[16777216]{0:T(1024)(128)(4,1)} %bitcast.43), calls=%async_computation.5 | async-start | bytes 8388608
  120.6 7.0 %slice-start.3 = ((s8[16777216]{0:T(1024)(128)(4,1)}), s8[4194304]{0:T(1024)(128)(4,1)S(1)}, s32[]{:S(2)}) async-start(s8[16777216]{0:T(1024)(128)(4,1)} %bitcast.43), calls=%async_computation.6 | async-start | bytes 8388608
  120.6 7.0 %collective-permute-start.3 = (bf16[192,2048]{1,0:T(8,128)(2,1)S(1)}, bf16[192,2048]{1,0:T(8,128)(2,1)S(1)}, u32[]{:S(2)}, u32[]{:S(2)}) collective-permute-start(bf16[192,2048]{1,0:T(8,128)(2,1)S(1)} %fusion.22), channel_id=1, source_target_pairs={{0,1},{1,0},{2,3},{3,2},{4,5},{5,4},{6,7},{7,6},{8,9},{9,8},{10,11... | collective-permute-start | bytes 2359304 | tf_op jit(solution)/shard_map/ppermute | solution.py:34
  130.6 6.9 %collective-permute-start.4 = (bf16[1024,1024]{1,0:T(8,128)(2,1)S(1)}, bf16[1024,1024]{1,0:T(8,128)(2,1)S(1)}, u32[]{:S(2)}, u32[]{:S(2)}) collective-permute-start(bf16[1024,1024]{1,0:T(8,128)(2,1)S(1)} %bitcast.39), channel_id=1, source_target_pairs={{0,1},{1,0},{2,3},{3,2},{4,5},{5,4},{6,7},{7,6},{8,9},{9,8},{10,11... | collective-permute-start | bytes 6291464 | tf_op jit(solution)/shard_map/ppermute | solution.py:34
  137.5 16.8 %slice-start.4 = ((s8[16777216]{0:T(1024)(128)(4,1)}), s8[4194304]{0:T(1024)(128)(4,1)S(1)}, s32[]{:S(2)}) async-start(s8[16777216]{0:T(1024)(128)(4,1)} %bitcast.45), calls=%async_computation.7 | async-start | bytes 8388608
  144.5 4.3 %copy-start.6 = (f32[192,2048]{1,0:T(8,128)S(1)}, f32[192,2048]{1,0:T(8,128)}, u32[]{:S(2)}) copy-start(f32[192,2048]{1,0:T(8,128)} %fusion.10) | copy-start | bytes 4718596
  144.5 9.8 %slice-start.5 = ((s8[16777216]{0:T(1024)(128)(4,1)}), s8[4194304]{0:T(1024)(128)(4,1)S(1)}, s32[]{:S(2)}) async-start(s8[16777216]{0:T(1024)(128)(4,1)} %bitcast.45), calls=%async_computation.8 | async-start | bytes 8388608
  144.5 9.8 %slice-start.6 = ((s8[16777216]{0:T(1024)(128)(4,1)}), s8[4194304]{0:T(1024)(128)(4,1)S(1)}, s32[]{:S(2)}) async-start(s8[16777216]{0:T(1024)(128)(4,1)} %bitcast.45), calls=%async_computation.9 | async-start | bytes 8388608
  148.4 5.9 %slice-start.7 = ((s8[16777216]{0:T(1024)(128)(4,1)}), s8[4194304]{0:T(1024)(128)(4,1)S(1)}, s32[]{:S(2)}) async-start(s8[16777216]{0:T(1024)(128)(4,1)} %bitcast.45), calls=%async_computation.10 | async-start | bytes 8388608
  148.4 5.9 %copy-start.5 = (f32[192,2048]{1,0:T(8,128)S(1)}, f32[192,2048]{1,0:T(8,128)}, u32[]{:S(2)}) copy-start(f32[192,2048]{1,0:T(8,128)} %fusion.8) | copy-start | bytes 4718596
  148.5 5.8 %collective-permute-start.5 = (bf16[192,2048]{1,0:T(8,128)(2,1)S(1)}, bf16[192,2048]{1,0:T(8,128)(2,1)S(1)}, u32[]{:S(2)}, u32[]{:S(2)}) collective-permute-start(bf16[192,2048]{1,0:T(8,128)(2,1)S(1)} %fusion.21), channel_id=1, source_target_pairs={{0,1},{1,0},{2,3},{3,2},{4,5},{5,4},{6,7},{7,6},{8,9},{9,8},{10,11... | collective-permute-start | bytes 2359304 | tf_op jit(solution)/shard_map/ppermute | solution.py:34

commit v15 on v14

--- a/solution.py
+++ b/solution.py
@@ -37,7 +37,7 @@
 def per_device(
     embeddings, candidates, block_owner, landmark_picks, inverse_width, mixture, whitening
 ):
-    unit_rows = normalize(embeddings)
+    own_rows = normalize(embeddings)
     block_count, block_rows = landmark_picks.shape
     cores = lax.axis_size("bw")
     half = block_rows // cores
@@ -46,24 +46,23 @@
     widths = jnp.concatenate([inverse_width, swap_cores(inverse_width)])
     weights = jnp.concatenate([mixture, swap_cores(mixture)])
     count = lax.axis_size(SPREAD)
-    chosen = normalize(lax.dynamic_slice_in_dim(candidates, core * half, half, axis=0))
-    chosen, widths, weights = lax.optimization_barrier((chosen, widths, weights))
+    chosen = candidates
     pieces = chosen.reshape(count, half // count, chosen.shape[1])
     spread = lax.all_to_all(pieces, SPREAD, 0, 0, tiled=True)
     kept = jnp.stack(
         [
-            lax.dynamic_index_in_dim(spread, block_owner[number], 0, keepdims=False)
+            normalize(lax.dynamic_index_in_dim(spread, block_owner[number], 0, keepdims=False))
             for number in range(block_count)
         ]
     )
+    kept, widths, weights = lax.optimization_barrier((kept, widths, weights))
     arrived = [
         lax.all_to_all(
             jnp.broadcast_to(kept[number][None], (count,) + kept.shape[1:]), SPREAD, 0, 0, tiled=True
         ).reshape(half, chosen.shape[1])
         for number in range(block_count)
     ]
-    share = unit_rows.shape[0] // cores
-    own_rows = lax.dynamic_slice_in_dim(unit_rows, core * share, share, axis=0)
+    share = own_rows.shape[0]
     own_features = jnp.zeros((share, whitening.shape[1]), jnp.float32)
     other_features = jnp.zeros((share, whitening.shape[1]), jnp.float32)
     for number in range(block_count):
@@ -99,8 +98,8 @@
 
 def solution(mesh):
     in_specs = (
-        P(SPREAD, None),
-        P(SPREAD, None),
+        P(SPREAD + ("bw",), None),
+        P(SPREAD + ("bw",), None),
         P(),
         P(),
         P("bw"),

time: 159 us -> 154 us (0.969)
  matrix products: 55.3 us -> 49.6 us
  other arithmetic: 7.89 us -> 2.34 us
  local copies, waits for them, and re-layouts: 3.46 us -> 8.86 us
    dot_general x2, matrix products: 12 us -> 4.89 us  [per_device(): jnp.dot(own_kernel, rows, preferred_element_type=jnp.float32)]
    another operation x0 -> x3, local copies, waits for them, and re-layouts: none -> 4.95 us
    convert_element_type x2 -> x1, other arithmetic: 3.47 us -> 0.08 us  [normalize(): return (widened * scale).astype(jnp.bfloat16)]
    dot_general x4, matrix products: 30.6 us -> 33.2 us  [inner_products(): jnp.einsum('rd,md->rm', unit_rows, landmark, preferred_element_type=jnp.f...]
    reduce_sum x2, other arithmetic: 2.3 us -> 0.29 us  [normalize(): jnp.sum(widened * widened, axis=-1, keepdims=True) + 1e-06]
  transfers between devices with their start and end apart: 8 -> 8, of which waited for: 1 -> 2; matrix products, arithmetic and copies ran while one was open for 33% -> 27% of each run, Pallas kernels for 0% -> 0%
where the time goes in v15:
time: 154 us; the launch traced here: 153 us
  matrix products  49.6 us (32%)
  blocking collectives  34.6 us (22%)
  starting transfers between devices  24.7 us (16%)
  waiting for transfers between devices  22.6 us (15%)
  between operations  10.4 us (7%)
  local copies, waits for them, and re-layouts  8.86 us (6%)
  other arithmetic  2.34 us (2%)
    all_to_all x1, blocking collectives, per_device(): lax.all_to_all(jnp.broadcast_to(kept[number][None], (count,) + kept.shape...  34.6 us
    dot_general x4, matrix products, inner_products(): jnp.einsum('rd,md->rm', unit_rows, landmark, preferred_element_type=jnp.f...  33.2 us
    all_to_all x1, waiting for transfers between devices, per_device(): spread = lax.all_to_all(pieces, SPREAD, 0, 0, tiled=True)  22.4 us
    all_to_all x1, starting transfers between devices, per_device(): spread = lax.all_to_all(pieces, SPREAD, 0, 0, tiled=True)  12.1 us
    dot_general x2, matrix products, reorder_columns(): ordered = jnp.dot(kernel, onehot, preferred_element_type=jnp.float32)  7.78 us
    all_to_all x1, starting transfers between devices, per_device(): lax.all_to_all(jnp.broadcast_to(kept[number][None], (count,) + kept.shape...  6.87 us
    ppermute x6, starting transfers between devices, swap_cores(): return lax.ppermute(value, 'bw', [(0, 1), (1, 0)])  5.7 us
    another operation x3, local copies, waits for them, and re-layouts  4.95 us
  transfers between devices with their start and end apart: 8, of which 2 were waited for; matrix products, arithmetic and copies ran while one was open for 27% of the time, Pallas kernels for 0%

profile of v15, /device:TPU:1, one launch (start us, length us, event | category | flops | bytes accessed | tf_op | source)
XLA Modules:
  0.0 153.1 jit_solution(8269435776426598156)
XLA Ops:
  0.0 1.2 dynamic-slice.6
  1.9 3.1 %constant_dynamic-slice_fusion = bf16[1024,1024]{1,0:T(8,128)(2,1)} fusion(bf16[2048,1024]{1,0:T(8,128)(2,1)} %param.8, s32[]{:T(128)S(6)} %subtract.2), kind=kLoop, calls=%fused_computation.54 | loop fusion | bytes 4194308 | tf_op jit(solution)/call_exported
  5.0 12.1 %all-to-all-start = ((bf16[64,16,1024]{2,1,0:T(8,128)(2,1)}), bf16[64,16,1024]{2,1,0:T(8,128)(2,1)S(1)}, u32[]{:S(2)}, u32[]{:S(2)}) async-start(bf16[64,16,1024]{2,1,0:T(8,128)(2,1)} %bitcast.1), calls=%async_computation | async-start | bytes 4194304 | tf_op jit(solution)/shard_map/all_to_all | solution.py:51
  17.1 1.0 collective-permute-start
  18.2 0.1 collective-permute-start.1
  18.3 0.6 fusion.60
  22.9 22.4 %all-to-all-done = bf16[64,16,1024]{2,1,0:T(8,128)(2,1)S(1)} async-done(((bf16[64,16,1024]{2,1,0:T(8,128)(2,1)}), bf16[64,16,1024]{2,1,0:T(8,128)(2,1)S(1)}, u32[]{:S(2)}, u32[]{:S(2)}) %all-to-all-start) | async-done | bytes 2097184 | tf_op jit(solution)/shard_map/all_to_all | solution.py:51
  45.3 0.1 fusion.35
  45.6 0.2 broadcast_in_dim.20
  45.9 34.6 %all_to_all.15 = bf16[64,16,1024]{2,1,0:T(8,128)(2,1)S(1)} all-to-all(bf16[64,16,1024]{2,1,0:T(8,128)(2,1)S(1)} %broadcast_in_dim.20), channel_id=1, replica_groups=mesh['row'=8,'lmk'=8,'bw'=2] {'row','lmk'}, dimensions={0} | all-to-all | bytes 4194304 | tf_op jit(solution)/shard_map/all_to_all | solution.py:60
  80.5 3.1 %collective-permute-start.2 = (bf16[1024,1024]{1,0:T(8,128)(2,1)S(1)}, bf16[1024,1024]{1,0:T(8,128)(2,1)}, u32[]{:S(2)}, u32[]{:S(2)}) collective-permute-start(bf16[1024,1024]{1,0:T(8,128)(2,1)S(1)} %bitcast.37), channel_id=1, source_target_pairs={{0,1},{1,0},{2,3},{3,2},{4,5},{5,4},{6,7},{7,6},{8,9},{9,8},{10,11... | collective-permute-start | bytes 6291464 | tf_op jit(solution)/shard_map/ppermute | solution.py:34
  83.6 0.6 dynamic-slice.2
  84.9 0.2 fusion.21
  85.1 1.6 %broadcast_in_dim.18 = bf16[64,16,1024]{2,1,0:T(8,128)(2,1)} broadcast(bf16[16,1024]{1,0:T(8,128)(2,1)S(1)} %get-tuple-element.22), dimensions={1,2} | broadcast | bytes 2129920 | tf_op jit(solution)/shard_map/broadcast_in_dim | solution.py:61
  86.7 6.9 %all-to-all-start.1 = ((bf16[64,16,1024]{2,1,0:T(8,128)(2,1)}), bf16[64,16,1024]{2,1,0:T(8,128)(2,1)}, u32[]{:S(2)}, u32[]{:S(2)}) async-start(bf16[64,16,1024]{2,1,0:T(8,128)(2,1)} %broadcast_in_dim.18), calls=%async_computation.1 | async-start | bytes 4194304 | tf_op jit(solution)/shard_map/all_to_all | solution.py:60
  93.6 0.7 fusion.59
  99.2 0.7 fusion.58
  99.9 7.9 %add_convert_fusion.3 = bf16[192,1024]{1,0:T(8,128)(2,1)S(1)} fusion(f32[]{:T(128)} %bitcast.24, f32[]{:T(128)} %bitcast.23, f32[]{:T(128)} %bitcast.22, f32[]{:T(128)} %bitcast.21, f32[]{:T(128)} %bitcast.20, f32[]{:T(128)} %bitcast.19, f32[]{:T(128)} %bitcast.18, f32[]{:T(128)} %bitcast.17, f32[]{:T(128)} %bitcast.16, f32[]{:T(128)} %bitcast.15, ...), kind=kOutput, calls=%fused_computation.39 | convolution fusion | flops 407961600 | bytes 2884676 | tf_op jit(solution)/shard_map/rd,md->rm/dot_general | solution.py:23
  107.9 8.6 %add_convert_fusion.2 = bf16[192,1024]{1,0:T(8,128)(2,1)S(1)} fusion(f32[]{:T(128)} %bitcast.24, f32[]{:T(128)} %bitcast.23, f32[]{:T(128)} %bitcast.22, f32[]{:T(128)} %bitcast.21, f32[]{:T(128)} %bitcast.20, f32[]{:T(128)} %bitcast.19, f32[]{:T(128)} %bitcast.18, f32[]{:T(128)} %bitcast.17, f32[]{:T(128)} %bitcast.16, f32[]{:T(128)} %bitcast.15, ...), kind=kOutput, calls=%fused_computation.38 | convolution fusion | flops 407961600 | bytes 2884676 | tf_op jit(solution)/shard_map/rd,md->rm/dot_general | solution.py:23
  116.6 3.9 %fusion.20 = bf16[192,2048]{1,0:T(8,128)(2,1)S(1)} fusion(s32[2048]{0:T(1024)S(1)} %bitcast.40, bf16[192,1024]{1,0:T(8,128)(2,1)S(1)} %add_convert_fusion.2, bf16[192,1024]{1,0:T(8,128)(2,1)S(1)} %add_convert_fusion.3, pred[]{:T(512)S(6)} %eq.25), kind=kOutput, calls=%fused_computation.19 | convolution fusion | flops 1618739200 | bytes 1581057 | tf_op jit(solution)/shard_map/dot_general | solution.py:29
  120.5 0.5 collective-permute-start.3
  121.0 3.0 %fusion.10 = f32[192,2048]{1,0:T(8,128)} fusion(bf16[192,2048]{1,0:T(8,128)(2,1)S(1)} %fusion.20, bf16[4096,2048]{1,0:T(8,128)(2,1)S(1)} %bitcast.42), kind=kOutput, calls=%fused_computation.12 | convolution fusion | flops 1610612736 | bytes 10747904 | tf_op jit(solution)/shard_map/dot_general | solution.py:87
  124.0 1.9 %fusion.8 = f32[192,2048]{1,0:T(8,128)S(1)} fusion(bf16[192,2048]{1,0:T(8,128)(2,1)S(1)} %collective-permute-done.3, bf16[4096,2048]{1,0:T(8,128)(2,1)S(1)} %bitcast.42), kind=kOutput, calls=%fused_computation.10 | convolution fusion | flops 1610612736 | bytes 10747904 | tf_op jit(solution)/shard_map/dot_general | solution.py:88
  125.9 0.3 collective-permute-start.4
  126.3 9.5 %add_convert_fusion.1 = bf16[192,1024]{1,0:T(8,128)(2,1)S(1)} fusion(f32[]{:T(128)} %bitcast.24, f32[]{:T(128)} %bitcast.23, f32[]{:T(128)} %bitcast.22, f32[]{:T(128)} %bitcast.21, f32[]{:T(128)} %bitcast.20, f32[]{:T(128)} %bitcast.19, f32[]{:T(128)} %bitcast.18, f32[]{:T(128)} %bitcast.17, f32[]{:T(128)} %bitcast.16, f32[]{:T(128)} %bitcast.15, ...), kind=kOutput, calls=%fused_computation.37 | convolution fusion | flops 407961600 | bytes 2884676 | tf_op jit(solution)/shard_map/rd,md->rm/dot_general | solution.py:23
  135.8 7.1 %add_convert_fusion = bf16[192,1024]{1,0:T(8,128)(2,1)S(1)} fusion(f32[]{:T(128)} %bitcast.24, f32[]{:T(128)} %bitcast.23, f32[]{:T(128)} %bitcast.22, f32[]{:T(128)} %bitcast.21, f32[]{:T(128)} %bitcast.20, f32[]{:T(128)} %bitcast.19, f32[]{:T(128)} %bitcast.18, f32[]{:T(128)} %bitcast.17, f32[]{:T(128)} %bitcast.16, f32[]{:T(128)} %bitcast.15, ...), kind=kOutput, calls=%fused_computation.36 | convolution fusion | flops 407961600 | bytes 2884676 | tf_op jit(solution)/shard_map/rd,md->rm/dot_general | solution.py:23
  142.9 3.9 %fusion.19 = bf16[192,2048]{1,0:T(8,128)(2,1)S(1)} fusion(s32[2048]{0:T(1024)S(1)} %bitcast.39, bf16[192,1024]{1,0:T(8,128)(2,1)S(1)} %add_convert_fusion, bf16[192,1024]{1,0:T(8,128)(2,1)S(1)} %add_convert_fusion.1, pred[]{:T(512)S(6)} %eq.25), kind=kOutput, calls=%fused_computation.18 | convolution fusion | flops 1618739200 | bytes 1581057 | tf_op jit(solution)/shard_map/dot_general | solution.py:29
  146.8 0.6 collective-permute-start.5
  147.4 1.9 %fusion.13 = bf16[192,2048]{1,0:T(8,128)(2,1)S(1)} fusion(f32[192,2048]{1,0:T(8,128)S(1)} %copy-done.6, bf16[192,2048]{1,0:T(8,128)(2,1)S(1)} %fusion.19, bf16[4096,2048]{1,0:T(8,128)(2,1)S(1)} %bitcast.44), kind=kOutput, calls=%fused_computation.16 | convolution fusion | flops 1611399168 | bytes 11534336 | tf_op jit(solution)/shard_map/dot_general | solution.py:87
  149.3 0.1 collective-permute-done.5
  149.4 1.9 %fusion.16 = bf16[192,2048]{1,0:T(8,128)(2,1)S(1)} fusion(f32[192,2048]{1,0:T(8,128)S(1)} %fusion.8, bf16[192,2048]{1,0:T(8,128)(2,1)S(1)} %collective-permute-done.5, bf16[4096,2048]{1,0:T(8,128)(2,1)S(1)} %bitcast.44), kind=kOutput, calls=%fused_computation.17 | convolution fusion | flops 1611399168 | bytes 11534336 | tf_op jit(solution)/shard_map/dot_general | solution.py:88
  151.3 1.8 %fusion.12 = bf16[384,2048]{1,0:T(8,128)(2,1)} fusion(bf16[192,2048]{1,0:T(8,128)(2,1)S(1)} %fusion.16, bf16[192,2048]{1,0:T(8,128)(2,1)S(1)} %fusion.13, pred[]{:T(512)S(6)} %eq.25), kind=kLoop, calls=%fused_computation.15 | loop fusion | flops 7077888 | bytes 3145729 | tf_op jit(solution)/shard_map/convert_element_type | solution.py:96
  (46 shorter events, 0.4 us)
Async XLA Ops:
  5.0 12.1 %copy-start.3 = (f32[4]{0:T(128)S(1)}, f32[4]{0:T(128)}, u32[]{:S(2)}) copy-start(f32[4]{0:T(128)} %param.11) | copy-start | bytes 52
  5.0 13.1 %copy-start.4 = (f32[4]{0:T(128)S(1)}, f32[4]{0:T(128)}, u32[]{:S(2)}) copy-start(f32[4]{0:T(128)} %param.12) | copy-start | bytes 52
  5.0 13.2 %copy-start.2 = (s32[2]{0:T(128)S(1)}, s32[2]{0:T(128)}, u32[]{:S(2)}) copy-start(s32[2]{0:T(128)} %param.9) | copy-start | bytes 28
  5.0 40.3 %all-to-all-start = ((bf16[64,16,1024]{2,1,0:T(8,128)(2,1)}), bf16[64,16,1024]{2,1,0:T(8,128)(2,1)S(1)}, u32[]{:S(2)}, u32[]{:S(2)}) async-start(bf16[64,16,1024]{2,1,0:T(8,128)(2,1)} %bitcast.1), calls=%async_computation | async-start | bytes 4194304 | tf_op jit(solution)/shard_map/all_to_all | solution.py:51
  17.1 5.6 %collective-permute-start = (f32[4]{0:T(128)S(1)}, f32[4]{0:T(128)S(1)}, u32[]{:S(2)}, u32[]{:S(2)}) collective-permute-start(f32[4]{0:T(128)S(1)} %copy-done.3), channel_id=1, source_target_pairs={{0,1},{1,0},{2,3},{3,2},{4,5},{5,4},{6,7},{7,6},{8,9},{9,8},{10,11... | collective-permute-start | bytes 56 | tf_op jit(solution)/shard_map/ppermute | solution.py:34
  18.2 4.6 %collective-permute-start.1 = (f32[4]{0:T(128)S(1)}, f32[4]{0:T(128)S(1)}, u32[]{:S(2)}, u32[]{:S(2)}) collective-permute-start(f32[4]{0:T(128)S(1)} %copy-done.4), channel_id=1, source_target_pairs={{0,1},{1,0},{2,3},{3,2},{4,5},{5,4},{6,7},{7,6},{8,9},{9,8},{10,11... | collective-permute-start | bytes 56 | tf_op jit(solution)/shard_map/ppermute | solution.py:34
  45.8 37.8 %copy-start.5 = (s32[128]{0:T(128)S(1)}, s32[128]{0:T(128)}, u32[]{:S(2)}) copy-start(s32[128]{0:T(128)} %constant.33) | copy-start | bytes 1540
  45.8 39.0 %copy-start = (bf16[384,1024]{1,0:T(8,128)(2,1)S(1)}, bf16[384,1024]{1,0:T(8,128)(2,1)}, u32[]{:S(2)}) copy-start(bf16[384,1024]{1,0:T(8,128)(2,1)} %param.7) | copy-start | bytes 2359300
  45.8 39.2 %copy-start.1 = (s32[2,2048]{1,0:T(2,128)S(1)}, s32[2,2048]{1,0:T(2,128)}, u32[]{:S(2)}) copy-start(s32[2,2048]{1,0:T(2,128)} %param.10) | copy-start | bytes 49156
  80.5 27.4 %collective-permute-start.2 = (bf16[1024,1024]{1,0:T(8,128)(2,1)S(1)}, bf16[1024,1024]{1,0:T(8,128)(2,1)}, u32[]{:S(2)}, u32[]{:S(2)}) collective-permute-start(bf16[1024,1024]{1,0:T(8,128)(2,1)S(1)} %bitcast.37), channel_id=1, source_target_pairs={{0,1},{1,0},{2,3},{3,2},{4,5},{5,4},{6,7},{7,6},{8,9},{9,8},{10,11... | collective-permute-start | bytes 6291464 | tf_op jit(solution)/shard_map/ppermute | solution.py:34
  86.7 39.2 %all-to-all-start.1 = ((bf16[64,16,1024]{2,1,0:T(8,128)(2,1)}), bf16[64,16,1024]{2,1,0:T(8,128)(2,1)}, u32[]{:S(2)}, u32[]{:S(2)}) async-start(bf16[64,16,1024]{2,1,0:T(8,128)(2,1)} %broadcast_in_dim.18), calls=%async_computation.1 | async-start | bytes 4194304 | tf_op jit(solution)/shard_map/all_to_all | solution.py:60
  99.9 21.1 %slice-start = ((s8[16777216]{0:T(1024)(128)(4,1)}), s8[4194304]{0:T(1024)(128)(4,1)S(1)}, s32[]{:S(2)}) async-start(s8[16777216]{0:T(1024)(128)(4,1)} %bitcast.41), calls=%async_computation.3 | async-start | bytes 8388608
  99.9 21.1 %slice-start.1 = ((s8[16777216]{0:T(1024)(128)(4,1)}), s8[4194304]{0:T(1024)(128)(4,1)S(1)}, s32[]{:S(2)}) async-start(s8[16777216]{0:T(1024)(128)(4,1)} %bitcast.41), calls=%async_computation.4 | async-start | bytes 8388608
  107.9 13.1 %slice-start.2 = ((s8[16777216]{0:T(1024)(128)(4,1)}), s8[4194304]{0:T(1024)(128)(4,1)S(1)}, s32[]{:S(2)}) async-start(s8[16777216]{0:T(1024)(128)(4,1)} %bitcast.41), calls=%async_computation.5 | async-start | bytes 8388608
  116.5 4.5 %slice-start.3 = ((s8[16777216]{0:T(1024)(128)(4,1)}), s8[4194304]{0:T(1024)(128)(4,1)S(1)}, s32[]{:S(2)}) async-start(s8[16777216]{0:T(1024)(128)(4,1)} %bitcast.41), calls=%async_computation.6 | async-start | bytes 8388608
  120.5 3.6 %collective-permute-start.3 = (bf16[192,2048]{1,0:T(8,128)(2,1)S(1)}, bf16[192,2048]{1,0:T(8,128)(2,1)S(1)}, u32[]{:S(2)}, u32[]{:S(2)}) collective-permute-start(bf16[192,2048]{1,0:T(8,128)(2,1)S(1)} %fusion.20), channel_id=1, source_target_pairs={{0,1},{1,0},{2,3},{3,2},{4,5},{5,4},{6,7},{7,6},{8,9},{9,8},{10,11... | collective-permute-start | bytes 2359304 | tf_op jit(solution)/shard_map/ppermute | solution.py:34
  125.9 9.9 %collective-permute-start.4 = (bf16[1024,1024]{1,0:T(8,128)(2,1)}, bf16[1024,1024]{1,0:T(8,128)(2,1)S(1)}, u32[]{:S(2)}, u32[]{:S(2)}) collective-permute-start(bf16[1024,1024]{1,0:T(8,128)(2,1)} %bitcast.5), channel_id=1, source_target_pairs={{0,1},{1,0},{2,3},{3,2},{4,5},{5,4},{6,7},{7,6},{8,9},{9,8},{10,11... | collective-permute-start | bytes 6291464 | tf_op jit(solution)/shard_map/ppermute | solution.py:34
  126.2 21.2 %slice-start.4 = ((s8[16777216]{0:T(1024)(128)(4,1)}), s8[4194304]{0:T(1024)(128)(4,1)S(1)}, s32[]{:S(2)}) async-start(s8[16777216]{0:T(1024)(128)(4,1)} %bitcast.43), calls=%async_computation.7 | async-start | bytes 8388608
  126.3 21.2 %slice-start.5 = ((s8[16777216]{0:T(1024)(128)(4,1)}), s8[4194304]{0:T(1024)(128)(4,1)S(1)}, s32[]{:S(2)}) async-start(s8[16777216]{0:T(1024)(128)(4,1)} %bitcast.43), calls=%async_computation.8 | async-start | bytes 8388608
  135.8 11.6 %slice-start.6 = ((s8[16777216]{0:T(1024)(128)(4,1)}), s8[4194304]{0:T(1024)(128)(4,1)S(1)}, s32[]{:S(2)}) async-start(s8[16777216]{0:T(1024)(128)(4,1)} %bitcast.43), calls=%async_computation.9 | async-start | bytes 8388608
  142.9 4.5 %slice-start.7 = ((s8[16777216]{0:T(1024)(128)(4,1)}), s8[4194304]{0:T(1024)(128)(4,1)S(1)}, s32[]{:S(2)}) async-start(s8[16777216]{0:T(1024)(128)(4,1)} %bitcast.43), calls=%async_computation.10 | async-start | bytes 8388608
  142.9 4.5 %copy-start.6 = (f32[192,2048]{1,0:T(8,128)S(1)}, f32[192,2048]{1,0:T(8,128)}, u32[]{:S(2)}) copy-start(f32[192,2048]{1,0:T(8,128)} %fusion.10) | copy-start | bytes 4718596
  146.8 2.6 %collective-permute-start.5 = (bf16[192,2048]{1,0:T(8,128)(2,1)S(1)}, bf16[192,2048]{1,0:T(8,128)(2,1)S(1)}, u32[]{:S(2)}, u32[]{:S(2)}) collective-permute-start(bf16[192,2048]{1,0:T(8,128)(2,1)S(1)} %fusion.19), channel_id=1, source_target_pairs={{0,1},{1,0},{2,3},{3,2},{4,5},{5,4},{6,7},{7,6},{8,9},{9,8},{10,11... | collective-permute-start | bytes 2359304 | tf_op jit(solution)/shard_map/ppermute | solution.py:34

commit v16 on v15

--- a/solution.py
+++ b/solution.py
@@ -88,12 +88,13 @@
         other_features = other_features + jnp.dot(
             other_kernel, rows, preferred_element_type=jnp.float32
         )
-    features = jnp.where(
-        core == 0,
-        jnp.concatenate([own_features, other_features], axis=0),
-        jnp.concatenate([other_features, own_features], axis=0),
+    features = jnp.zeros((cores * share, whitening.shape[1]), jnp.bfloat16)
+    features = lax.dynamic_update_slice_in_dim(
+        features, own_features.astype(jnp.bfloat16), core * share, axis=0
     )
-    return features.astype(jnp.bfloat16)
+    return lax.dynamic_update_slice_in_dim(
+        features, other_features.astype(jnp.bfloat16), (1 - core) * share, axis=0
+    )
 
 
 def solution(mesh):

time: 154 us -> 163 us (1.058)
  matrix products: 49.6 us -> 55.9 us
  other arithmetic: 2.34 us -> 0.55 us
    dot_general x2, matrix products: 3.77 us -> 8.04 us  [per_device(): jnp.dot(other_kernel, rows, preferred_element_type=jnp.float32)]
    dot_general x2, matrix products: 4.89 us -> 8.64 us  [per_device(): jnp.dot(own_kernel, rows, preferred_element_type=jnp.float32)]
    all_to_all x1, waiting for transfers between devices: 0.01 us -> 1.92 us  [per_device(): lax.all_to_all(jnp.broadcast_to(kept[number][None], (count,) + kept.shape...]
    convert_element_type x1 -> x0, other arithmetic: 1.8 us -> none  [per_device(): return features.astype(jnp.bfloat16)]
    dot_general x4, matrix products: 33.2 us -> 31.4 us  [inner_products(): jnp.einsum('rd,md->rm', unit_rows, landmark, preferred_element_type=jnp.f...]
where the time goes in v16:
time: 163 us; the launch traced here: 162 us
  matrix products  55.9 us (34%)
  blocking collectives  34.6 us (21%)
  starting transfers between devices  26 us (16%)
  waiting for transfers between devices  24.2 us (15%)
  between operations  10.7 us (7%)
  local copies, waits for them, and re-layouts  10.1 us (6%)
    all_to_all x1, blocking collectives, per_device(): lax.all_to_all(jnp.broadcast_to(kept[number][None], (count,) + kept.shape...  34.6 us
    dot_general x4, matrix products, inner_products(): jnp.einsum('rd,md->rm', unit_rows, landmark, preferred_element_type=jnp.f...  31.4 us
    all_to_all x1, waiting for transfers between devices, per_device(): spread = lax.all_to_all(pieces, SPREAD, 0, 0, tiled=True)  22.3 us
    all_to_all x1, starting transfers between devices, per_device(): spread = lax.all_to_all(pieces, SPREAD, 0, 0, tiled=True)  12.1 us
    dot_general x2, matrix products, per_device(): jnp.dot(own_kernel, rows, preferred_element_type=jnp.float32)  8.64 us
    dot_general x2, matrix products, per_device(): jnp.dot(other_kernel, rows, preferred_element_type=jnp.float32)  8.04 us
    dot_general x2, matrix products, reorder_columns(): ordered = jnp.dot(kernel, onehot, preferred_element_type=jnp.float32)  7.77 us
    ppermute x6, starting transfers between devices, swap_cores(): return lax.ppermute(value, 'bw', [(0, 1), (1, 0)])  7 us
  transfers between devices with their start and end apart: 8, of which 2 were waited for; matrix products, arithmetic and copies ran while one was open for 27% of the time, Pallas kernels for 0%

profile of v16, /device:TPU:1, one launch (start us, length us, event | category | flops | bytes accessed | tf_op | source)
XLA Modules:
  0.0 162.0 jit_solution(8369053663100125792)
XLA Ops:
  0.0 1.2 dynamic-slice.6
  1.9 3.1 %constant_dynamic-slice_fusion = bf16[1024,1024]{1,0:T(8,128)(2,1)} fusion(bf16[2048,1024]{1,0:T(8,128)(2,1)} %param.8, s32[]{:T(128)S(6)} %subtract.2), kind=kLoop, calls=%fused_computation.55 | loop fusion | bytes 4194308 | tf_op jit(solution)/call_exported
  5.0 12.1 %all-to-all-start = ((bf16[64,16,1024]{2,1,0:T(8,128)(2,1)}), bf16[64,16,1024]{2,1,0:T(8,128)(2,1)S(1)}, u32[]{:S(2)}, u32[]{:S(2)}) async-start(bf16[64,16,1024]{2,1,0:T(8,128)(2,1)} %bitcast.1), calls=%async_computation | async-start | bytes 4194304 | tf_op jit(solution)/shard_map/all_to_all | solution.py:51
  17.1 1.0 collective-permute-start
  18.2 0.6 fusion.71
  23.0 22.3 %all-to-all-done = bf16[64,16,1024]{2,1,0:T(8,128)(2,1)S(1)} async-done(((bf16[64,16,1024]{2,1,0:T(8,128)(2,1)}), bf16[64,16,1024]{2,1,0:T(8,128)(2,1)S(1)}, u32[]{:S(2)}, u32[]{:S(2)}) %all-to-all-start) | async-done | bytes 2097184 | tf_op jit(solution)/shard_map/all_to_all | solution.py:51
  45.3 0.1 fusion.46
  45.5 0.2 broadcast_in_dim.24
  45.8 34.6 %all_to_all.15 = bf16[64,16,1024]{2,1,0:T(8,128)(2,1)S(1)} all-to-all(bf16[64,16,1024]{2,1,0:T(8,128)(2,1)S(1)} %broadcast_in_dim.24), channel_id=1, replica_groups=mesh['row'=8,'lmk'=8,'bw'=2] {'row','lmk'}, dimensions={0} | all-to-all | bytes 4194304 | tf_op jit(solution)/shard_map/all_to_all | solution.py:60
  80.5 3.1 %collective-permute-start.2 = (bf16[1024,1024]{1,0:T(8,128)(2,1)S(1)}, bf16[1024,1024]{1,0:T(8,128)(2,1)}, u32[]{:S(2)}, u32[]{:S(2)}) collective-permute-start(bf16[1024,1024]{1,0:T(8,128)(2,1)S(1)} %bitcast.37), channel_id=1, source_target_pairs={{0,1},{1,0},{2,3},{3,2},{4,5},{5,4},{6,7},{7,6},{8,9},{9,8},{10,11... | collective-permute-start | bytes 6291464 | tf_op jit(solution)/shard_map/ppermute | solution.py:34
  83.6 0.6 dynamic-slice.2
  84.8 0.2 fusion.32
  85.0 0.7 fusion.70
  90.8 1.6 broadcast_in_dim.22
  92.4 6.9 %all-to-all-start.1 = ((bf16[64,16,1024]{2,1,0:T(8,128)(2,1)}), bf16[64,16,1024]{2,1,0:T(8,128)(2,1)}, u32[]{:S(2)}, u32[]{:S(2)}) async-start(bf16[64,16,1024]{2,1,0:T(8,128)(2,1)} %broadcast_in_dim.22), calls=%async_computation.1 | async-start | bytes 4194304 | tf_op jit(solution)/shard_map/all_to_all | solution.py:60
  99.3 0.7 fusion.69
  100.0 7.9 %add_convert_fusion.3 = bf16[192,1024]{1,0:T(8,128)(2,1)S(1)} fusion(f32[]{:T(128)} %bitcast.24, f32[]{:T(128)} %bitcast.23, f32[]{:T(128)} %bitcast.22, f32[]{:T(128)} %bitcast.21, f32[]{:T(128)} %bitcast.20, f32[]{:T(128)} %bitcast.19, f32[]{:T(128)} %bitcast.18, f32[]{:T(128)} %bitcast.17, f32[]{:T(128)} %bitcast.16, f32[]{:T(128)} %bitcast.15, ...), kind=kOutput, calls=%fused_computation.41 | convolution fusion | flops 407961600 | bytes 2884676 | tf_op jit(solution)/shard_map/rd,md->rm/dot_general | solution.py:23
  107.9 8.6 %add_convert_fusion.2 = bf16[192,1024]{1,0:T(8,128)(2,1)S(1)} fusion(f32[]{:T(128)} %bitcast.24, f32[]{:T(128)} %bitcast.23, f32[]{:T(128)} %bitcast.22, f32[]{:T(128)} %bitcast.21, f32[]{:T(128)} %bitcast.20, f32[]{:T(128)} %bitcast.19, f32[]{:T(128)} %bitcast.18, f32[]{:T(128)} %bitcast.17, f32[]{:T(128)} %bitcast.16, f32[]{:T(128)} %bitcast.15, ...), kind=kOutput, calls=%fused_computation.40 | convolution fusion | flops 407961600 | bytes 2884676 | tf_op jit(solution)/shard_map/rd,md->rm/dot_general | solution.py:23
  116.5 3.9 %fusion.19 = bf16[192,2048]{1,0:T(8,128)(2,1)S(1)} fusion(s32[2048]{0:T(1024)S(1)} %bitcast.40, bf16[192,1024]{1,0:T(8,128)(2,1)S(1)} %add_convert_fusion.2, bf16[192,1024]{1,0:T(8,128)(2,1)S(1)} %add_convert_fusion.3, pred[]{:T(512)S(6)} %eq.24), kind=kOutput, calls=%fused_computation.17 | convolution fusion | flops 1618739200 | bytes 1581057 | tf_op jit(solution)/shard_map/dot_general | solution.py:29
  120.4 0.5 collective-permute-start.3
  120.9 3.0 %fusion.10 = f32[192,2048]{1,0:T(8,128)} fusion(bf16[192,2048]{1,0:T(8,128)(2,1)S(1)} %fusion.19, bf16[4096,2048]{1,0:T(8,128)(2,1)S(1)} %bitcast.42), kind=kOutput, calls=%fused_computation.12 | convolution fusion | flops 1610612736 | bytes 10747904 | tf_op jit(solution)/shard_map/dot_general | solution.py:87
  124.0 1.9 %fusion.8 = f32[192,2048]{1,0:T(8,128)S(1)} fusion(bf16[192,2048]{1,0:T(8,128)(2,1)S(1)} %collective-permute-done.3, bf16[4096,2048]{1,0:T(8,128)(2,1)S(1)} %bitcast.42), kind=kOutput, calls=%fused_computation.10 | convolution fusion | flops 1610612736 | bytes 10747904 | tf_op jit(solution)/shard_map/dot_general | solution.py:88
  125.9 1.9 %all-to-all-done.1 = bf16[64,16,1024]{2,1,0:T(8,128)(2,1)} async-done(((bf16[64,16,1024]{2,1,0:T(8,128)(2,1)}), bf16[64,16,1024]{2,1,0:T(8,128)(2,1)}, u32[]{:S(2)}, u32[]{:S(2)}) %all-to-all-start.1) | async-done | bytes 2097184 | tf_op jit(solution)/shard_map/all_to_all | solution.py:60
  127.8 1.9 %collective-permute-start.4 = (bf16[1024,1024]{1,0:T(8,128)(2,1)}, bf16[1024,1024]{1,0:T(8,128)(2,1)S(1)}, u32[]{:S(2)}, u32[]{:S(2)}) collective-permute-start(bf16[1024,1024]{1,0:T(8,128)(2,1)} %bitcast.5), channel_id=1, source_target_pairs={{0,1},{1,0},{2,3},{3,2},{4,5},{5,4},{6,7},{7,6},{8,9},{9,8},{10,11... | collective-permute-start | bytes 6291464 | tf_op jit(solution)/shard_map/ppermute | solution.py:34
  129.7 8.3 %add_convert_fusion.1 = bf16[192,1024]{1,0:T(8,128)(2,1)S(1)} fusion(f32[]{:T(128)} %bitcast.24, f32[]{:T(128)} %bitcast.23, f32[]{:T(128)} %bitcast.22, f32[]{:T(128)} %bitcast.21, f32[]{:T(128)} %bitcast.20, f32[]{:T(128)} %bitcast.19, f32[]{:T(128)} %bitcast.18, f32[]{:T(128)} %bitcast.17, f32[]{:T(128)} %bitcast.16, f32[]{:T(128)} %bitcast.15, ...), kind=kOutput, calls=%fused_computation.39 | convolution fusion | flops 407961600 | bytes 2884676 | tf_op jit(solution)/shard_map/rd,md->rm/dot_general | solution.py:23
  138.0 6.7 %add_convert_fusion = bf16[192,1024]{1,0:T(8,128)(2,1)S(1)} fusion(f32[]{:T(128)} %bitcast.24, f32[]{:T(128)} %bitcast.23, f32[]{:T(128)} %bitcast.22, f32[]{:T(128)} %bitcast.21, f32[]{:T(128)} %bitcast.20, f32[]{:T(128)} %bitcast.19, f32[]{:T(128)} %bitcast.18, f32[]{:T(128)} %bitcast.17, f32[]{:T(128)} %bitcast.16, f32[]{:T(128)} %bitcast.15, ...), kind=kOutput, calls=%fused_computation.38 | convolution fusion | flops 407961600 | bytes 2884676 | tf_op jit(solution)/shard_map/rd,md->rm/dot_general | solution.py:23
  144.7 3.9 %fusion.18 = bf16[192,2048]{1,0:T(8,128)(2,1)S(1)} fusion(s32[2048]{0:T(1024)S(1)} %bitcast.39, bf16[192,1024]{1,0:T(8,128)(2,1)S(1)} %add_convert_fusion, bf16[192,1024]{1,0:T(8,128)(2,1)S(1)} %add_convert_fusion.1, pred[]{:T(512)S(6)} %eq.24), kind=kOutput, calls=%fused_computation.16 | convolution fusion | flops 1618739200 | bytes 1581057 | tf_op jit(solution)/shard_map/dot_general | solution.py:29
  148.6 0.3 collective-permute-start.5
  148.9 0.2 broadcast_in_dim.20
  149.1 5.6 %fusion.26 = bf16[384,2048]{1,0:T(8,128)(2,1)S(1)} fusion(bf16[384,2048]{1,0:T(8,128)(2,1)S(1)} %broadcast_in_dim.20, s32[]{:T(128)S(6)} %select_n.30, f32[192,2048]{1,0:T(8,128)} %fusion.10, bf16[192,2048]{1,0:T(8,128)(2,1)S(1)} %fusion.18, bf16[4096,2048]{1,0:T(8,128)(2,1)} %param.13), kind=kOutput, calls=%fused_computation.20 | convolution fusion | flops 1611399168 | bytes 11534340 | tf_op jit(solution)/shard_map/dot_general | solution.py:87
  154.7 1.1 copy-done
  155.8 6.1 %fusion.29 = bf16[384,2048]{1,0:T(8,128)(2,1)} fusion(bf16[384,2048]{1,0:T(8,128)(2,1)} %copy-done, s32[]{:T(128)S(6)} %select_n.31, f32[192,2048]{1,0:T(8,128)S(1)} %fusion.8, bf16[192,2048]{1,0:T(8,128)(2,1)S(1)} %collective-permute-done.5, bf16[4096,2048]{1,0:T(8,128)(2,1)} %param.13), kind=kOutput, calls=%fused_computation.21 | convolution fusion | flops 1611399168 | bytes 11534340 | tf_op jit(solution)/shard_map/dot_general | solution.py:88
  (37 shorter events, 0.5 us)
Async XLA Ops:
  5.0 12.1 %copy-start.4 = (f32[4]{0:T(128)S(1)}, f32[4]{0:T(128)}, u32[]{:S(2)}) copy-start(f32[4]{0:T(128)} %param.11) | copy-start | bytes 52
  5.0 13.1 %copy-start.5 = (f32[4]{0:T(128)S(1)}, f32[4]{0:T(128)}, u32[]{:S(2)}) copy-start(f32[4]{0:T(128)} %param.12) | copy-start | bytes 52
  5.0 13.2 %copy-start.3 = (s32[2]{0:T(128)S(1)}, s32[2]{0:T(128)}, u32[]{:S(2)}) copy-start(s32[2]{0:T(128)} %param.9) | copy-start | bytes 28
  5.0 40.3 %all-to-all-start = ((bf16[64,16,1024]{2,1,0:T(8,128)(2,1)}), bf16[64,16,1024]{2,1,0:T(8,128)(2,1)S(1)}, u32[]{:S(2)}, u32[]{:S(2)}) async-start(bf16[64,16,1024]{2,1,0:T(8,128)(2,1)} %bitcast.1), calls=%async_computation | async-start | bytes 4194304 | tf_op jit(solution)/shard_map/all_to_all | solution.py:51
  17.1 5.8 %collective-permute-start = (f32[4]{0:T(128)S(1)}, f32[4]{0:T(128)S(1)}, u32[]{:S(2)}, u32[]{:S(2)}) collective-permute-start(f32[4]{0:T(128)S(1)} %copy-done.4), channel_id=1, source_target_pairs={{0,1},{1,0},{2,3},{3,2},{4,5},{5,4},{6,7},{7,6},{8,9},{9,8},{10,11... | collective-permute-start | bytes 56 | tf_op jit(solution)/shard_map/ppermute | solution.py:34
  18.1 4.8 %collective-permute-start.1 = (f32[4]{0:T(128)S(1)}, f32[4]{0:T(128)S(1)}, u32[]{:S(2)}, u32[]{:S(2)}) collective-permute-start(f32[4]{0:T(128)S(1)} %copy-done.5), channel_id=1, source_target_pairs={{0,1},{1,0},{2,3},{3,2},{4,5},{5,4},{6,7},{7,6},{8,9},{9,8},{10,11... | collective-permute-start | bytes 56 | tf_op jit(solution)/shard_map/ppermute | solution.py:34
  45.8 37.8 %copy-start.6 = (s32[128]{0:T(128)S(1)}, s32[128]{0:T(128)}, u32[]{:S(2)}) copy-start(s32[128]{0:T(128)} %constant.41) | copy-start | bytes 1540
  45.8 39.0 %copy-start.1 = (bf16[384,1024]{1,0:T(8,128)(2,1)S(1)}, bf16[384,1024]{1,0:T(8,128)(2,1)}, u32[]{:S(2)}) copy-start(bf16[384,1024]{1,0:T(8,128)(2,1)} %param.7) | copy-start | bytes 2359300
  45.8 39.2 %copy-start.2 = (s32[2,2048]{1,0:T(2,128)S(1)}, s32[2,2048]{1,0:T(2,128)}, u32[]{:S(2)}) copy-start(s32[2,2048]{1,0:T(2,128)} %param.10) | copy-start | bytes 49156
  80.5 27.4 %collective-permute-start.2 = (bf16[1024,1024]{1,0:T(8,128)(2,1)S(1)}, bf16[1024,1024]{1,0:T(8,128)(2,1)}, u32[]{:S(2)}, u32[]{:S(2)}) collective-permute-start(bf16[1024,1024]{1,0:T(8,128)(2,1)S(1)} %bitcast.37), channel_id=1, source_target_pairs={{0,1},{1,0},{2,3},{3,2},{4,5},{5,4},{6,7},{7,6},{8,9},{9,8},{10,11... | collective-permute-start | bytes 6291464 | tf_op jit(solution)/shard_map/ppermute | solution.py:34
  92.4 35.4 %all-to-all-start.1 = ((bf16[64,16,1024]{2,1,0:T(8,128)(2,1)}), bf16[64,16,1024]{2,1,0:T(8,128)(2,1)}, u32[]{:S(2)}, u32[]{:S(2)}) async-start(bf16[64,16,1024]{2,1,0:T(8,128)(2,1)} %broadcast_in_dim.22), calls=%async_computation.1 | async-start | bytes 4194304 | tf_op jit(solution)/shard_map/all_to_all | solution.py:60
  100.0 21.0 %slice-start = ((s8[16777216]{0:T(1024)(128)(4,1)}), s8[4194304]{0:T(1024)(128)(4,1)S(1)}, s32[]{:S(2)}) async-start(s8[16777216]{0:T(1024)(128)(4,1)} %bitcast.41), calls=%async_computation.3 | async-start | bytes 8388608
  100.0 21.0 %slice-start.1 = ((s8[16777216]{0:T(1024)(128)(4,1)}), s8[4194304]{0:T(1024)(128)(4,1)S(1)}, s32[]{:S(2)}) async-start(s8[16777216]{0:T(1024)(128)(4,1)} %bitcast.41), calls=%async_computation.4 | async-start | bytes 8388608
  107.9 13.1 %slice-start.2 = ((s8[16777216]{0:T(1024)(128)(4,1)}), s8[4194304]{0:T(1024)(128)(4,1)S(1)}, s32[]{:S(2)}) async-start(s8[16777216]{0:T(1024)(128)(4,1)} %bitcast.41), calls=%async_computation.5 | async-start | bytes 8388608
  116.5 4.5 %slice-start.3 = ((s8[16777216]{0:T(1024)(128)(4,1)}), s8[4194304]{0:T(1024)(128)(4,1)S(1)}, s32[]{:S(2)}) async-start(s8[16777216]{0:T(1024)(128)(4,1)} %bitcast.41), calls=%async_computation.6 | async-start | bytes 8388608
  120.4 3.6 %collective-permute-start.3 = (bf16[192,2048]{1,0:T(8,128)(2,1)S(1)}, bf16[192,2048]{1,0:T(8,128)(2,1)S(1)}, u32[]{:S(2)}, u32[]{:S(2)}) collective-permute-start(bf16[192,2048]{1,0:T(8,128)(2,1)S(1)} %fusion.19), channel_id=1, source_target_pairs={{0,1},{1,0},{2,3},{3,2},{4,5},{5,4},{6,7},{7,6},{8,9},{9,8},{10,11... | collective-permute-start | bytes 2359304 | tf_op jit(solution)/shard_map/ppermute | solution.py:34
  127.8 10.2 %collective-permute-start.4 = (bf16[1024,1024]{1,0:T(8,128)(2,1)}, bf16[1024,1024]{1,0:T(8,128)(2,1)S(1)}, u32[]{:S(2)}, u32[]{:S(2)}) collective-permute-start(bf16[1024,1024]{1,0:T(8,128)(2,1)} %bitcast.5), channel_id=1, source_target_pairs={{0,1},{1,0},{2,3},{3,2},{4,5},{5,4},{6,7},{7,6},{8,9},{9,8},{10,11... | collective-permute-start | bytes 6291464 | tf_op jit(solution)/shard_map/ppermute | solution.py:34
  148.6 6.1 %collective-permute-start.5 = (bf16[192,2048]{1,0:T(8,128)(2,1)S(1)}, bf16[192,2048]{1,0:T(8,128)(2,1)S(1)}, u32[]{:S(2)}, u32[]{:S(2)}) collective-permute-start(bf16[192,2048]{1,0:T(8,128)(2,1)S(1)} %fusion.18), channel_id=1, source_target_pairs={{0,1},{1,0},{2,3},{3,2},{4,5},{5,4},{6,7},{7,6},{8,9},{9,8},{10,11... | collective-permute-start | bytes 2359304 | tf_op jit(solution)/shard_map/ppermute | solution.py:34
  154.7 1.1 copy-start
